TPU v7x, 256 devices: a whole 4x4x8 slice. The times are simulated.
256 devices in a mesh: lon: 16 (over x_lo, z), lat: 16 (over y, x_hi, core).
Axes of the slice: x: 4 (x_hi: 2, x_lo: 2; x = x_hi * 2 + x_lo), y: 4, z: 8, core: 2. Of those that a mesh axis runs over, the one named last changes fastest.
Arguments:
- state: float32 [4, 4, 512, 4096], P(None, None, 'lat', 'lon'), may hold values from -3 to 3
- cotangent: float32 [4, 4, 512, 4096], P(None, None, 'lat', 'lon'), may hold values from -6 to 6
- seamask: int32 [512, 4096], P('lat', 'lon'), may hold values 0 or 1
- levels: int32 [512, 4096], P('lat', 'lon'), may hold values from 1 to 4
Outputs:
- final_state: float32 [4, 4, 512, 4096], P(None, None, 'lat', 'lon')
- adjoint_state: float32 [4, 4, 512, 4096], P(None, None, 'lat', 'lon')
All inputs are finite; a program needn't handle non-finite values. No bound on the sum of `seamask` on one device may be relied on, other than what follows from the above.
Results may differ from a plain program's by a relative error of at most 0.0003.
Values sent between devices are 32-bit elements; how exact they have to be, the bound alone decides.
No kernel may reach another device: no remote copies, remote signals or barrier semaphores. Data moves between devices by JAX's collectives and lax.ppermute only.
A program may use at most 64 MiB of HBM per device.

v0:
```python
import jax
import jax.numpy as jnp
from jax import lax
from jax.sharding import PartitionSpec as P

courant = 0.4
vert_mix = 0.1
rotation = 0.3
buoyancy = 0.3
bottom_drag = 0.2


def slab_of(values, start, length, along):
    return lax.slice_in_dim(values, start, start + length, axis=values.ndim + along)


def face_div(fields, speeds, wet_mask, along):
    extent = fields.shape[along]
    faces = extent - 5
    cells = [slab_of(fields, offset, faces, along) for offset in range(6)]
    face_speed = 0.5 * (slab_of(speeds, 2, faces, along) + slab_of(speeds, 3, faces, along))
    open_face = slab_of(wet_mask, 2, faces, along) * slab_of(wet_mask, 3, faces, along)
    central = (
        37.0 * (cells[2] + cells[3]) - 8.0 * (cells[1] + cells[4]) + (cells[0] + cells[5])
    ) / 60.0
    damping = (
        10.0 * (cells[3] - cells[2]) - 5.0 * (cells[4] - cells[1]) + (cells[5] - cells[0])
    ) / 60.0
    flux = open_face * (face_speed * central - jnp.sqrt(face_speed * face_speed + 0.0001) * damping)
    return slab_of(flux, 1, faces - 1, along) - slab_of(flux, 0, faces - 1, along)


def advance(padded, sea_rim, level_rim, first_row, lat_total):
    level_count = padded.shape[1]
    lat_cells = padded.shape[2]
    lon_cells = padded.shape[3]
    level_index = jnp.arange(level_count, dtype=jnp.int32)[:, None, None]
    wet_mask = (sea_rim[None] * (level_index < level_rim[None]).astype(jnp.int32)).astype(
        jnp.float32
    )
    bottom = (sea_rim[None] * (level_index == level_rim[None] - 1).astype(jnp.int32)).astype(
        jnp.float32
    )
    divergence = face_div(padded, padded[2], wet_mask, -1)[:, :, 3 : lat_cells - 3, :]
    divergence = divergence + face_div(padded, padded[3], wet_mask, -2)[:, :, :, 3 : lon_cells - 3]
    center = padded[:, :, 3 : lat_cells - 3, 3 : lon_cells - 3]
    wet_center = wet_mask[:, 3 : lat_cells - 3, 3 : lon_cells - 3]
    bottom_center = bottom[:, 3 : lat_cells - 3, 3 : lon_cells - 3]
    zero_level = jnp.zeros_like(center[:, :1])
    zero_wet = jnp.zeros_like(wet_center[:1])
    above_cells = jnp.concatenate([zero_level, center[:, :-1]], axis=1)
    below_cells = jnp.concatenate([center[:, 1:], zero_level], axis=1)
    wet_above = jnp.concatenate([zero_wet, wet_center[:-1]], axis=0)
    wet_below = jnp.concatenate([wet_center[1:], zero_wet], axis=0)
    vertical = vert_mix * (wet_above * (above_cells - center) + wet_below * (below_cells - center))
    density = (-0.2 * padded[0] + 0.8 * padded[1]) * wet_mask
    pressure = buoyancy * jnp.cumsum(density, axis=0)
    press_east = 0.5 * (
        pressure[:, 3 : lat_cells - 3, 4 : lon_cells - 2]
        - pressure[:, 3 : lat_cells - 3, 2 : lon_cells - 4]
    )
    press_north = 0.5 * (
        pressure[:, 4 : lat_cells - 2, 3 : lon_cells - 3]
        - pressure[:, 2 : lat_cells - 4, 3 : lon_cells - 3]
    )
    row_index = (first_row + 3 + jnp.arange(lat_cells - 6, dtype=jnp.int32)).astype(jnp.float32)
    latitude = jnp.pi * ((row_index + 0.5) / lat_total - 0.5)
    coriolis = (rotation * jnp.sin(latitude))[:, None]
    east_now = center[2]
    north_now = center[3]
    force_east = coriolis * north_now - press_east - bottom_drag * bottom_center * east_now
    force_north = -coriolis * east_now - press_north - bottom_drag * bottom_center * north_now
    forcing = jnp.concatenate(
        [jnp.zeros_like(center[:2]), jnp.stack([force_east, force_north])], axis=0
    )
    return (center - courant * divergence + vertical + forcing) * wet_center[None]


def halo(block, sides, width):
    for axis, dim in sides:
        count = lax.axis_size(axis)
        forward = [(i, (i + 1) % count) for i in range(count)]
        backward = [(target, source) for source, target in forward]
        low = lax.ppermute(
            lax.slice_in_dim(block, block.shape[dim] - width, None, axis=dim), axis, forward
        )
        high = lax.ppermute(lax.slice_in_dim(block, 0, width, axis=dim), axis, backward)
        block = jnp.concatenate([low, block, high], axis=dim)
    return block


def inside_rows(lat_start, rim_depth, row_count, lat_total):
    global_row = lat_start - rim_depth + jnp.arange(row_count + 2 * rim_depth, dtype=jnp.int32)
    return ((global_row >= 0) & (global_row < lat_total))[:, None]


def shards(state, cotangent, seamask, levels):
    fields, level_count, row_count, col_count = state.shape
    lat_total = row_count * lax.axis_size("lat")
    lat_start = lax.axis_index("lat") * row_count
    margin = 12
    reach = 6
    planes = fields * level_count
    stacked = jnp.concatenate(
        [
            state.reshape(planes, row_count, col_count),
            cotangent.reshape(planes, row_count, col_count),
            seamask.astype(jnp.float32)[None],
            levels.astype(jnp.float32)[None],
        ],
        axis=0,
    )
    wide = halo(stacked, (("lon", 2), ("lat", 1)), margin)
    inside = inside_rows(lat_start, margin, row_count, lat_total)
    wide = wide * inside.astype(jnp.float32)
    cut = margin - reach
    slab = wide[:planes].reshape(fields, level_count, *wide.shape[1:])
    cot_slab = wide[planes : 2 * planes, cut:-cut, cut:-cut].reshape(
        fields, level_count, row_count + 2 * reach, col_count + 2 * reach
    )
    sea_slab = wide[2 * planes].astype(jnp.int32)
    lev_slab = wide[2 * planes + 1].astype(jnp.int32)
    first_row = lat_start - margin

    def two_steps(rows_in):
        half_way = advance(rows_in, sea_slab, lev_slab, first_row, lat_total)
        return advance(half_way, sea_slab[3:-3, 3:-3], lev_slab[3:-3, 3:-3], first_row + 3, lat_total)

    ahead, backward = jax.vjp(two_steps, slab)
    gradient = backward(cot_slab)[0]
    final_state = ahead[:, :, reach : reach + row_count, reach : reach + col_count]
    adjoint_state = gradient[:, :, margin : margin + row_count, margin : margin + col_count]
    return (final_state, adjoint_state)


def solution(mesh):
    placed = (
        P(None, None, "lat", "lon"),
        P(None, None, "lat", "lon"),
        P("lat", "lon"),
        P("lat", "lon"),
    )
    return jax.shard_map(
        shards,
        mesh=mesh,
        in_specs=placed,
        out_specs=(P(None, None, "lat", "lon"), P(None, None, "lat", "lon")),
        check_vma=False,
    )
```

profile of v0, /device:TPU:1, one launch (start us, length us, event | category | flops | bytes accessed | tf_op | source)
XLA Modules:
  0.0 123.0 jit_solution(9906363649710863062)
XLA Ops:
  1.4 1.3 %pad_maximum_fusion.1 = f32[34,32,256]{2,1,0:T(8,128)S(1)} fusion(f32[1,32,256]{2,1,0:T(8,128)S(1)} %get-tuple-element.147, f32[1,32,256]{2,1,0:T(8,128)S(1)} %get-tuple-element.148, f32[16,32,256]{2,1,0:T(8,128)} %bitcast.133, f32[16,32,256]{2,1,0:T(8,128)} %bitcast.136), kind=kLoop, calls=%fused_computation.80 | loop fusion | flops 835584 | bytes 2228224 | tf_op jit(solution)/shard_map/concatenate | solution.py:104
  3.4 2.5 %collective-permute-start = (f32[34,32,12]{0,1,2:T(8,128)S(1)}, f32[34,32,12]{0,1,2:T(8,128)S(1)}, u32[]{:S(2)}, u32[]{:S(2)}) collective-permute-start(f32[34,32,12]{0,1,2:T(8,128)S(1)} %copy.17), channel_id=1, source_target_pairs={{0,16},{16,32},{32,48},{48,64},{64,80},{80,96},{96,112},{112,128},... | collective-permute-start | bytes 156680 | tf_op jit(solution)/shard_map/ppermute | solution.py:84
  6.4 5.0 %collective-permute-start.1 = (f32[34,32,12]{0,1,2:T(8,128)S(1)}, f32[34,32,12]{0,1,2:T(8,128)S(1)}, u32[]{:S(2)}, u32[]{:S(2)}) collective-permute-start(f32[34,32,12]{0,1,2:T(8,128)S(1)} %copy.18), channel_id=1, source_target_pairs={{16,0},{32,16},{48,32},{64,48},{80,64},{96,80},{112,96},{128,112},... | collective-permute-start | bytes 156680 | tf_op jit(solution)/shard_map/ppermute | solution.py:87
  11.4 4.0 %collective-permute-done = f32[34,32,12]{0,1,2:T(8,128)S(1)} collective-permute-done((f32[34,32,12]{0,1,2:T(8,128)S(1)}, f32[34,32,12]{0,1,2:T(8,128)S(1)}, u32[]{:S(2)}, u32[]{:S(2)}) %collective-permute-start) | collective-permute-done | bytes 52256 | tf_op jit(solution)/shard_map/ppermute | solution.py:84
  17.7 3.7 %collective-permute-start.2 = (f32[34,12,280]{2,0,1:T(8,128)S(1)}, f32[34,12,280]{2,0,1:T(8,128)}, u32[]{:S(2)}, u32[]{:S(2)}) collective-permute-start(f32[34,12,280]{2,0,1:T(8,128)S(1)} %copy.21), channel_id=1, source_target_pairs={{0,1},{1,2},{2,3},{3,4},{4,5},{5,6},{6,7},{7,8},{8,9},{9,10},{10,1... | collective-permute-start | bytes 1370888 | tf_op jit(solution)/shard_map/ppermute | solution.py:84
  21.4 1.1 copy.22
  22.6 10.6 %collective-permute-done.2 = f32[34,12,280]{2,0,1:T(8,128)} collective-permute-done((f32[34,12,280]{2,0,1:T(8,128)S(1)}, f32[34,12,280]{2,0,1:T(8,128)}, u32[]{:S(2)}, u32[]{:S(2)}) %collective-permute-start.2) | collective-permute-done | bytes 456992 | tf_op jit(solution)/shard_map/ppermute | solution.py:84
  33.2 1.2 %copy.23 = f32[34,12,280]{2,1,0:T(8,128)S(1)} copy(f32[34,12,280]{2,0,1:T(8,128)} %collective-permute-done.2) | data formatting | bytes 913920 | tf_op jit(solution)/shard_map/ppermute | solution.py:84
  34.4 5.3 %collective-permute-done.3 = f32[34,12,280]{2,0,1:T(8,128)} collective-permute-done((f32[34,12,280]{2,0,1:T(8,128)}, f32[34,12,280]{2,0,1:T(8,128)}, u32[]{:S(2)}, u32[]{:S(2)}) %collective-permute-start.3) | collective-permute-done | bytes 456992 | tf_op jit(solution)/shard_map/ppermute | solution.py:87
  39.8 1.2 %copy.24 = f32[34,12,280]{2,1,0:T(8,128)S(1)} copy(f32[34,12,280]{2,0,1:T(8,128)} %collective-permute-done.3) | data formatting | bytes 913920 | tf_op jit(solution)/shard_map/ppermute | solution.py:87
  41.0 4.1 %maximum_multiply_fusion = f32[34,56,280]{2,1,0:T(8,128)S(1)} fusion(f32[34,12,280]{2,1,0:T(8,128)S(1)} %copy.24, f32[34,32,12]{2,1,0:T(8,128)S(1)} %copy.20, f32[1,32,256]{2,1,0:T(8,128)S(1)} %get-tuple-element.147, f32[1,32,256]{2,1,0:T(8,128)S(1)} %get-tuple-element.148, f32[16,32,256]{2,1,0:T(8,128)S(1)} %bitcast.135, f32[16,32,256]{2,1,0:T(8,128)S(1)} %bitcast.138, ...), kind=kLoop, calls=%fused_computation | loop fusion | flops 4264960 | bytes 4265184 | tf_op jit(solution)/shard_map/mul | solution.py:115
  46.9 1.0 add_sqrt_fusion.2
  51.3 1.2 %add_bitcast_fusion.7 = (f32[1,4,44,268]{3,2,1,0:T(8,128)S(1)}, f32[1,4,44,268]{3,2,1,0:T(8,128)S(1)}, f32[4,44,268]{2,1,0:T(8,128)}, f32[4,44,268]{2,1,0:T(8,12...) fusion(f32[4,4,44,268]{3,2,1,0:T(8,128)S(1)} %get-tuple-element.23, s32[44,268]{1,0:T(8,128)S(1)} %slice.508, ...), kind=kLoop, calls=%fused_computation.215 | loop fusion | flops 754688 | bytes 1604064 | tf_op jit(solution)/shard_map/transpose(jvp())/broadcast_in_dim | solution.py:70
  54.5 1.8 %subtract_multiply_fusion.2 = (f32[4,4,56,275]{3,2,1,0:T(8,128)S(1)}, f32[4,4,56,275]{3,2,1,0:T(8,128)S(1)}, f32[4,4,56,275]{3,2,1,0:T(8,128)S(1)}) fusion(f32[4,56,275]{2,1,0:T(8,128)S(1)} %fusion.54, f32[4,56,275]{2,1,0:T(8,128)S(1)} %get-tuple-element.42, f32[4,56,275]{2,1,0:T(8,128)S(1)} %slice_multiply_fusion.10, f32[4,4,56,280]{3,2,1,0:T(8,128)S(1)} %bitcast.128), kind=kLoop, calls=%fused_computation.38 | loop fusion | flops 4435200 | bytes 9609600 | tf_op jit(solution)/shard_map/jvp()/mul | solution.py:29
  57.0 1.2 %subtract_multiply_fusion.1 = (f32[4,4,51,280]{3,2,1,0:T(8,128)S(1)}, f32[4,4,51,280]{3,2,1,0:T(8,128)S(1)}, f32[4,4,51,280]{3,2,1,0:T(8,128)S(1)}) fusion(f32[4,51,280]{2,1,0:T(8,128)S(1)} %fusion.53, f32[4,51,280]{2,1,0:T(8,128)S(1)} %get-tuple-element.45, f32[4,51,280]{2,1,0:T(8,128)S(1)} %slice_multiply_fusion.9, f32[4,4,56,280]{3,2,1,0:T(8,128)S(1)} %bitcast.129), kind=kLoop, calls=%fused_computation.35 | loop fusion | flops 4112640 | bytes 8910720 | tf_op jit(solution)/shard_map/jvp()/mul | solution.py:29
  60.8 1.5 %fusion.5 = f32[4,4,50,274]{3,2,1,0:T(8,128)S(1)} fusion(f32[4,4,50,280]{3,2,1,0:T(8,128)S(1)} %get-tuple-element.106, f32[4,4,50,280]{3,2,1,0:T(8,128)S(1)} %get-tuple-element.105, f32[4,4,56,274]{3,2,1,0:T(8,128)S(1)} %get-tuple-element.104, f32[4,4,56,274]{3,2,1,0:T(8,128)S(1)} %get-tuple-element.103, f32[1,4,50,274]{3,2,1,0:T(8,128)S(1)} %get-tuple-element.62, ...), kind=kLoop, calls=%fused_computation.8 | loop fusion | flops 3507200 | bytes 7672016 | tf_op jit(solution)/shard_map/jvp()/mul | solution.py:76
  63.8 14.7 %multiply_add_fusion.7 = (f32[4,4,50,269]{3,2,1,0:T(8,128)S(1)}, f32[4,4,50,269]{3,2,1,0:T(8,128)S(1)}, f32[4,4,50,269]{3,2,1,0:T(8,128)S(1)}, f32[4,4,50,269]{3...) fusion(f32[4,4,50,269]{3,2,1,0:T(8,128)S(1)} %get-tuple-element, ...), kind=kLoop, calls=%fused_computation.52 | loop fusion | flops 8070000 | bytes 12912000 | tf_op jit(solution)/shard_map/transpose(jvp())/add_any | solution.py:24
  79.4 1.0 add_bitcast_fusion.4
  81.7 3.0 %multiply_add_fusion.10 = (f32[4,4,45,274]{3,2,1,0:T(8,128)S(1)}, f32[4,4,45,274]{3,2,1,0:T(8,128)S(1)}, f32[4,4,45,274]{3,2,1,0:T(8,128)S(1)}, f32[4,4,45,274]{...) fusion(f32[4,4,45,274]{3,2,1,0:T(8,128)S(1)} %get-tuple-element, ...), kind=kLoop, calls=%fused_computation.82 | loop fusion | flops 7398000 | bytes 11836800 | tf_op jit(solution)/shard_map/transpose(jvp())/add_any | solution.py:24
  86.1 1.2 broadcast_multiply_fusion.9
  87.3 4.6 %broadcast_multiply_fusion.1 = (f32[4,4,50,274]{3,2,1,0:T(8,128)}, f32[4,4,50,274]{3,2,1,0:T(8,128)S(1)}) fusion(f32[4,50,274]{2,1,0:T(8,128)S(1)} %copy-done.20, f32[4,50,274]{2,1,0:T(8,128)S(1)} %copy-done.18, f32[1,4,50,274]{3,2,1,0:T(8,128)S(1)} %copy-done.40, f32[4,4,50,269]{3,2,1,0:T(8,128)S(1)} %get-tuple-element.60, ...), kind=kLoop, calls=%fused_computation.92 | loop fusion | flops 3945600 | bytes 13723008 | tf_op jit(solution)/shard_map/transpose(jvp())/mul | solution.py:55
  91.9 2.2 %add_bitcast_fusion.3 = (f32[1,4,50,274]{3,2,1,0:T(8,128)S(1)}, f32[1,4,50,274]{3,2,1,0:T(8,128)S(1)}, f32[4,50,274]{2,1,0:T(8,128)}, f32[4,50,274]{2,1,0:T(8,12...) fusion(f32[4,4,50,274]{3,2,1,0:T(8,128)S(1)} %get-tuple-element.13, s32[50,274]{1,0:T(8,128)} %copy-done.49, ...), kind=kLoop, calls=%fused_computation.155 | loop fusion | flops 876800 | bytes 1863600 | tf_op jit(solution)/shard_map/transpose(jvp())/broadcast_in_dim | solution.py:70
  94.4 1.2 %copy-done.4 = f32[4,4,50,274]{3,2,1,0:T(8,128)S(1)} copy-done((f32[4,4,50,274]{3,2,1,0:T(8,128)S(1)}, f32[4,4,50,274]{3,2,1,0:T(8,128)}, u32[]{:S(2)}) %copy-start.4) | copy-done | bytes 876824
  96.8 1.5 %fusion.99 = (f32[4,3,44,268]{3,2,1,0:T(8,128)S(1)}, f32[4,3,44,268]{3,2,1,0:T(8,128)}) fusion(f32[4,4,50,274]{3,2,1,0:T(8,128)S(1)} %fusion.5), kind=kLoop, calls=%fused_computation.276 | loop fusion | bytes 2264064 | tf_op jit(solution)/shard_map/jvp()/slice | solution.py:51
  101.3 1.3 %multiply_add_fusion.4 = (f32[4,4,51,280]{3,2,1,0:T(8,128)S(1)}, f32[4,4,51,280]{3,2,1,0:T(8,128)S(1)}, f32[4,4,51,280]{3,2,1,0:T(8,128)S(1)}, f32[4,4,51,280]{3...) fusion(f32[4,4,51,280]{3,2,1,0:T(8,128)S(1)} %get-tuple-element.15, ...), kind=kLoop, calls=%fused_computation.47 | loop fusion | flops 5369280 | bytes 8225280 | tf_op jit(solution)/shard_map/transpose(jvp())/add_any | solution.py:24
  104.2 1.3 %multiply_add_fusion.1 = (f32[4,4,56,275]{3,2,1,0:T(8,128)S(1)}, f32[4,4,56,275]{3,2,1,0:T(8,128)S(1)}, f32[4,4,56,275]{3,2,1,0:T(8,128)S(1)}, f32[4,4,56,275]{3...) fusion(f32[4,4,56,275]{3,2,1,0:T(8,128)S(1)} %get-tuple-element.19, ...), kind=kLoop, calls=%fused_computation.42 | loop fusion | flops 5790400 | bytes 8870400 | tf_op jit(solution)/shard_map/transpose(jvp())/add_any | solution.py:24
  105.7 1.0 add_bitcast_fusion
  109.9 1.4 %fusion.66 = (f32[1,4,44,268]{3,2,1,0:T(8,128)}, f32[1,4,44,268]{3,2,1,0:T(8,128)}) fusion(f32[4,50,274]{2,1,0:T(8,128)S(1)} %reduce-window_multiply_fusion, f32[4,4,50,274]{3,2,1,0:T(8,128)S(1)} %fusion.5, s32[44,268]{1,0:T(8,128)S(1)} %copy-done.51, s32[44,268]{1,0:T(8,128)S(1)} %copy-done.53, f32[44]{0:T(128)S(1)} %get-tuple-element.149, ...), kind=kLoop, calls=%fused_computation.208 | loop fusion | flops 754688 | bytes 1604064 | tf_op jit(solution)/shard_map/jvp()/stack | solution.py:74
  114.0 1.2 %broadcast_multiply_fusion.8 = (f32[1,4,56,280]{3,2,1,0:T(8,128)S(1)}, f32[1,4,56,280]{3,2,1,0:T(8,128)}) fusion(s32[56,280]{1,0:T(8,128)S(1)} %copy-done.23, s32[56,280]{1,0:T(8,128)S(1)} %copy-done.27, f32[4,50,274]{2,1,0:T(8,128)S(1)} %copy-done.37, f32[4,50,274]{2,1,0:T(8,128)S(1)} %copy-done.36, f32[4,50,274]{2,1,0:T(8,128)S(1)} %copy-done.35, ...), kind=kOutput, calls=%fused_computation.226 | output fusion | flops 815360 | bytes 1504000 | tf_op jit(solution)/shard_map/transpose(jvp(jit(cumsum)))/reduce_window_sum | solution.py:57
  115.3 2.7 %pad_add_fusion = f32[4,4,56,280]{3,2,1,0:T(8,128)S(1)} fusion(f32[4,4,56,275]{3,2,1,0:T(8,128)S(1)} %get-tuple-element.18, f32[1,4,56,280]{3,2,1,0:T(8,128)} %add_bitcast_fusion.1, f32[4,4,51,280]{3,2,1,0:T(8,128)S(1)} %get-tuple-element.50, f32[4,4,51,280]{3,2,1,0:T(8,128)S(1)} %get-tuple-element.49, f32[4,4,51,280]{3,2,1,0:T(8,128)S(1)} %get-tuple-element.48, ...), kind=kLoop, calls=%fused_computation.15 | loop fusion | flops 2508800 | bytes 9102080 | tf_op jit(solution)/shard_map/transpose(jvp())/add_any | solution.py:14
  118.1 3.0 %pad_add_fusion.3 = f32[4,4,32,256]{3,2,1,0:T(8,128)} fusion(f32[1,4,56,280]{3,2,1,0:T(8,128)} %add_bitcast_fusion, f32[4,4,56,275]{3,2,1,0:T(8,128)S(1)} %get-tuple-element.55, f32[4,4,56,275]{3,2,1,0:T(8,128)S(1)} %get-tuple-element.54, f32[4,4,56,275]{3,2,1,0:T(8,128)S(1)} %get-tuple-element.53, f32[4,4,56,275]{3,2,1,0:T(8,128)S(1)} %get-tuple-element.52, ...), kind=kLoop, calls=%fused_computation.96 | loop fusion | flops 786432 | bytes 6227456 | tf_op jit(solution)/shard_map/transpose(jvp())/add_any | solution.py:44
  121.1 1.8 %fusion.13 = f32[4,4,32,256]{3,2,1,0:T(8,128)} fusion(f32[1,4,44,268]{3,2,1,0:T(8,128)S(1)} %copy-done.42, f32[1,4,44,268]{3,2,1,0:T(8,128)S(1)} %copy-done.41, f32[4,4,44,268]{3,2,1,0:T(8,128)S(1)} %get-tuple-element.98, f32[4,4,44,268]{3,2,1,0:T(8,128)S(1)} %get-tuple-element.97, f32[4,4,44,268]{3,2,1,0:T(8,128)S(1)} %get-tuple-element.96, ...), kind=kLoop, calls=%fused_computation.104 | loop fusion | flops 1572864 | bytes 3916304 | tf_op jit(solution)/shard_map/jvp()/mul | solution.py:76
  (198 shorter events, 31.2 us)
Async XLA Ops:
  2.9 13.8 %copy-start.2 = (f32[4,4,32,256]{3,2,1,0:T(8,128)S(1)}, f32[4,4,32,256]{3,2,1,0:T(8,128)}, u32[]{:S(2)}) copy-start(f32[4,4,32,256]{3,2,1,0:T(8,128)} %param.5) | copy-start | bytes 1572868
  2.9 13.8 %copy-start.3 = (f32[4,4,32,256]{3,2,1,0:T(8,128)S(1)}, f32[4,4,32,256]{3,2,1,0:T(8,128)}, u32[]{:S(2)}) copy-start(f32[4,4,32,256]{3,2,1,0:T(8,128)} %param.4) | copy-start | bytes 1572868
  3.4 12.0 %collective-permute-start = (f32[34,32,12]{0,1,2:T(8,128)S(1)}, f32[34,32,12]{0,1,2:T(8,128)S(1)}, u32[]{:S(2)}, u32[]{:S(2)}) collective-permute-start(f32[34,32,12]{0,1,2:T(8,128)S(1)} %copy.17), channel_id=1, source_target_pairs={{0,16},{16,32},{32,48},{48,64},{64,80},{80,96},{96,112},{112,128},... | collective-permute-start | bytes 156680 | tf_op jit(solution)/shard_map/ppermute | solution.py:84
  6.4 9.6 %collective-permute-start.1 = (f32[34,32,12]{0,1,2:T(8,128)S(1)}, f32[34,32,12]{0,1,2:T(8,128)S(1)}, u32[]{:S(2)}, u32[]{:S(2)}) collective-permute-start(f32[34,32,12]{0,1,2:T(8,128)S(1)} %copy.18), channel_id=1, source_target_pairs={{16,0},{32,16},{48,32},{64,48},{80,64},{96,80},{112,96},{128,112},... | collective-permute-start | bytes 156680 | tf_op jit(solution)/shard_map/ppermute | solution.py:87
  17.7 15.5 %collective-permute-start.2 = (f32[34,12,280]{2,0,1:T(8,128)S(1)}, f32[34,12,280]{2,0,1:T(8,128)}, u32[]{:S(2)}, u32[]{:S(2)}) collective-permute-start(f32[34,12,280]{2,0,1:T(8,128)S(1)} %copy.21), channel_id=1, source_target_pairs={{0,1},{1,2},{2,3},{3,4},{4,5},{5,6},{6,7},{7,8},{8,9},{9,10},{10,1... | collective-permute-start | bytes 1370888 | tf_op jit(solution)/shard_map/ppermute | solution.py:84
  22.5 17.3 %collective-permute-start.3 = (f32[34,12,280]{2,0,1:T(8,128)}, f32[34,12,280]{2,0,1:T(8,128)}, u32[]{:S(2)}, u32[]{:S(2)}) collective-permute-start(f32[34,12,280]{2,0,1:T(8,128)} %copy.22), channel_id=1, source_target_pairs={{1,0},{2,1},{3,2},{4,3},{5,4},{6,5},{7,6},{8,7},{9,8},{10,9},{11,1... | collective-permute-start | bytes 1370888 | tf_op jit(solution)/shard_map/ppermute | solution.py:87
  45.1 1.7 %copy-start.22 = (s32[56,280]{1,0:T(8,128)}, s32[56,280]{1,0:T(8,128)S(1)}, u32[]{:S(2)}) copy-start(s32[56,280]{1,0:T(8,128)S(1)} %get-tuple-element.44) | copy-start | bytes 188164
  45.1 1.7 %copy-start.26 = (s32[56,280]{1,0:T(8,128)}, s32[56,280]{1,0:T(8,128)S(1)}, u32[]{:S(2)}) copy-start(s32[56,280]{1,0:T(8,128)S(1)} %get-tuple-element.43) | copy-start | bytes 188164
  45.2 14.8 %copy-start.7 = (s32[50,274]{1,0:T(8,128)}, s32[50,274]{1,0:T(8,128)S(1)}, u32[]{:S(2)}) copy-start(s32[50,274]{1,0:T(8,128)S(1)} %slice.467) | copy-start | bytes 164404
  45.6 4.2 %copy-start.30 = (f32[3,44,268]{2,1,0:T(8,128)}, f32[3,44,268]{2,1,0:T(8,128)S(1)}, u32[]{:S(2)}) copy-start(f32[3,44,268]{2,1,0:T(8,128)S(1)} %get-tuple-element.134) | copy-start | bytes 424516
  45.6 4.3 %copy-start.28 = (f32[3,44,268]{2,1,0:T(8,128)}, f32[3,44,268]{2,1,0:T(8,128)S(1)}, u32[]{:S(2)}) copy-start(f32[3,44,268]{2,1,0:T(8,128)S(1)} %get-tuple-element.133) | copy-start | bytes 424516
  46.3 5.0 %copy-start.50 = (s32[44,268]{1,0:T(8,128)}, s32[44,268]{1,0:T(8,128)S(1)}, u32[]{:S(2)}) copy-start(s32[44,268]{1,0:T(8,128)S(1)} %slice.508) | copy-start | bytes 141508
  48.1 6.4 %copy-start.10 = (f32[4,56,275]{2,1,0:T(8,128)}, f32[4,56,275]{2,1,0:T(8,128)S(1)}, u32[]{:S(2)}) copy-start(f32[4,56,275]{2,1,0:T(8,128)S(1)} %slice_multiply_fusion.10) | copy-start | bytes 739204
  48.2 8.8 %copy-start.13 = (f32[4,51,280]{2,1,0:T(8,128)}, f32[4,51,280]{2,1,0:T(8,128)S(1)}, u32[]{:S(2)}) copy-start(f32[4,51,280]{2,1,0:T(8,128)S(1)} %slice_multiply_fusion.9) | copy-start | bytes 685444
  49.5 11.2 %copy-start.17 = (f32[4,50,274]{2,1,0:T(8,128)}, f32[4,50,274]{2,1,0:T(8,128)S(1)}, u32[]{:S(2)}) copy-start(f32[4,50,274]{2,1,0:T(8,128)S(1)} %slice.464) | copy-start | bytes 657604
  49.8 13.5 %copy-start.15 = (f32[4,50,269]{2,1,0:T(8,128)}, f32[4,50,269]{2,1,0:T(8,128)S(1)}, u32[]{:S(2)}) copy-start(f32[4,50,269]{2,1,0:T(8,128)S(1)} %slice_multiply_fusion.5) | copy-start | bytes 645604
  53.7 27.6 %copy-start.24 = (f32[4,45,274]{2,1,0:T(8,128)}, f32[4,45,274]{2,1,0:T(8,128)S(1)}, u32[]{:S(2)}) copy-start(f32[4,45,274]{2,1,0:T(8,128)S(1)} %slice_multiply_fusion.11) | copy-start | bytes 591844
  53.8 6.3 %copy-start.49 = (s32[50,274]{1,0:T(8,128)}, s32[50,274]{1,0:T(8,128)S(1)}, u32[]{:S(2)}) copy-start(s32[50,274]{1,0:T(8,128)S(1)} %slice.459) | copy-start | bytes 164404
  85.6 1.7 %copy-start.18 = (f32[4,50,274]{2,1,0:T(8,128)S(1)}, f32[4,50,274]{2,1,0:T(8,128)}, u32[]{:S(2)}) copy-start(f32[4,50,274]{2,1,0:T(8,128)} %copy-done.17) | copy-start | bytes 657604
  85.6 1.7 %copy-start.20 = (f32[4,50,274]{2,1,0:T(8,128)S(1)}, f32[4,50,274]{2,1,0:T(8,128)}, u32[]{:S(2)}) copy-start(f32[4,50,274]{2,1,0:T(8,128)} %get-tuple-element.143) | copy-start | bytes 657604
  85.6 1.7 %copy-start.40 = (f32[1,4,50,274]{3,2,1,0:T(8,128)S(1)}, f32[1,4,50,274]{3,2,1,0:T(8,128)}, u32[]{:S(2)}) copy-start(f32[1,4,50,274]{3,2,1,0:T(8,128)} %add_bitcast_fusion.4) | copy-start | bytes 657604
  91.9 2.2 %copy-start.19 = (f32[4,50,274]{2,1,0:T(8,128)S(1)}, f32[4,50,274]{2,1,0:T(8,128)}, u32[]{:S(2)}) copy-start(f32[4,50,274]{2,1,0:T(8,128)} %get-tuple-element.141) | copy-start | bytes 657604
  96.8 1.7 %copy-start.31 = (f32[3,44,268]{2,1,0:T(8,128)S(1)}, f32[3,44,268]{2,1,0:T(8,128)}, u32[]{:S(2)}) copy-start(f32[3,44,268]{2,1,0:T(8,128)} %copy-done.30) | copy-start | bytes 424516
  98.4 2.4 %copy-start.12 = (f32[4,51,280]{2,1,0:T(8,128)S(1)}, f32[4,51,280]{2,1,0:T(8,128)}, u32[]{:S(2)}) copy-start(f32[4,51,280]{2,1,0:T(8,128)} %get-tuple-element.16) | copy-start | bytes 685444
  98.4 2.4 %copy-start.14 = (f32[4,51,280]{2,1,0:T(8,128)S(1)}, f32[4,51,280]{2,1,0:T(8,128)}, u32[]{:S(2)}) copy-start(f32[4,51,280]{2,1,0:T(8,128)} %copy-done.13) | copy-start | bytes 685444
  106.9 1.7 %copy-start.43 = (f32[4,45,274]{2,1,0:T(8,128)S(1)}, f32[4,45,274]{2,1,0:T(8,128)}, u32[]{:S(2)}) copy-start(f32[4,45,274]{2,1,0:T(8,128)} %get-tuple-element.136) | copy-start | bytes 591844
  106.9 1.8 %copy-start.44 = (f32[4,45,274]{2,1,0:T(8,128)S(1)}, f32[4,45,274]{2,1,0:T(8,128)}, u32[]{:S(2)}) copy-start(f32[4,45,274]{2,1,0:T(8,128)} %get-tuple-element.140) | copy-start | bytes 591844
  118.0 3.0 %copy-start.41 = (f32[1,4,44,268]{3,2,1,0:T(8,128)S(1)}, f32[1,4,44,268]{3,2,1,0:T(8,128)}, u32[]{:S(2)}) copy-start(f32[1,4,44,268]{3,2,1,0:T(8,128)} %get-tuple-element.63) | copy-start | bytes 566020
  118.0 3.0 %copy-start.42 = (f32[1,4,44,268]{3,2,1,0:T(8,128)S(1)}, f32[1,4,44,268]{3,2,1,0:T(8,128)}, u32[]{:S(2)}) copy-start(f32[1,4,44,268]{3,2,1,0:T(8,128)} %get-tuple-element.64) | copy-start | bytes 566020
  118.0 3.0 %copy-start.54 = (f32[4,32,256]{2,1,0:T(8,128)S(1)}, f32[4,32,256]{2,1,0:T(8,128)}, u32[]{:S(2)}) copy-start(f32[4,32,256]{2,1,0:T(8,128)} %slice.520) | copy-start | bytes 393220
  118.0 3.0 %copy-start.55 = (f32[4,32,256]{2,1,0:T(8,128)S(1)}, f32[4,32,256]{2,1,0:T(8,128)}, u32[]{:S(2)}) copy-start(f32[4,32,256]{2,1,0:T(8,128)} %pad_slice_fusion) | copy-start | bytes 393220
  118.1 3.0 %copy-start.56 = (f32[4,32,256]{2,1,0:T(8,128)S(1)}, f32[4,32,256]{2,1,0:T(8,128)}, u32[]{:S(2)}) copy-start(f32[4,32,256]{2,1,0:T(8,128)} %pad_slice_fusion.1) | copy-start | bytes 393220
  (30 other events, 35.0 us)
where the time goes:
time: 124 us; the launch traced here: 123 us
  other arithmetic  69.9 us (56%)
  local copies, waits for them, and re-layouts  20.3 us (16%)
  waiting for transfers between devices  19.9 us (16%)
  starting transfers between devices  11.2 us (9%)
  between operations  1.81 us (1%)
    add_any x4, other arithmetic, face_div(): cells[1] + cells[4]  20.3 us
    ppermute x2, waiting for transfers between devices, halo(): lax.ppermute(lax.slice_in_dim(block, block.shape[dim] - width, None, axis...  14.6 us
    unnamed x114, local copies, waits for them, and re-layouts  6.35 us
    ppermute x2, starting transfers between devices, halo(): lax.ppermute(lax.slice_in_dim(block, block.shape[dim] - width, None, axis...  6.2 us
    mul x4, other arithmetic, advance(): wet_below * (below_cells - center)  5.65 us
    ppermute x2, waiting for transfers between devices, halo(): lax.ppermute(lax.slice_in_dim(block, 0, width, axis=dim), axis, backward)  5.35 us
    ppermute x2, starting transfers between devices, halo(): lax.ppermute(lax.slice_in_dim(block, 0, width, axis=dim), axis, backward)  4.96 us
    mul x1, other arithmetic, shards(): wide = wide * inside.astype(jnp.float32)  4.06 us
  transfers between devices with their start and end apart: 4, of which 3 were waited for; matrix products, arithmetic and copies ran while one was open for 3% of the time, Pallas kernels for 0%

commit v1 on v0

v1 whole, which is shorter than its diff:
```python
import jax
import jax.numpy as jnp
from jax import lax
from jax.sharding import PartitionSpec as P
from jax.experimental import pallas as pl
from jax.experimental.pallas import tpu as pltpu
import functools

courant = 0.4
vert_mix = 0.1
rotation = 0.3
buoyancy = 0.3
bottom_drag = 0.2


SIXTIETH = 1.0 / 60.0
INTERPRET = False
CENTRAL = {-2: 1.0, -1: -8.0, 0: 37.0, 1: 37.0, 2: -8.0, 3: 1.0}
DAMPING = {-2: -1.0, -1: 5.0, 0: -10.0, 1: 10.0, 2: -5.0, 3: 1.0}


def shifted(x, step, axis):
    n = x.shape[axis]
    step = step % n
    if step == 0:
        return x
    return pltpu.roll(x, n - step, axis)


def wet_of(depth, k):
    return jnp.where(depth > k + 0.5, 1.0, 0.0)


def bottom_of(depth, k):
    return jnp.where(jnp.abs(depth - (k + 1.0)) < 0.5, 1.0, 0.0)


def face_terms(q, axis):
    m2 = shifted(q, -2, axis)
    m1 = shifted(q, -1, axis)
    p1 = shifted(q, 1, axis)
    p2 = shifted(q, 2, axis)
    p3 = shifted(q, 3, axis)
    central = (37.0 * (q + p1) - 8.0 * (m1 + p2) + (m2 + p3)) * SIXTIETH
    damping = (10.0 * (p1 - q) - 5.0 * (p2 - m1) + (p3 - m2)) * SIXTIETH
    return central, damping


def face_speed(wet, speed, axis):
    open_face = wet * shifted(wet, 1, axis)
    w = 0.5 * (speed + shifted(speed, 1, axis))
    s = jnp.sqrt(w * w + 0.0001)
    return open_face, w, s


def forward(src, store, depth, cor):
    level_count = src.shape[1]
    column = None
    for k in range(level_count):
        wet = wet_of(depth, k)
        bottom = bottom_of(depth, k)
        q = [src[f, k] for f in range(4)]
        density = (-0.2 * q[0] + 0.8 * q[1]) * wet
        column = density if column is None else column + density
        pressure = buoyancy * column
        div = [None] * 4
        for axis, speed in ((1, q[2]), (0, q[3])):
            open_face, w, s = face_speed(wet, speed, axis)
            for f in range(4):
                central, damping = face_terms(q[f], axis)
                flux = open_face * (w * central - s * damping)
                part = flux - shifted(flux, -1, axis)
                div[f] = part if div[f] is None else div[f] + part
        press_east = 0.5 * (shifted(pressure, 1, 1) - shifted(pressure, -1, 1))
        press_north = 0.5 * (shifted(pressure, 1, 0) - shifted(pressure, -1, 0))
        force = [
            None,
            None,
            cor * q[3] - press_east - bottom_drag * bottom * q[2],
            -cor * q[2] - press_north - bottom_drag * bottom * q[3],
        ]
        for f in range(4):
            vertical = None
            if k > 0:
                vertical = wet_of(depth, k - 1) * (src[f, k - 1] - q[f])
            if k < level_count - 1:
                below = wet_of(depth, k + 1) * (src[f, k + 1] - q[f])
                vertical = below if vertical is None else vertical + below
            value = q[f] - courant * div[f] + vert_mix * vertical
            if force[f] is not None:
                value = value + force[f]
            store(f, k, value * wet)


def backward(x, lam, store, g_ref, depth, cor):
    level_count = x.shape[1]
    for k in range(level_count):
        wet = wet_of(depth, k)
        for f in range(4):
            g_ref[f, k] = wet * lam[f, k]
    density_bar = [None] * level_count
    column = None
    for k in reversed(range(level_count)):
        gu = g_ref[2, k]
        gv = g_ref[3, k]
        pbar = 0.5 * (shifted(gu, 1, 1) - shifted(gu, -1, 1)) + 0.5 * (
            shifted(gv, 1, 0) - shifted(gv, -1, 0)
        )
        column = pbar if column is None else column + pbar
        density_bar[k] = buoyancy * column
    for k in range(level_count):
        wet = wet_of(depth, k)
        bottom = bottom_of(depth, k)
        q = [x[f, k] for f in range(4)]
        g = [g_ref[f, k] for f in range(4)]
        acc = list(g)
        for f in range(4):
            vertical = None
            if k > 0:
                vertical = wet * g_ref[f, k - 1] - wet_of(depth, k - 1) * g[f]
            if k < level_count - 1:
                below = wet * g_ref[f, k + 1] - wet_of(depth, k + 1) * g[f]
                vertical = below if vertical is None else vertical + below
            acc[f] = acc[f] + vert_mix * vertical
        acc[2] = acc[2] - bottom_drag * bottom * g[2] - cor * g[3]
        acc[3] = acc[3] + cor * g[2] - bottom_drag * bottom * g[3]
        acc[0] = acc[0] - 0.2 * wet * density_bar[k]
        acc[1] = acc[1] + 0.8 * wet * density_bar[k]
        div_bar = [-courant * g[f] for f in range(4)]
        for axis, speed_field in ((1, 2), (0, 3)):
            open_face, w, s = face_speed(wet, q[speed_field], axis)
            ratio = w / s
            w_bar = None
            for f in range(4):
                flux_bar = open_face * (div_bar[f] - shifted(div_bar[f], 1, axis))
                central, damping = face_terms(q[f], axis)
                part = flux_bar * (central - ratio * damping)
                w_bar = part if w_bar is None else w_bar + part
                alpha = flux_bar * w * SIXTIETH
                beta = -flux_bar * s * SIXTIETH
                for j in range(-2, 4):
                    acc[f] = acc[f] + shifted(CENTRAL[j] * alpha + DAMPING[j] * beta, -j, axis)
            acc[speed_field] = acc[speed_field] + 0.5 * (w_bar + shifted(w_bar, -1, axis))
        for f in range(4):
            store(f, k, acc[f])


def two_step_kernel(margin, rows, cols, x0, lam, depth_ref, cor_ref, final_ref, grad_ref, x1, mu, g_ref):
    depth = depth_ref[...]
    cor = cor_ref[...]

    def crop(value):
        return shifted(shifted(value, margin, 0), margin, 1)[:rows, :cols]

    def keep(ref):
        def put(f, k, value):
            ref[f, k] = value
        return put

    def keep_cropped(ref):
        def put(f, k, value):
            ref[f, k] = crop(value)
        return put

    forward(x0, keep(x1), depth, cor)
    forward(x1, keep_cropped(final_ref), depth, cor)
    backward(x1, lam, keep(mu), g_ref, depth, cor)
    backward(x0, mu, keep_cropped(grad_ref), g_ref, depth, cor)


def halo(block, sides, width):
    for axis, dim in sides:
        count = lax.axis_size(axis)
        forward_pairs = [(i, (i + 1) % count) for i in range(count)]
        backward_pairs = [(target, source) for source, target in forward_pairs]
        low = lax.ppermute(
            lax.slice_in_dim(block, block.shape[dim] - width, None, axis=dim), axis, forward_pairs
        )
        high = lax.ppermute(lax.slice_in_dim(block, 0, width, axis=dim), axis, backward_pairs)
        block = jnp.concatenate([low, block, high], axis=dim)
    return block


def inside_rows(lat_start, rim_depth, row_count, lat_total):
    global_row = lat_start - rim_depth + jnp.arange(row_count + 2 * rim_depth, dtype=jnp.int32)
    return ((global_row >= 0) & (global_row < lat_total))[:, None]


def shards(state, cotangent, seamask, levels):
    fields, level_count, row_count, col_count = state.shape
    lat_total = row_count * lax.axis_size("lat")
    lat_start = lax.axis_index("lat") * row_count
    margin = 12
    reach = 6
    planes = fields * level_count
    stacked = jnp.concatenate(
        [
            state.reshape(planes, row_count, col_count),
            (seamask * levels).astype(jnp.float32)[None],
        ],
        axis=0,
    )
    wide = halo(stacked, (("lon", 2), ("lat", 1)), margin)
    cot_wide = halo(
        cotangent.reshape(planes, row_count, col_count), (("lon", 2), ("lat", 1)), reach
    )
    wide = wide * inside_rows(lat_start, margin, row_count, lat_total).astype(jnp.float32)
    cot_wide = cot_wide * inside_rows(lat_start, reach, row_count, lat_total).astype(jnp.float32)
    frame_rows = row_count + 2 * margin
    frame_cols = -(-(col_count + 2 * margin) // 128) * 128
    extra = frame_cols - (col_count + 2 * margin)
    cut = margin - reach
    x0 = jnp.pad(wide[:planes], ((0, 0), (0, 0), (0, extra))).reshape(
        fields, level_count, frame_rows, frame_cols
    )
    depth = jnp.pad(wide[planes], ((0, 0), (0, extra)))
    lam = jnp.pad(cot_wide, ((0, 0), (cut, cut), (cut, cut + extra))).reshape(
        fields, level_count, frame_rows, frame_cols
    )
    row_index = (lat_start - margin + jnp.arange(frame_rows, dtype=jnp.int32)).astype(jnp.float32)
    latitude = jnp.pi * ((row_index + 0.5) / lat_total - 0.5)
    cor = jnp.broadcast_to((rotation * jnp.sin(latitude))[:, None], (frame_rows, frame_cols))
    frame = (fields, level_count, frame_rows, frame_cols)
    out_block = jax.ShapeDtypeStruct((fields, level_count, row_count, col_count), jnp.float32)
    vmem = pl.BlockSpec(memory_space=pltpu.VMEM)
    final_state, adjoint_state = pl.pallas_call(
        functools.partial(two_step_kernel, margin, row_count, col_count),
        out_shape=(out_block, out_block),
        in_specs=[vmem, vmem, vmem, vmem],
        out_specs=(vmem, vmem),
        scratch_shapes=[pltpu.VMEM(frame, jnp.float32) for _ in range(3)],
        interpret=INTERPRET,
    )(x0, lam, depth, cor)
    return (final_state, adjoint_state)


def solution(mesh):
    placed = (
        P(None, None, "lat", "lon"),
        P(None, None, "lat", "lon"),
        P("lat", "lon"),
        P("lat", "lon"),
    )
    return jax.shard_map(
        shards,
        mesh=mesh,
        in_specs=placed,
        out_specs=(P(None, None, "lat", "lon"), P(None, None, "lat", "lon")),
        check_vma=False,
    )
```

time: 124 us -> 71.4 us (0.58)
  other arithmetic: 69.9 us -> 3.62 us
  Pallas kernels: 0 us -> 25.8 us
  local copies, waits for them, and re-layouts: 20.3 us -> 4.38 us
  starting transfers between devices: 11.2 us -> 18.2 us
  waiting for transfers between devices: 19.9 us -> 18.6 us
    add_any x12 -> x0, other arithmetic: 28.7 us -> none  [the longest x4 20.3 us: face_div(): cells[1] + cells[4]]
    pallas_call x0 -> x1, Pallas kernels: none -> 25.8 us  [shards(): pl.pallas_call(functools.partial(two_step_kernel, margin, row_count, col_...]
    mul x27 -> x3, other arithmetic: 20.6 us -> 1.05 us  [the longest x1 0.51 us: shards(): wide * inside_rows(lat_start, margin, row_count, lat_total).astype(jnp.fl...]
    slice x21 -> x1, local copies, waits for them, and re-layouts: 8.81 us -> 0.09 us  [shards(): wide[:planes]]
    unnamed x114 -> x4, local copies, waits for them, and re-layouts: 6.35 us -> 0.01 us
    broadcast_in_dim x7 -> x1, other arithmetic: 7.09 us -> 0.84 us  [shards(): (seamask * levels).astype(jnp.float32)[None]]
    another operation x6 -> x0, other arithmetic: 5.05 us -> none  [the longest x4 2.98 us: advance(): pressure = buoyancy * jnp.cumsum(density, axis=0)]
    ppermute x2 -> x4, waiting for transfers between devices: 14.6 us -> 10.3 us  [halo(): lax.ppermute(lax.slice_in_dim(block, block.shape[dim] - width, None, axis...]
  transfers between devices with their start and end apart: 4 -> 8, of which waited for: 3 -> 4; matrix products, arithmetic and copies ran while one was open for 3% -> 4% of each run, Pallas kernels for 0% -> 0%
where the time goes in v1:
time: 71.4 us; the launch traced here: 71.2 us
  Pallas kernels  25.8 us (36%)
  waiting for transfers between devices  18.6 us (26%)
  starting transfers between devices  18.2 us (25%)
  local copies, waits for them, and re-layouts  4.38 us (6%)
  other arithmetic  3.62 us (5%)
  between operations  0.73 us (1%)
    pallas_call x1, Pallas kernels, shards(): pl.pallas_call(functools.partial(two_step_kernel, margin, row_count, col_...  25.8 us
    ppermute x4, waiting for transfers between devices, halo(): lax.ppermute(lax.slice_in_dim(block, block.shape[dim] - width, None, axis...  10.3 us
    ppermute x4, starting transfers between devices, halo(): lax.ppermute(lax.slice_in_dim(block, block.shape[dim] - width, None, axis...  9.6 us
    ppermute x4, starting transfers between devices, halo(): lax.ppermute(lax.slice_in_dim(block, 0, width, axis=dim), axis, backward_...  8.57 us
    ppermute x4, waiting for transfers between devices, halo(): lax.ppermute(lax.slice_in_dim(block, 0, width, axis=dim), axis, backward_...  8.28 us
    pad x1, local copies, waits for them, and re-layouts, shards(): jnp.pad(cot_wide, ((0, 0), (cut, cut), (cut, cut + extra)))  1.54 us
  transfers between devices with their start and end apart: 8, of which 4 were waited for; matrix products, arithmetic and copies ran while one was open for 4% of the time, Pallas kernels for 0%

profile of v1, /device:TPU:1, one launch (start us, length us, event | category | flops | bytes accessed | tf_op | source)
XLA Modules:
  0.0 71.2 jit_solution(10367331447735536265)
XLA Ops:
  0.6 0.0 copy-start
  0.6 0.8 %convert_bitcast_fusion = f32[1,32,256]{2,1,0:T(8,128)S(1)} fusion(s32[32,256]{1,0:T(8,128)} %param.6, s32[32,256]{1,0:T(8,128)} %param.7), kind=kLoop, calls=%fused_computation.11 | loop fusion | flops 16384 | bytes 98304 | tf_op jit(solution)/shard_map/broadcast_in_dim | solution.py:199
  1.5 1.2 %fusion = (f32[17,32,12]{2,1,0:T(8,128)S(1)}, f32[17,32,12]{2,1,0:T(8,128)S(1)}) fusion(f32[16,32,256]{2,1,0:T(8,128)} %bitcast.13, f32[1,32,256]{2,1,0:T(8,128)S(1)} %convert_bitcast_fusion), kind=kLoop, calls=%fused_computation.5 | loop fusion | flops 13056 | bytes 609280 | tf_op jit(solution)/shard_map/concatenate | solution.py:196
  2.6 0.0 copy-start.1
  2.7 2.5 %collective-permute-start = (f32[17,32,12]{2,1,0:T(8,128)S(1)}, f32[17,32,12]{2,1,0:T(8,128)S(1)}, u32[]{:S(2)}, u32[]{:S(2)}) collective-permute-start(f32[17,32,12]{2,1,0:T(8,128)S(1)} %get-tuple-element.6), channel_id=1, source_target_pairs={{0,16},{16,32},{32,48},{48,64},{64,80},{80,96},{96,112},{112,128},... | collective-permute-start | bytes 78344 | tf_op jit(solution)/shard_map/ppermute | solution.py:176
  5.2 5.0 %collective-permute-start.1 = (f32[17,32,12]{2,1,0:T(8,128)S(1)}, f32[17,32,12]{2,1,0:T(8,128)S(1)}, u32[]{:S(2)}, u32[]{:S(2)}) collective-permute-start(f32[17,32,12]{2,1,0:T(8,128)S(1)} %get-tuple-element.7), channel_id=1, source_target_pairs={{16,0},{32,16},{48,32},{64,48},{80,64},{96,80},{112,96},{128,112},... | collective-permute-start | bytes 78344 | tf_op jit(solution)/shard_map/ppermute | solution.py:179
  10.1 0.1 fusion.2
  10.3 0.1 collective-permute-start.4
  10.4 3.6 %collective-permute-start.5 = (f32[16,32,6]{2,1,0:T(8,128)S(1)}, f32[16,32,6]{2,1,0:T(8,128)S(1)}, u32[]{:S(2)}, u32[]{:S(2)}) collective-permute-start(f32[16,32,6]{2,1,0:T(8,128)S(1)} %get-tuple-element.9), channel_id=1, source_target_pairs={{16,0},{32,16},{48,32},{64,48},{80,64},{96,80},{112,96},{128,112},... | collective-permute-start | bytes 36872 | tf_op jit(solution)/shard_map/ppermute | solution.py:179
  14.0 8.0 %collective-permute-done.4 = f32[16,32,6]{2,1,0:T(8,128)S(1)} collective-permute-done((f32[16,32,6]{2,1,0:T(8,128)S(1)}, f32[16,32,6]{2,1,0:T(8,128)S(1)}, u32[]{:S(2)}, u32[]{:S(2)}) %collective-permute-start.4) | collective-permute-done | bytes 12320 | tf_op jit(solution)/shard_map/ppermute | solution.py:176
  22.0 0.0 collective-permute-done.5
  22.0 0.2 pad_maximum_fusion.4
  22.2 3.7 %collective-permute-start.6 = (f32[16,6,268]{2,1,0:T(8,128)S(1)}, f32[16,6,268]{2,1,0:T(8,128)S(1)}, u32[]{:S(2)}, u32[]{:S(2)}) collective-permute-start(f32[16,6,268]{2,1,0:T(8,128)S(1)} %get-tuple-element.2), channel_id=1, source_target_pairs={{0,1},{1,2},{2,3},{3,4},{4,5},{5,6},{6,7},{7,8},{8,9},{9,10},{10,1... | collective-permute-start | bytes 308744 | tf_op jit(solution)/shard_map/ppermute | solution.py:176
  25.9 0.0 collective-permute-start.7
  25.9 0.0 collective-permute-done
  25.9 0.0 collective-permute-done.1
  25.9 0.4 pad_maximum_fusion
  26.3 0.1 fusion.1
  26.4 3.3 %collective-permute-start.2 = (f32[17,12,280]{2,1,0:T(8,128)S(1)}, f32[17,12,280]{2,1,0:T(8,128)S(1)}, u32[]{:S(2)}, u32[]{:S(2)}) collective-permute-start(f32[17,12,280]{2,1,0:T(8,128)S(1)} %get-tuple-element.4), channel_id=1, source_target_pairs={{0,1},{1,2},{2,3},{3,4},{4,5},{5,6},{6,7},{7,8},{8,9},{9,10},{10,1... | collective-permute-start | bytes 685448 | tf_op jit(solution)/shard_map/ppermute | solution.py:176
  29.7 0.0 collective-permute-start.3
  29.7 0.0 collective-permute-done.6
  29.7 2.9 %collective-permute-done.7 = f32[16,6,268]{2,1,0:T(8,128)S(1)} collective-permute-done((f32[16,6,268]{2,1,0:T(8,128)S(1)}, f32[16,6,268]{2,1,0:T(8,128)S(1)}, u32[]{:S(2)}, u32[]{:S(2)}) %collective-permute-start.7) | collective-permute-done | bytes 102944 | tf_op jit(solution)/shard_map/ppermute | solution.py:179
  32.6 0.5 maximum_multiply_fusion.1
  33.1 1.5 %pad.13 = f32[16,56,384]{2,1,0:T(8,128)} pad(f32[16,44,268]{2,1,0:T(8,128)S(1)} %maximum_multiply_fusion.1, f32[]{:T(128)} %constant.9.clone.1), padding=0_0x6_6x6_110 | pad | bytes 2130948 | tf_op jit(solution)/shard_map/jit(_pad)/pad | solution.py:217
  34.6 2.3 %collective-permute-done.2 = f32[17,12,280]{2,1,0:T(8,128)S(1)} collective-permute-done((f32[17,12,280]{2,1,0:T(8,128)S(1)}, f32[17,12,280]{2,1,0:T(8,128)S(1)}, u32[]{:S(2)}, u32[]{:S(2)}) %collective-permute-start.2) | collective-permute-done | bytes 228512 | tf_op jit(solution)/shard_map/ppermute | solution.py:176
  36.9 5.4 %collective-permute-done.3 = f32[17,12,280]{2,1,0:T(8,128)S(1)} collective-permute-done((f32[17,12,280]{2,1,0:T(8,128)S(1)}, f32[17,12,280]{2,1,0:T(8,128)S(1)}, u32[]{:S(2)}, u32[]{:S(2)}) %collective-permute-start.3) | collective-permute-done | bytes 228512 | tf_op jit(solution)/shard_map/ppermute | solution.py:179
  42.3 0.5 maximum_multiply_fusion
  42.8 0.1 slice.44
  42.9 1.2 %pad.12 = f32[16,56,384]{2,1,0:T(8,128)} pad(f32[16,56,280]{2,1,0:T(8,128)S(1)} %slice.44, f32[]{:T(128)} %constant.9.clone.1), padding=0_0x0_0x0_104 | pad | bytes 2379780 | tf_op jit(solution)/shard_map/jit(_pad)/pad | solution.py:213
  44.1 0.6 pad.14.depth_ref
  44.8 0.7 broadcast_in_dim.5.cor_ref
  45.5 25.8 %shard_map.59 = (f32[4,4,32,256]{3,2,1,0:T(8,128)}, f32[4,4,32,256]{3,2,1,0:T(8,128)}) custom-call(f32[4,4,56,384]{3,2,1,0:T(8,128)} %bitcast.9, f32[4,4,56,384]{3,2,1,0:T(8,128)} %bitcast.8, f32[56,384]{1,0:T(8,128)} %pad.14.depth_ref, f32[56,384]{1,0:T(8,128)} %broadcast_in_dim.5.cor_ref), custom_call_target="tpu_custom_call" | custom-call | tf_op jit(solution)/shard_map/pallas_call | solution.py:226
  (6 shorter events, 0.1 us)
Async XLA Ops:
  0.6 9.5 %copy-start = (f32[4,4,32,256]{3,2,1,0:T(8,128)S(1)}, f32[4,4,32,256]{3,2,1,0:T(8,128)}, u32[]{:S(2)}) copy-start(f32[4,4,32,256]{3,2,1,0:T(8,128)} %param.5) | copy-start | bytes 1572868
  2.6 23.3 %copy-start.1 = (f32[4,4,32,256]{3,2,1,0:T(8,128)S(1)}, f32[4,4,32,256]{3,2,1,0:T(8,128)}, u32[]{:S(2)}) copy-start(f32[4,4,32,256]{3,2,1,0:T(8,128)} %param.4) | copy-start | bytes 1572868
  2.7 23.3 %collective-permute-start = (f32[17,32,12]{2,1,0:T(8,128)S(1)}, f32[17,32,12]{2,1,0:T(8,128)S(1)}, u32[]{:S(2)}, u32[]{:S(2)}) collective-permute-start(f32[17,32,12]{2,1,0:T(8,128)S(1)} %get-tuple-element.6), channel_id=1, source_target_pairs={{0,16},{16,32},{32,48},{48,64},{64,80},{80,96},{96,112},{112,128},... | collective-permute-start | bytes 78344 | tf_op jit(solution)/shard_map/ppermute | solution.py:176
  5.2 20.7 %collective-permute-start.1 = (f32[17,32,12]{2,1,0:T(8,128)S(1)}, f32[17,32,12]{2,1,0:T(8,128)S(1)}, u32[]{:S(2)}, u32[]{:S(2)}) collective-permute-start(f32[17,32,12]{2,1,0:T(8,128)S(1)} %get-tuple-element.7), channel_id=1, source_target_pairs={{16,0},{32,16},{48,32},{64,48},{80,64},{96,80},{112,96},{128,112},... | collective-permute-start | bytes 78344 | tf_op jit(solution)/shard_map/ppermute | solution.py:179
  10.3 11.7 %collective-permute-start.4 = (f32[16,32,6]{2,1,0:T(8,128)S(1)}, f32[16,32,6]{2,1,0:T(8,128)S(1)}, u32[]{:S(2)}, u32[]{:S(2)}) collective-permute-start(f32[16,32,6]{2,1,0:T(8,128)S(1)} %get-tuple-element.8), channel_id=1, source_target_pairs={{0,16},{16,32},{32,48},{48,64},{64,80},{80,96},{96,112},{112,128},... | collective-permute-start | bytes 36872 | tf_op jit(solution)/shard_map/ppermute | solution.py:176
  10.4 11.7 %collective-permute-start.5 = (f32[16,32,6]{2,1,0:T(8,128)S(1)}, f32[16,32,6]{2,1,0:T(8,128)S(1)}, u32[]{:S(2)}, u32[]{:S(2)}) collective-permute-start(f32[16,32,6]{2,1,0:T(8,128)S(1)} %get-tuple-element.9), channel_id=1, source_target_pairs={{16,0},{32,16},{48,32},{64,48},{80,64},{96,80},{112,96},{128,112},... | collective-permute-start | bytes 36872 | tf_op jit(solution)/shard_map/ppermute | solution.py:179
  22.2 7.5 %collective-permute-start.6 = (f32[16,6,268]{2,1,0:T(8,128)S(1)}, f32[16,6,268]{2,1,0:T(8,128)S(1)}, u32[]{:S(2)}, u32[]{:S(2)}) collective-permute-start(f32[16,6,268]{2,1,0:T(8,128)S(1)} %get-tuple-element.2), channel_id=1, source_target_pairs={{0,1},{1,2},{2,3},{3,4},{4,5},{5,6},{6,7},{7,8},{8,9},{9,10},{10,1... | collective-permute-start | bytes 308744 | tf_op jit(solution)/shard_map/ppermute | solution.py:176
  25.9 6.7 %collective-permute-start.7 = (f32[16,6,268]{2,1,0:T(8,128)S(1)}, f32[16,6,268]{2,1,0:T(8,128)S(1)}, u32[]{:S(2)}, u32[]{:S(2)}) collective-permute-start(f32[16,6,268]{2,1,0:T(8,128)S(1)} %get-tuple-element.3), channel_id=1, source_target_pairs={{1,0},{2,1},{3,2},{4,3},{5,4},{6,5},{7,6},{8,7},{9,8},{10,9},{11,1... | collective-permute-start | bytes 308744 | tf_op jit(solution)/shard_map/ppermute | solution.py:179
  26.4 10.6 %collective-permute-start.2 = (f32[17,12,280]{2,1,0:T(8,128)S(1)}, f32[17,12,280]{2,1,0:T(8,128)S(1)}, u32[]{:S(2)}, u32[]{:S(2)}) collective-permute-start(f32[17,12,280]{2,1,0:T(8,128)S(1)} %get-tuple-element.4), channel_id=1, source_target_pairs={{0,1},{1,2},{2,3},{3,4},{4,5},{5,6},{6,7},{7,8},{8,9},{9,10},{10,1... | collective-permute-start | bytes 685448 | tf_op jit(solution)/shard_map/ppermute | solution.py:176
  29.7 12.6 %collective-permute-start.3 = (f32[17,12,280]{2,1,0:T(8,128)S(1)}, f32[17,12,280]{2,1,0:T(8,128)S(1)}, u32[]{:S(2)}, u32[]{:S(2)}) collective-permute-start(f32[17,12,280]{2,1,0:T(8,128)S(1)} %get-tuple-element.5), channel_id=1, source_target_pairs={{1,0},{2,1},{3,2},{4,3},{5,4},{6,5},{7,6},{8,7},{9,8},{10,9},{11,1... | collective-permute-start | bytes 685448 | tf_op jit(solution)/shard_map/ppermute | solution.py:179

commit v2 on v1

--- a/solution.py
+++ b/solution.py
@@ -168,17 +168,55 @@
     backward(x0, mu, keep_cropped(grad_ref), g_ref, depth, cor)
 
 
-def halo(block, sides, width):
-    for axis, dim in sides:
-        count = lax.axis_size(axis)
-        forward_pairs = [(i, (i + 1) % count) for i in range(count)]
-        backward_pairs = [(target, source) for source, target in forward_pairs]
-        low = lax.ppermute(
-            lax.slice_in_dim(block, block.shape[dim] - width, None, axis=dim), axis, forward_pairs
-        )
-        high = lax.ppermute(lax.slice_in_dim(block, 0, width, axis=dim), axis, backward_pairs)
-        block = jnp.concatenate([low, block, high], axis=dim)
-    return block
+def ring(count, step):
+    return [(i, (i + step) % count) for i in range(count)]
+
+
+def lat_round(blocks, widths):
+    count = lax.axis_size("lat")
+    cols = blocks[0].shape[-1]
+
+    def message(take_last):
+        parts = []
+        for b, w in zip(blocks, widths):
+            piece = b[:, b.shape[1] - w :, :] if take_last else b[:, :w, :]
+            parts.append(piece.reshape(-1, cols))
+        return jnp.concatenate(parts, axis=0)
+
+    lows = lax.ppermute(message(True), "lat", ring(count, 1))
+    highs = lax.ppermute(message(False), "lat", ring(count, -1))
+    out = []
+    offset = 0
+    for b, w in zip(blocks, widths):
+        n = b.shape[0] * w
+        lo = lows[offset : offset + n].reshape(b.shape[0], w, cols)
+        hi = highs[offset : offset + n].reshape(b.shape[0], w, cols)
+        offset += n
+        out.append(jnp.concatenate([lo, b, hi], axis=1))
+    return out
+
+
+def lon_round(blocks, width):
+    count = lax.axis_size("lon")
+
+    def message(take_last):
+        parts = []
+        for b in blocks:
+            piece = b[:, :, b.shape[2] - width :] if take_last else b[:, :, :width]
+            parts.append(jnp.transpose(piece, (2, 0, 1)).reshape(width, -1))
+        return jnp.concatenate(parts, axis=1)
+
+    lows = lax.ppermute(message(True), "lon", ring(count, 1))
+    highs = lax.ppermute(message(False), "lon", ring(count, -1))
+    out = []
+    offset = 0
+    for b in blocks:
+        n = b.shape[0] * b.shape[1]
+        lo = jnp.transpose(lows[:, offset : offset + n].reshape(width, b.shape[0], b.shape[1]), (1, 2, 0))
+        hi = jnp.transpose(highs[:, offset : offset + n].reshape(width, b.shape[0], b.shape[1]), (1, 2, 0))
+        offset += n
+        out.append(jnp.concatenate([lo, b, hi], axis=2))
+    return out
 
 
 def inside_rows(lat_start, rim_depth, row_count, lat_total):
@@ -200,10 +238,9 @@
         ],
         axis=0,
     )
-    wide = halo(stacked, (("lon", 2), ("lat", 1)), margin)
-    cot_wide = halo(
-        cotangent.reshape(planes, row_count, col_count), (("lon", 2), ("lat", 1)), reach
-    )
+    cot = cotangent.reshape(planes, row_count, col_count)
+    wide, cot_wide = lat_round([stacked, cot], [margin, reach])
+    wide, cot_wide = lon_round([wide, cot_wide], margin)
     wide = wide * inside_rows(lat_start, margin, row_count, lat_total).astype(jnp.float32)
     cot_wide = cot_wide * inside_rows(lat_start, reach, row_count, lat_total).astype(jnp.float32)
     frame_rows = row_count + 2 * margin
@@ -214,7 +251,7 @@
         fields, level_count, frame_rows, frame_cols
     )
     depth = jnp.pad(wide[planes], ((0, 0), (0, extra)))
-    lam = jnp.pad(cot_wide, ((0, 0), (cut, cut), (cut, cut + extra))).reshape(
+    lam = jnp.pad(cot_wide, ((0, 0), (cut, cut), (0, extra))).reshape(
         fields, level_count, frame_rows, frame_cols
     )
     row_index = (lat_start - margin + jnp.arange(frame_rows, dtype=jnp.int32)).astype(jnp.float32)

time: 71.4 us -> 70.5 us (0.987)
  local copies, waits for them, and re-layouts: 4.38 us -> 13.8 us
  starting transfers between devices: 18.2 us -> 10.8 us
  waiting for transfers between devices: 18.6 us -> 15 us
    ppermute x8 -> x4, starting transfers between devices: 18.2 us -> 10.8 us  [the longest x1 6.34 us: lon_round(): highs = lax.ppermute(message(False), 'lon', ring(count, -1))]
    slice x2 -> x14, local copies, waits for them, and re-layouts: 0.19 us -> 5.41 us  [the longest x2 1.85 us: lat_round(): hi = highs[offset:offset + n].reshape(b.shape[0], w, cols)]
    ppermute x8 -> x4, waiting for transfers between devices: 18.6 us -> 15 us  [the longest x1 6.27 us: lon_round(): lows = lax.ppermute(message(True), 'lon', ring(count, 1))]
    unnamed x4 -> x11, local copies, waits for them, and re-layouts: 0.01 us -> 1.88 us
    mul x1, other arithmetic: 0.51 us -> 1.92 us  [shards(): wide * inside_rows(lat_start, margin, row_count, lat_total).astype(jnp.fl...]
    transpose x0 -> x5, local copies, waits for them, and re-layouts: none -> 1.17 us  [the longest x3 0.62 us: message(): parts.append(jnp.transpose(piece, (2, 0, 1)).reshape(width, -1))]
    concatenate x1, other arithmetic: 1.16 us -> 0.04 us  [shards(): jnp.concatenate([state.reshape(planes, row_count, col_count), (seamask *...]
    reshape x0 -> x14, local copies, waits for them, and re-layouts: none -> 0.98 us  [the longest x4 0.61 us: message(): parts.append(jnp.transpose(piece, (2, 0, 1)).reshape(width, -1))]
  transfers between devices with their start and end apart: 8 -> 4, of which waited for: 4 -> 3; matrix products, arithmetic and copies ran while one was open for 4% -> 2% of each run, Pallas kernels for 0% -> 0%
where the time goes in v2:
time: 70.5 us; the launch traced here: 70.2 us
  Pallas kernels  26 us (37%)
  waiting for transfers between devices  15 us (21%)
  local copies, waits for them, and re-layouts  13.8 us (20%)
  starting transfers between devices  10.8 us (15%)
  other arithmetic  3.62 us (5%)
  between operations  0.94 us (1%)
    pallas_call x1, Pallas kernels, shards(): pl.pallas_call(functools.partial(two_step_kernel, margin, row_count, col_...  26 us
    ppermute x1, starting transfers between devices, lon_round(): highs = lax.ppermute(message(False), 'lon', ring(count, -1))  6.34 us
    ppermute x1, waiting for transfers between devices, lon_round(): lows = lax.ppermute(message(True), 'lon', ring(count, 1))  6.27 us
    ppermute x1, waiting for transfers between devices, lat_round(): highs = lax.ppermute(message(False), 'lat', ring(count, -1))  5.22 us
    ppermute x1, starting transfers between devices, lat_round(): lows = lax.ppermute(message(True), 'lat', ring(count, 1))  4.2 us
    ppermute x1, waiting for transfers between devices, lat_round(): lows = lax.ppermute(message(True), 'lat', ring(count, 1))  3.48 us
    mul x1, other arithmetic, shards(): wide * inside_rows(lat_start, margin, row_count, lat_total).astype(jnp.fl...  1.92 us
    unnamed x11, local copies, waits for them, and re-layouts  1.88 us
  transfers between devices with their start and end apart: 4, of which 3 were waited for; matrix products, arithmetic and copies ran while one was open for 2% of the time, Pallas kernels for 0%

profile of v2, /device:TPU:1, one launch (start us, length us, event | category | flops | bytes accessed | tf_op | source)
XLA Modules:
  0.0 70.2 jit_solution(7793025323148865789)
XLA Ops:
  0.6 1.0 %fusion.2 = (f32[16,6,256]{2,1,0:T(8,128)S(1)}, f32[16,6,256]{2,1,0:T(8,128)S(1)}) fusion(f32[16,32,256]{2,1,0:T(8,128)} %bitcast.35), kind=kLoop, calls=%fused_computation.23 | loop fusion | bytes 393216 | tf_op jit(solution)/shard_map/slice | solution.py:182
  1.8 0.8 %convert_bitcast_fusion = f32[1,32,256]{2,1,0:T(8,128)S(1)} fusion(s32[32,256]{1,0:T(8,128)} %param.6, s32[32,256]{1,0:T(8,128)} %param.7), kind=kLoop, calls=%fused_computation.16 | loop fusion | flops 16384 | bytes 98304 | tf_op jit(solution)/shard_map/broadcast_in_dim | solution.py:237
  2.7 4.2 %collective-permute-start = (f32[300,256]{1,0:T(8,128)S(1)}, f32[300,256]{1,0:T(8,128)S(1)}, u32[]{:S(2)}, u32[]{:S(2)}) collective-permute-start(f32[300,256]{1,0:T(8,128)S(1)} %pad_maximum_fusion.1), channel_id=1, source_target_pairs={{0,1},{1,2},{2,3},{3,4},{4,5},{5,6},{6,7},{7,8},{8,9},{9,10},{10,1... | collective-permute-start | bytes 921608 | tf_op jit(solution)/shard_map/ppermute | solution.py:186
  7.3 3.5 %collective-permute-done = f32[300,256]{1,0:T(8,128)S(1)} collective-permute-done((f32[300,256]{1,0:T(8,128)S(1)}, f32[300,256]{1,0:T(8,128)S(1)}, u32[]{:S(2)}, u32[]{:S(2)}) %collective-permute-start) | collective-permute-done | bytes 307232 | tf_op jit(solution)/shard_map/ppermute | solution.py:186
  10.9 5.2 %collective-permute-done.1 = f32[300,256]{1,0:T(8,128)} collective-permute-done((f32[300,256]{1,0:T(8,128)S(1)}, f32[300,256]{1,0:T(8,128)}, u32[]{:S(2)}, u32[]{:S(2)}) %collective-permute-start.1) | collective-permute-done | bytes 307232 | tf_op jit(solution)/shard_map/ppermute | solution.py:187
  16.1 0.9 %slice.80 = f32[96,256]{1,0:T(8,128)S(1)} slice(f32[300,256]{1,0:T(8,128)} %collective-permute-done.1), slice={[204:300], [0:256]} | slice | bytes 196608 | tf_op jit(solution)/shard_map/slice | solution.py:193
  17.0 0.9 %slice.77 = f32[204,256]{1,0:T(8,128)S(1)} slice(f32[300,256]{1,0:T(8,128)} %collective-permute-done.1), slice={[0:204], [0:256]} | slice | bytes 417792 | tf_op jit(solution)/shard_map/slice | solution.py:193
  18.0 0.3 constant_dynamic-update-slice_fusion
  18.4 0.2 slice_bitcast_fusion.1
  18.6 0.2 copy.19
  18.8 0.1 reshape.106
  18.9 0.2 copy.22
  19.4 0.2 fusion.1
  19.6 0.2 copy.20
  19.7 0.2 copy.23
  20.0 6.3 %collective-permute-start.3 = (f32[12,1656]{1,0:T(8,128)S(1)}, f32[12,1656]{1,0:T(8,128)S(1)}, u32[]{:S(2)}, u32[]{:S(2)}) collective-permute-start(f32[12,1656]{1,0:T(8,128)S(1)} %pad_maximum_fusion.5), channel_id=1, source_target_pairs={{0,240},{16,0},{32,16},{48,32},{64,48},{80,64},{96,80},{112,96},{1... | collective-permute-start | bytes 238472 | tf_op jit(solution)/shard_map/ppermute | solution.py:210
  26.5 0.2 collective-permute-start.2
  26.7 6.3 %collective-permute-done.2 = f32[12,1656]{1,0:T(8,128)S(1)} collective-permute-done((f32[12,1656]{1,0:T(8,128)S(1)}, f32[12,1656]{1,0:T(8,128)S(1)}, u32[]{:S(2)}, u32[]{:S(2)}) %collective-permute-start.2) | collective-permute-done | bytes 79520 | tf_op jit(solution)/shard_map/ppermute | solution.py:209
  33.0 1.0 %copy.21 = f32[12,952]{0,1:T(8,128)} copy(f32[12,952]{1,0:T(8,128)S(1)} %slice.82) | data formatting | bytes 91392 | tf_op jit(solution)/shard_map/slice | solution.py:215
  34.0 1.0 %copy.24 = f32[12,952]{0,1:T(8,128)} copy(f32[12,952]{1,0:T(8,128)S(1)} %slice.85) | data formatting | bytes 91392 | tf_op jit(solution)/shard_map/slice | solution.py:216
  35.0 1.9 %maximum_multiply_fusion = f32[17,56,280]{2,1,0:T(8,128)S(1)} fusion(f32[17,56,12]{2,1,0:T(8,128)} %bitcast.32, f32[17,12,256]{2,1,0:T(8,128)S(1)} %reshape.102, f32[1,32,256]{2,1,0:T(8,128)S(1)} %convert_bitcast_fusion, f32[16,32,256]{2,1,0:T(8,128)S(1)} %bitcast.30, f32[17,12,256]{2,1,0:T(8,128)S(1)} %reshape.99, f32[17,56,12]{2,1,0:T(8,128)} %bitcast.31, ...), kind=kLoop, calls=%fused_computation | loop fusion | flops 1599360 | bytes 2132704 | tf_op jit(solution)/shard_map/mul | solution.py:244
  36.9 1.1 %copy-done = f32[17,56,280]{2,1,0:T(8,128)} copy-done((f32[17,56,280]{2,1,0:T(8,128)}, f32[17,56,280]{2,1,0:T(8,128)S(1)}, u32[]{:S(2)}) %copy-start) | copy-done | bytes 1066264
  38.4 0.3 copy.25
  38.7 0.3 copy.26
  39.0 0.5 maximum_multiply_fusion.1
  39.5 0.4 copy.29
  39.8 1.2 %pad.13.clone = f32[16,56,384]{2,1,0:T(8,128)} pad(f32[16,44,280]{2,1,0:T(8,128)S(1)} %copy.29, f32[]{:T(128)} %constant.9.clone.1), padding=0_0x6_6x0_104 | pad | bytes 2164740 | tf_op jit(solution)/shard_map/jit(_pad)/pad | solution.py:254
  41.0 0.6 slice-done
  41.7 1.2 %pad.12 = f32[16,56,384]{2,1,0:T(8,128)} pad(f32[16,56,280]{2,1,0:T(8,128)S(1)} %slice-done, f32[]{:T(128)} %constant.9.clone.1), padding=0_0x0_0x0_104 | pad | bytes 2379780 | tf_op jit(solution)/shard_map/jit(_pad)/pad | solution.py:250
  42.8 0.6 pad.14.depth_ref
  43.5 0.7 %broadcast_in_dim.5.cor_ref = f32[56,384]{1,0:T(8,128)} broadcast(f32[56]{0:T(128)S(1)} %sine_multiply_fusion), dimensions={0} | broadcast | bytes 86240 | tf_op jit(solution)/shard_map/broadcast_in_dim | solution.py:259
  44.2 26.0 %shard_map.59 = (f32[4,4,32,256]{3,2,1,0:T(8,128)}, f32[4,4,32,256]{3,2,1,0:T(8,128)}) custom-call(f32[4,4,56,384]{3,2,1,0:T(8,128)} %bitcast.27, f32[4,4,56,384]{3,2,1,0:T(8,128)} %bitcast.26, f32[56,384]{1,0:T(8,128)} %pad.14.depth_ref, f32[56,384]{1,0:T(8,128)} %broadcast_in_dim.5.cor_ref), custom_call_target="tpu_custom_call" | custom-call | tf_op jit(solution)/shard_map/pallas_call | solution.py:263
  (41 shorter events, 1.5 us)
Async XLA Ops:
  0.6 2.0 %copy-start.1 = (f32[4,4,32,256]{3,2,1,0:T(8,128)S(1)}, f32[4,4,32,256]{3,2,1,0:T(8,128)}, u32[]{:S(2)}) copy-start(f32[4,4,32,256]{3,2,1,0:T(8,128)} %param.4) | copy-start | bytes 1572868
  2.7 8.0 %collective-permute-start = (f32[300,256]{1,0:T(8,128)S(1)}, f32[300,256]{1,0:T(8,128)S(1)}, u32[]{:S(2)}, u32[]{:S(2)}) collective-permute-start(f32[300,256]{1,0:T(8,128)S(1)} %pad_maximum_fusion.1), channel_id=1, source_target_pairs={{0,1},{1,2},{2,3},{3,4},{4,5},{5,6},{6,7},{7,8},{8,9},{9,10},{10,1... | collective-permute-start | bytes 921608 | tf_op jit(solution)/shard_map/ppermute | solution.py:186
  7.1 9.0 %collective-permute-start.1 = (f32[300,256]{1,0:T(8,128)S(1)}, f32[300,256]{1,0:T(8,128)}, u32[]{:S(2)}, u32[]{:S(2)}) collective-permute-start(f32[300,256]{1,0:T(8,128)S(1)} %pad_maximum_fusion.2), channel_id=1, source_target_pairs={{0,15},{1,0},{2,1},{3,2},{4,3},{5,4},{6,5},{7,6},{8,7},{9,8},{10,9... | collective-permute-start | bytes 921608 | tf_op jit(solution)/shard_map/ppermute | solution.py:187
  7.2 10.8 %copy-start.2 = (f32[4,4,32,256]{3,2,1,0:T(8,128)S(1)}, f32[4,4,32,256]{3,2,1,0:T(8,128)}, u32[]{:S(2)}) copy-start(f32[4,4,32,256]{3,2,1,0:T(8,128)} %param.5) | copy-start | bytes 1572868
  20.0 13.9 %collective-permute-start.3 = (f32[12,1656]{1,0:T(8,128)S(1)}, f32[12,1656]{1,0:T(8,128)S(1)}, u32[]{:S(2)}, u32[]{:S(2)}) collective-permute-start(f32[12,1656]{1,0:T(8,128)S(1)} %pad_maximum_fusion.5), channel_id=1, source_target_pairs={{0,240},{16,0},{32,16},{48,32},{64,48},{80,64},{96,80},{112,96},{1... | collective-permute-start | bytes 238472 | tf_op jit(solution)/shard_map/ppermute | solution.py:210
  26.5 6.5 %collective-permute-start.2 = (f32[12,1656]{1,0:T(8,128)S(1)}, f32[12,1656]{1,0:T(8,128)S(1)}, u32[]{:S(2)}, u32[]{:S(2)}) collective-permute-start(f32[12,1656]{1,0:T(8,128)S(1)} %pad_maximum_fusion.4), channel_id=1, source_target_pairs={{0,16},{16,32},{32,48},{48,64},{64,80},{80,96},{96,112},{112,128},... | collective-permute-start | bytes 238472 | tf_op jit(solution)/shard_map/ppermute | solution.py:209
  36.9 1.1 %copy-start = (f32[17,56,280]{2,1,0:T(8,128)}, f32[17,56,280]{2,1,0:T(8,128)S(1)}, u32[]{:S(2)}) copy-start(f32[17,56,280]{2,1,0:T(8,128)S(1)} %maximum_multiply_fusion) | copy-start | bytes 3198724
  39.8 1.8 %slice-start = ((f32[17,56,280]{2,1,0:T(8,128)}), f32[16,56,280]{2,1,0:T(8,128)S(1)}, s32[]{:S(2)}) async-start(f32[17,56,280]{2,1,0:T(8,128)} %copy-done), calls=%async_computation | async-start | bytes 2752512 | tf_op jit(solution)/shard_map/slice | solution.py:250

commit v3 on v1

--- a/solution.py
+++ b/solution.py
@@ -145,12 +145,53 @@
             store(f, k, acc[f])
 
 
-def two_step_kernel(margin, rows, cols, x0, lam, depth_ref, cor_ref, final_ref, grad_ref, x1, mu, g_ref):
+def assemble(dst, own, south, north, east, west, lane_pos, rowmask):
+    rows, cols = own.shape
+    depth = south.shape[0]
+    frame_rows = dst.shape[0]
+    dst[...] = jnp.zeros(dst.shape, jnp.float32)
+    dst[0:rows, 0:cols] = own
+    dst[rows : rows + depth, 0:cols] = south
+    dst[frame_rows - depth : frame_rows, 0:cols] = north
+    lane = lax.broadcasted_iota(jnp.int32, (frame_rows, 128), 1)
+    from_east = shifted(east, lane_pos, 1)[:, 0:128]
+    from_west = shifted(west, lane_pos - 116, 1)[:, 0:128]
+    dst[:, cols : cols + 128] = jnp.where(lane < 12, from_east, jnp.where(lane >= 116, from_west, 0.0))
+    dst[...] = dst[...] * rowmask
+
+
+def two_step_kernel(
+    margin, reach, own_x, own_c, own_d, north, south, west, east, rowmask_ref, cor_ref,
+    final_ref, grad_ref, x0, lam, x1, mu, g_ref, depth_ref,
+):
+    fields, level_count, rows, cols = own_x.shape
+    planes = fields * level_count
+    frame_rows = x0.shape[2]
+    rowmask = jnp.broadcast_to(rowmask_ref[...], (frame_rows, x0.shape[3]))
+    cor = jnp.broadcast_to(cor_ref[...], (frame_rows, x0.shape[3]))
+    east_msg = east[...]
+    west_msg = west[...]
+    for f in range(fields):
+        for k in range(level_count):
+            p = f * level_count + k
+            assemble(
+                x0.at[f, k], own_x[f, k], south[margin * p : margin * (p + 1), :],
+                north[margin * p : margin * (p + 1), :], east_msg, west_msg, 12 * p, rowmask,
+            )
+    assemble(
+        depth_ref, own_d[...], south[margin * planes : margin * (planes + 1), :],
+        north[margin * planes : margin * (planes + 1), :], east_msg, west_msg, 12 * planes, rowmask,
+    )
+    base = margin * (planes + 1)
+    for f in range(fields):
+        for k in range(level_count):
+            p = f * level_count + k
+            assemble(
+                lam.at[f, k], own_c[f, k], south[base + reach * p : base + reach * (p + 1), :],
+                north[base + reach * p : base + reach * (p + 1), :], east_msg, west_msg,
+                12 * (planes + 1 + p), rowmask,
+            )
     depth = depth_ref[...]
-    cor = cor_ref[...]
-
-    def crop(value):
-        return shifted(shifted(value, margin, 0), margin, 1)[:rows, :cols]
 
     def keep(ref):
         def put(f, k, value):
@@ -159,7 +200,7 @@
 
     def keep_cropped(ref):
         def put(f, k, value):
-            ref[f, k] = crop(value)
+            ref[f, k] = value[:rows, :cols]
         return put
 
     forward(x0, keep(x1), depth, cor)
@@ -168,22 +209,8 @@
     backward(x0, mu, keep_cropped(grad_ref), g_ref, depth, cor)
 
 
-def halo(block, sides, width):
-    for axis, dim in sides:
-        count = lax.axis_size(axis)
-        forward_pairs = [(i, (i + 1) % count) for i in range(count)]
-        backward_pairs = [(target, source) for source, target in forward_pairs]
-        low = lax.ppermute(
-            lax.slice_in_dim(block, block.shape[dim] - width, None, axis=dim), axis, forward_pairs
-        )
-        high = lax.ppermute(lax.slice_in_dim(block, 0, width, axis=dim), axis, backward_pairs)
-        block = jnp.concatenate([low, block, high], axis=dim)
-    return block
-
-
-def inside_rows(lat_start, rim_depth, row_count, lat_total):
-    global_row = lat_start - rim_depth + jnp.arange(row_count + 2 * rim_depth, dtype=jnp.int32)
-    return ((global_row >= 0) & (global_row < lat_total))[:, None]
+def ring(count, step):
+    return [(i, (i + step) % count) for i in range(count)]
 
 
 def shards(state, cotangent, seamask, levels):
@@ -193,44 +220,65 @@
     margin = 12
     reach = 6
     planes = fields * level_count
-    stacked = jnp.concatenate(
-        [
-            state.reshape(planes, row_count, col_count),
-            (seamask * levels).astype(jnp.float32)[None],
-        ],
-        axis=0,
-    )
-    wide = halo(stacked, (("lon", 2), ("lat", 1)), margin)
-    cot_wide = halo(
-        cotangent.reshape(planes, row_count, col_count), (("lon", 2), ("lat", 1)), reach
-    )
-    wide = wide * inside_rows(lat_start, margin, row_count, lat_total).astype(jnp.float32)
-    cot_wide = cot_wide * inside_rows(lat_start, reach, row_count, lat_total).astype(jnp.float32)
+    depth = (seamask * levels).astype(jnp.float32)
+    stacked = jnp.concatenate([state.reshape(planes, row_count, col_count), depth[None]], axis=0)
+    cot = cotangent.reshape(planes, row_count, col_count)
+
+    def lat_message(take_last):
+        a = stacked[:, row_count - margin :, :] if take_last else stacked[:, :margin, :]
+        c = cot[:, row_count - reach :, :] if take_last else cot[:, :reach, :]
+        return jnp.concatenate([a.reshape(-1, col_count), c.reshape(-1, col_count)], axis=0)
+
+    lat_count = lax.axis_size("lat")
+    north = lax.ppermute(lat_message(True), "lat", ring(lat_count, 1))
+    south = lax.ppermute(lat_message(False), "lat", ring(lat_count, -1))
+    split = (planes + 1) * margin
     frame_rows = row_count + 2 * margin
     frame_cols = -(-(col_count + 2 * margin) // 128) * 128
-    extra = frame_cols - (col_count + 2 * margin)
-    cut = margin - reach
-    x0 = jnp.pad(wide[:planes], ((0, 0), (0, 0), (0, extra))).reshape(
-        fields, level_count, frame_rows, frame_cols
-    )
-    depth = jnp.pad(wide[planes], ((0, 0), (0, extra)))
-    lam = jnp.pad(cot_wide, ((0, 0), (cut, cut), (cut, cut + extra))).reshape(
-        fields, level_count, frame_rows, frame_cols
-    )
-    row_index = (lat_start - margin + jnp.arange(frame_rows, dtype=jnp.int32)).astype(jnp.float32)
-    latitude = jnp.pi * ((row_index + 0.5) / lat_total - 0.5)
-    cor = jnp.broadcast_to((rotation * jnp.sin(latitude))[:, None], (frame_rows, frame_cols))
+    msg_cols = -(-(12 * (2 * planes + 1)) // 128) * 128
+
+    def lon_message(take_last):
+        lo, hi = (col_count - 12, col_count) if take_last else (0, 12)
+        a = jnp.concatenate(
+            [
+                stacked[:, :, lo:hi],
+                south[:split, lo:hi].reshape(planes + 1, margin, 12),
+                north[:split, lo:hi].reshape(planes + 1, margin, 12),
+            ],
+            axis=1,
+        )
+        c = jnp.concatenate(
+            [
+                cot[:, :, lo:hi],
+                south[split:, lo:hi].reshape(planes, reach, 12),
+                jnp.zeros((planes, 2 * (margin - reach), 12), jnp.float32),
+                north[split:, lo:hi].reshape(planes, reach, 12),
+            ],
+            axis=1,
+        )
+        m = jnp.transpose(jnp.concatenate([a, c], axis=0), (1, 0, 2)).reshape(frame_rows, -1)
+        return jnp.pad(m, ((0, 0), (0, msg_cols - m.shape[1])))
+
+    lon_count = lax.axis_size("lon")
+    west = lax.ppermute(lon_message(True), "lon", ring(lon_count, 1))
+    east = lax.ppermute(lon_message(False), "lon", ring(lon_count, -1))
+    frame_index = jnp.arange(frame_rows, dtype=jnp.int32)
+    global_row = lat_start + jnp.where(frame_index < row_count + margin, frame_index, frame_index - frame_rows)
+    rowmask = ((global_row >= 0) & (global_row < lat_total)).astype(jnp.float32)[:, None]
+    latitude = jnp.pi * ((global_row.astype(jnp.float32) + 0.5) / lat_total - 0.5)
+    cor = (rotation * jnp.sin(latitude))[:, None]
     frame = (fields, level_count, frame_rows, frame_cols)
     out_block = jax.ShapeDtypeStruct((fields, level_count, row_count, col_count), jnp.float32)
     vmem = pl.BlockSpec(memory_space=pltpu.VMEM)
     final_state, adjoint_state = pl.pallas_call(
-        functools.partial(two_step_kernel, margin, row_count, col_count),
+        functools.partial(two_step_kernel, margin, reach),
         out_shape=(out_block, out_block),
-        in_specs=[vmem, vmem, vmem, vmem],
+        in_specs=[vmem] * 9,
         out_specs=(vmem, vmem),
-        scratch_shapes=[pltpu.VMEM(frame, jnp.float32) for _ in range(3)],
+        scratch_shapes=[pltpu.VMEM(frame, jnp.float32) for _ in range(5)]
+        + [pltpu.VMEM((frame_rows, frame_cols), jnp.float32)],
         interpret=INTERPRET,
-    )(x0, lam, depth, cor)
+    )(state, cotangent, depth, north, south, west, east, rowmask, cor)
     return (final_state, adjoint_state)
 
 

time: 71.4 us -> 59.1 us (0.83)
  waiting for transfers between devices: 18.6 us -> 7.66 us
  local copies, waits for them, and re-layouts: 4.38 us -> 15.1 us
  starting transfers between devices: 18.2 us -> 10.1 us
  Pallas kernels: 25.8 us -> 21.7 us
    ppermute x8 -> x4, waiting for transfers between devices: 18.6 us -> 7.66 us  [the longest x1 6.27 us: shards(): south = lax.ppermute(lat_message(False), 'lat', ring(lat_count, -1))]
    ppermute x8 -> x4, starting transfers between devices: 18.2 us -> 10.1 us  [the longest x1 4.24 us: shards(): east = lax.ppermute(lon_message(False), 'lon', ring(lon_count, -1))]
    reshape x0 -> x18, local copies, waits for them, and re-layouts: none -> 6.35 us  [the longest x4 5.53 us: lat_message(): c.reshape(-1, col_count)]
    pallas_call x1, Pallas kernels: 25.8 us -> 21.7 us  [shards(): pl.pallas_call(functools.partial(two_step_kernel, margin, reach), out_sha...]
    slice x3 -> x10, local copies, waits for them, and re-layouts: 0.28 us -> 3.89 us  [the longest x1 2.62 us: lat_message(): c = cot[:, row_count - reach:, :] if take_last else cot[:, :reach, :]]
    unnamed x4 -> x21, local copies, waits for them, and re-layouts: 0.01 us -> 3.51 us
    pad x3 -> x2, local copies, waits for them, and re-layouts: 3.37 us -> 0.02 us  [lon_message(): return jnp.pad(m, ((0, 0), (0, msg_cols - m.shape[1])))]
    concatenate x0 -> x3, local copies, waits for them, and re-layouts: none -> 1.21 us  [the longest x1 0.68 us: lon_message(): jnp.concatenate([cot[:, :, lo:hi], south[split:, lo:hi].reshape(planes, r...]
  transfers between devices with their start and end apart: 8 -> 4, of which waited for: 4 -> 2; matrix products, arithmetic and copies ran while one was open for 4% -> 11% of each run, Pallas kernels for 0% -> 0%
where the time goes in v3:
time: 59.1 us; the launch traced here: 58.9 us
  Pallas kernels  21.7 us (37%)
  local copies, waits for them, and re-layouts  15.1 us (26%)
  starting transfers between devices  10.1 us (17%)
  waiting for transfers between devices  7.66 us (13%)
  other arithmetic  3.34 us (6%)
  between operations  0.98 us (2%)
    pallas_call x1, Pallas kernels, shards(): pl.pallas_call(functools.partial(two_step_kernel, margin, reach), out_sha...  21.7 us
    ppermute x1, waiting for transfers between devices, shards(): south = lax.ppermute(lat_message(False), 'lat', ring(lat_count, -1))  6.27 us
    reshape x4, local copies, waits for them, and re-layouts, lat_message(): c.reshape(-1, col_count)  5.53 us
    ppermute x1, starting transfers between devices, shards(): east = lax.ppermute(lon_message(False), 'lon', ring(lon_count, -1))  4.24 us
    ppermute x1, starting transfers between devices, shards(): north = lax.ppermute(lat_message(True), 'lat', ring(lat_count, 1))  4.12 us
    unnamed x21, local copies, waits for them, and re-layouts  3.51 us
    slice x1, local copies, waits for them, and re-layouts, lat_message(): c = cot[:, row_count - reach:, :] if take_last else cot[:, :reach, :]  2.62 us
    ppermute x1, starting transfers between devices, shards(): west = lax.ppermute(lon_message(True), 'lon', ring(lon_count, 1))  1.71 us
  transfers between devices with their start and end apart: 4, of which 2 were waited for; matrix products, arithmetic and copies ran while one was open for 11% of the time, Pallas kernels for 0%

profile of v3, /device:TPU:1, one launch (start us, length us, event | category | flops | bytes accessed | tf_op | source)
XLA Modules:
  0.0 58.9 jit_solution(16589302822965476333)
XLA Ops:
  0.6 2.2 %copy.108 = f32[4,4,32,256]{2,1,0,3:T(4,128)S(1)} copy(f32[4,4,32,256]{3,2,1,0:T(8,128)} %own_c.1) | data formatting | bytes 1048576 | tf_op args[1]
  2.8 2.6 %fusion.11 = (f32[16,6,256]{1,0,2:T(8,128)}, f32[16,6,256]{1,0,2:T(8,128)}) fusion(f32[16,32,256]{1,0,2:T(8,128)S(1)} %bitcast.23), kind=kLoop, calls=%fused_computation.26 | loop fusion | bytes 393216 | tf_op jit(solution)/shard_map/slice | solution.py:229
  5.5 2.7 %reshape.124 = f32[96,256]{0,1:T(8,128)S(1)} reshape(f32[16,6,256]{1,0,2:T(8,128)} %get-tuple-element.5) | data formatting | bytes 196608 | tf_op jit(solution)/shard_map/reshape | solution.py:230
  8.2 0.1 copy.130
  8.4 0.7 %pad_maximum_fusion.2 = f32[300,256]{1,0:T(8,128)} fusion(f32[96,256]{1,0:T(8,128)S(1)} %copy.130, f32[204,256]{1,0:T(8,128)S(1)} %reshape.109), kind=kLoop, calls=%fused_computation.10 | loop fusion | flops 76800 | bytes 614400 | tf_op jit(solution)/shard_map/concatenate | solution.py:230
  9.2 4.1 %collective-permute-start = (f32[300,256]{1,0:T(8,128)}, f32[300,256]{1,0:T(8,128)S(1)}, u32[]{:S(2)}, u32[]{:S(2)}) collective-permute-start(f32[300,256]{1,0:T(8,128)} %pad_maximum_fusion.2), channel_id=1, source_target_pairs={{0,1},{1,2},{2,3},{3,4},{4,5},{5,6},{6,7},{7,8},{8,9},{9,10},{10,1... | collective-permute-start | bytes 921608 | tf_op jit(solution)/shard_map/ppermute | solution.py:233
  13.3 2.6 %reshape.125 = f32[96,256]{0,1:T(8,128)S(1)} reshape(f32[16,6,256]{1,0,2:T(8,128)} %get-tuple-element.4) | data formatting | bytes 196608 | tf_op jit(solution)/shard_map/reshape | solution.py:230
  15.9 0.1 copy.131
  16.1 0.7 %pad_maximum_fusion.3 = f32[300,256]{1,0:T(8,128)} fusion(f32[96,256]{1,0:T(8,128)S(1)} %copy.131, f32[204,256]{1,0:T(8,128)S(1)} %reshape.112), kind=kLoop, calls=%fused_computation.11 | loop fusion | flops 76800 | bytes 614400 | tf_op jit(solution)/shard_map/concatenate | solution.py:230
  16.8 0.7 %pad.20.clone = f32[33,56]{1,0:T(8,128)} pad(f32[16,12]{1,0:T(8,128)S(1)} %broadcast.99, f32[]{:T(128)} %constant.34), padding=17_0x38_6 | pad | bytes 8164 | tf_op jit(solution)/shard_map/concatenate | solution.py:250
  17.5 0.6 %fusion.10 = (f32[16,32,12]{1,0,2:T(8,128)S(1)}, f32[16,32,12]{1,0,2:T(8,128)}) fusion(f32[16,32,256]{1,0,2:T(8,128)S(1)} %bitcast.24), kind=kLoop, calls=%fused_computation.25 | loop fusion | bytes 98304 | tf_op jit(solution)/shard_map/slice | solution.py:252
  18.1 0.1 fusion.2
  18.4 0.1 reshape.122
  18.6 6.3 %collective-permute-done.1.south = f32[300,256]{1,0:T(8,128)S(1)} collective-permute-done((f32[300,256]{1,0:T(8,128)}, f32[300,256]{1,0:T(8,128)S(1)}, u32[]{:S(2)}, u32[]{:S(2)}) %collective-permute-start.1) | collective-permute-done | bytes 307232 | tf_op jit(solution)/shard_map/ppermute | solution.py:234
  25.0 0.1 reshape.121
  25.1 0.1 fusion.13
  25.2 0.1 fusion.12
  25.4 0.3 copy.126
  25.8 0.1 reshape.117
  26.0 0.1 reshape.116
  26.2 0.3 copy.117
  26.5 0.2 maximum_bitcast_fusion.1
  26.8 0.1 copy.119
  27.0 1.7 %collective-permute-start.2 = (f32[56,512]{1,0:T(8,128)S(1)}, f32[56,512]{1,0:T(8,128)S(1)}, u32[]{:S(2)}, u32[]{:S(2)}) collective-permute-start(f32[56,512]{1,0:T(8,128)S(1)} %pad.7), channel_id=1, source_target_pairs={{0,16},{16,32},{32,48},{48,64},{64,80},{80,96},{96,112},{112,128},... | collective-permute-start | bytes 344072 | tf_op jit(solution)/shard_map/ppermute | solution.py:263
  28.7 0.1 copy.128
  28.9 4.2 %collective-permute-start.3 = (f32[56,512]{1,0:T(8,128)S(1)}, f32[56,512]{1,0:T(8,128)S(1)}, u32[]{:S(2)}, u32[]{:S(2)}) collective-permute-start(f32[56,512]{1,0:T(8,128)S(1)} %pad.8), channel_id=1, source_target_pairs={{0,240},{16,0},{32,16},{48,32},{64,48},{80,64},{96,80},{112,96},{1... | collective-permute-start | bytes 344072 | tf_op jit(solution)/shard_map/ppermute | solution.py:264
  33.1 0.6 %fusion.9.rowmask_ref = f32[56,1]{1,0:T(8,128)} fusion(s32[]{:T(128)S(6)} %mul.33), kind=kLoop, calls=%fused_computation.24 | loop fusion | flops 448 | bytes 228 | tf_op jit(solution)/shard_map/convert_element_type | solution.py:267
  33.7 0.7 %sine_multiply_fusion.cor_ref = f32[56,1]{1,0:T(8,128)} fusion(s32[]{:T(128)S(6)} %mul.33), kind=kLoop, calls=%fused_computation.20 | loop fusion | flops 560 | bytes 228 | tf_op jit(solution)/shard_map/mul | solution.py:269
  34.5 1.4 %collective-permute-done.2.west = f32[56,512]{1,0:T(8,128)S(1)} collective-permute-done((f32[56,512]{1,0:T(8,128)S(1)}, f32[56,512]{1,0:T(8,128)S(1)}, u32[]{:S(2)}, u32[]{:S(2)}) %collective-permute-start.2) | collective-permute-done | bytes 114720 | tf_op jit(solution)/shard_map/ppermute | solution.py:263
  35.8 0.6 %copy-done.5 = f32[56,512]{1,0:T(8,128)} copy-done((f32[56,512]{1,0:T(8,128)}, f32[56,512]{1,0:T(8,128)S(1)}, u32[]{:S(2)}) %copy-start.5) | copy-done | bytes 114712
  36.5 0.6 %copy-done.6 = f32[56,512]{1,0:T(8,128)} copy-done((f32[56,512]{1,0:T(8,128)}, f32[56,512]{1,0:T(8,128)S(1)}, u32[]{:S(2)}) %copy-start.6) | copy-done | bytes 114712
  37.1 21.7 %shard_map.59 = (f32[4,4,32,256]{3,2,1,0:T(8,128)}, f32[4,4,32,256]{3,2,1,0:T(8,128)}) custom-call(f32[4,4,32,256]{3,2,1,0:T(8,128)} %own_x.1, f32[4,4,32,256]{3,2,1,0:T(8,128)} %own_c.1, f32[32,256]{1,0:T(8,128)} %copy-done.3, f32[300,256]{1,0:T(8,128)} %copy-done.1, f32[300,256]{1,0:T(8,128)} %copy-done.2, f32[56,512]{1,0:T(8,128)} %copy-done.5, ...), custom_call_target="tpu_custom_call" | custom-call | tf_op jit(solution)/shard_map/pallas_call | solution.py:273
  (44 shorter events, 0.9 us)
Async XLA Ops:
  5.5 2.8 %copy-start.8 = (s32[32,256]{1,0:T(8,128)S(1)}, s32[32,256]{1,0:T(8,128)}, u32[]{:S(2)}) copy-start(s32[32,256]{1,0:T(8,128)} %param.6) | copy-start | bytes 98308
  5.5 2.8 %copy-start.9 = (s32[32,256]{1,0:T(8,128)S(1)}, s32[32,256]{1,0:T(8,128)}, u32[]{:S(2)}) copy-start(s32[32,256]{1,0:T(8,128)} %param.7) | copy-start | bytes 98308
  5.5 2.9 %copy-start = (f32[4,4,32,256]{3,2,1,0:T(8,128)S(1)}, f32[4,4,32,256]{3,2,1,0:T(8,128)}, u32[]{:S(2)}) copy-start(f32[4,4,32,256]{3,2,1,0:T(8,128)} %own_x.1) | copy-start | bytes 1572868
  8.3 17.0 %copy-start.3 = (f32[32,256]{1,0:T(8,128)}, f32[32,256]{1,0:T(8,128)S(1)}, u32[]{:S(2)}) copy-start(f32[32,256]{1,0:T(8,128)S(1)} %multiply_convert_fusion.own_d) | copy-start | bytes 98308
  9.2 9.1 %collective-permute-start = (f32[300,256]{1,0:T(8,128)}, f32[300,256]{1,0:T(8,128)S(1)}, u32[]{:S(2)}, u32[]{:S(2)}) collective-permute-start(f32[300,256]{1,0:T(8,128)} %pad_maximum_fusion.2), channel_id=1, source_target_pairs={{0,1},{1,2},{2,3},{3,4},{4,5},{5,6},{6,7},{7,8},{8,9},{9,10},{10,1... | collective-permute-start | bytes 921608 | tf_op jit(solution)/shard_map/ppermute | solution.py:233
  16.8 8.0 %collective-permute-start.1 = (f32[300,256]{1,0:T(8,128)}, f32[300,256]{1,0:T(8,128)S(1)}, u32[]{:S(2)}, u32[]{:S(2)}) collective-permute-start(f32[300,256]{1,0:T(8,128)} %pad_maximum_fusion.3), channel_id=1, source_target_pairs={{0,15},{1,0},{2,1},{3,2},{4,3},{5,4},{6,5},{7,6},{8,7},{9,8},{10,9... | collective-permute-start | bytes 921608 | tf_op jit(solution)/shard_map/ppermute | solution.py:234
  18.3 7.6 %copy-start.1 = (f32[300,256]{1,0:T(8,128)}, f32[300,256]{1,0:T(8,128)S(1)}, u32[]{:S(2)}) copy-start(f32[300,256]{1,0:T(8,128)S(1)} %collective-permute-done.north) | copy-start | bytes 921604
  24.8 1.3 %copy-start.2 = (f32[300,256]{1,0:T(8,128)}, f32[300,256]{1,0:T(8,128)S(1)}, u32[]{:S(2)}) copy-start(f32[300,256]{1,0:T(8,128)S(1)} %collective-permute-done.1.south) | copy-start | bytes 921604
  25.4 1.1 %copy-start.4 = (f32[16,32,12]{1,0,2:T(8,128)S(1)}, f32[16,32,12]{1,0,2:T(8,128)}, u32[]{:S(2)}) copy-start(f32[16,32,12]{1,0,2:T(8,128)} %get-tuple-element.3) | copy-start | bytes 73732
  25.4 1.1 %copy-start.7 = (f32[33,56]{1,0:T(8,128)S(1)}, f32[33,56]{1,0:T(8,128)}, u32[]{:S(2)}) copy-start(f32[33,56]{1,0:T(8,128)} %pad.20.clone) | copy-start | bytes 22180
  27.0 8.9 %collective-permute-start.2 = (f32[56,512]{1,0:T(8,128)S(1)}, f32[56,512]{1,0:T(8,128)S(1)}, u32[]{:S(2)}, u32[]{:S(2)}) collective-permute-start(f32[56,512]{1,0:T(8,128)S(1)} %pad.7), channel_id=1, source_target_pairs={{0,16},{16,32},{32,48},{48,64},{64,80},{80,96},{96,112},{112,128},... | collective-permute-start | bytes 344072 | tf_op jit(solution)/shard_map/ppermute | solution.py:263
  28.9 7.0 %collective-permute-start.3 = (f32[56,512]{1,0:T(8,128)S(1)}, f32[56,512]{1,0:T(8,128)S(1)}, u32[]{:S(2)}, u32[]{:S(2)}) collective-permute-start(f32[56,512]{1,0:T(8,128)S(1)} %pad.8), channel_id=1, source_target_pairs={{0,240},{16,0},{32,16},{48,32},{64,48},{80,64},{96,80},{112,96},{1... | collective-permute-start | bytes 344072 | tf_op jit(solution)/shard_map/ppermute | solution.py:264
  35.8 0.7 %copy-start.5 = (f32[56,512]{1,0:T(8,128)}, f32[56,512]{1,0:T(8,128)S(1)}, u32[]{:S(2)}) copy-start(f32[56,512]{1,0:T(8,128)S(1)} %collective-permute-done.2.west) | copy-start | bytes 344068
  36.5 0.6 %copy-start.6 = (f32[56,512]{1,0:T(8,128)}, f32[56,512]{1,0:T(8,128)S(1)}, u32[]{:S(2)}) copy-start(f32[56,512]{1,0:T(8,128)S(1)} %collective-permute-done.3.east) | copy-start | bytes 344068

commit v4 on v3

--- a/solution.py
+++ b/solution.py
@@ -145,7 +145,11 @@
             store(f, k, acc[f])
 
 
-def assemble(dst, own, south, north, east, west, lane_pos, rowmask):
+def strip_place(p):
+    return p // 10, 12 * (p % 10)
+
+
+def assemble(dst, own, south, north, east, west, p, rowmask):
     rows, cols = own.shape
     depth = south.shape[0]
     frame_rows = dst.shape[0]
@@ -154,8 +158,9 @@
     dst[rows : rows + depth, 0:cols] = south
     dst[frame_rows - depth : frame_rows, 0:cols] = north
     lane = lax.broadcasted_iota(jnp.int32, (frame_rows, 128), 1)
-    from_east = shifted(east, lane_pos, 1)[:, 0:128]
-    from_west = shifted(west, lane_pos - 116, 1)[:, 0:128]
+    block, offset = strip_place(p)
+    from_east = shifted(east[:, 128 * block : 128 * (block + 1)], offset, 1)
+    from_west = shifted(west[:, 128 * block : 128 * (block + 1)], offset - 116, 1)
     dst[:, cols : cols + 128] = jnp.where(lane < 12, from_east, jnp.where(lane >= 116, from_west, 0.0))
     dst[...] = dst[...] * rowmask
 
@@ -176,11 +181,11 @@
             p = f * level_count + k
             assemble(
                 x0.at[f, k], own_x[f, k], south[margin * p : margin * (p + 1), :],
-                north[margin * p : margin * (p + 1), :], east_msg, west_msg, 12 * p, rowmask,
+                north[margin * p : margin * (p + 1), :], east_msg, west_msg, p, rowmask,
             )
     assemble(
         depth_ref, own_d[...], south[margin * planes : margin * (planes + 1), :],
-        north[margin * planes : margin * (planes + 1), :], east_msg, west_msg, 12 * planes, rowmask,
+        north[margin * planes : margin * (planes + 1), :], east_msg, west_msg, planes, rowmask,
     )
     base = margin * (planes + 1)
     for f in range(fields):
@@ -189,7 +194,7 @@
             assemble(
                 lam.at[f, k], own_c[f, k], south[base + reach * p : base + reach * (p + 1), :],
                 north[base + reach * p : base + reach * (p + 1), :], east_msg, west_msg,
-                12 * (planes + 1 + p), rowmask,
+                planes + 1 + p, rowmask,
             )
     depth = depth_ref[...]
 
@@ -207,6 +212,66 @@
     forward(x1, keep_cropped(final_ref), depth, cor)
     backward(x1, lam, keep(mu), g_ref, depth, cor)
     backward(x0, mu, keep_cropped(grad_ref), g_ref, depth, cor)
+
+
+def lat_pack_kernel(margin, reach, own_x, own_c, own_d, north_msg, south_msg):
+    fields, level_count, rows, cols = own_x.shape
+    planes = fields * level_count
+    for f in range(fields):
+        for k in range(level_count):
+            p = f * level_count + k
+            north_msg[margin * p : margin * (p + 1), :] = own_x[f, k, rows - margin : rows, :]
+            south_msg[margin * p : margin * (p + 1), :] = own_x[f, k, 0:margin, :]
+    north_msg[margin * planes : margin * (planes + 1), :] = own_d[rows - margin : rows, :]
+    south_msg[margin * planes : margin * (planes + 1), :] = own_d[0:margin, :]
+    base = margin * (planes + 1)
+    for f in range(fields):
+        for k in range(level_count):
+            p = f * level_count + k
+            north_msg[base + reach * p : base + reach * (p + 1), :] = own_c[f, k, rows - reach : rows, :]
+            south_msg[base + reach * p : base + reach * (p + 1), :] = own_c[f, k, 0:reach, :]
+
+
+def lon_pack_kernel(margin, reach, own_x, own_c, own_d, north, south, west_msg, east_msg, ext):
+    fields, level_count, rows, cols = own_x.shape
+    planes = fields * level_count
+    frame_rows = ext.shape[0]
+    lane = lax.broadcasted_iota(jnp.int32, (frame_rows, 128), 1)
+    west_acc = [jnp.zeros((frame_rows, 128), jnp.float32) for _ in range(west_msg.shape[1] // 128)]
+    east_acc = [jnp.zeros((frame_rows, 128), jnp.float32) for _ in range(east_msg.shape[1] // 128)]
+
+    def add_plane(p, own, south_rows, north_rows):
+        depth = south_rows.shape[0]
+        ext[...] = jnp.zeros(ext.shape, jnp.float32)
+        ext[0:rows, :] = own
+        ext[rows : rows + depth, :] = south_rows
+        ext[frame_rows - depth : frame_rows, :] = north_rows
+        block, offset = strip_place(p)
+        keep = (lane >= offset) & (lane < offset + 12)
+        last = shifted(ext[:, cols - 128 : cols], 116 - offset, 1)
+        first = shifted(ext[:, 0:128], -offset, 1)
+        west_acc[block] = west_acc[block] + jnp.where(keep, last, 0.0)
+        east_acc[block] = east_acc[block] + jnp.where(keep, first, 0.0)
+
+    for f in range(fields):
+        for k in range(level_count):
+            p = f * level_count + k
+            add_plane(p, own_x[f, k], south[margin * p : margin * (p + 1), :], north[margin * p : margin * (p + 1), :])
+    add_plane(
+        planes, own_d[...], south[margin * planes : margin * (planes + 1), :],
+        north[margin * planes : margin * (planes + 1), :],
+    )
+    base = margin * (planes + 1)
+    for f in range(fields):
+        for k in range(level_count):
+            p = f * level_count + k
+            add_plane(
+                planes + 1 + p, own_c[f, k], south[base + reach * p : base + reach * (p + 1), :],
+                north[base + reach * p : base + reach * (p + 1), :],
+            )
+    for block in range(len(west_acc)):
+        west_msg[:, 128 * block : 128 * (block + 1)] = west_acc[block]
+        east_msg[:, 128 * block : 128 * (block + 1)] = east_acc[block]
 
 
 def ring(count, step):
@@ -221,47 +286,34 @@
     reach = 6
     planes = fields * level_count
     depth = (seamask * levels).astype(jnp.float32)
-    stacked = jnp.concatenate([state.reshape(planes, row_count, col_count), depth[None]], axis=0)
-    cot = cotangent.reshape(planes, row_count, col_count)
-
-    def lat_message(take_last):
-        a = stacked[:, row_count - margin :, :] if take_last else stacked[:, :margin, :]
-        c = cot[:, row_count - reach :, :] if take_last else cot[:, :reach, :]
-        return jnp.concatenate([a.reshape(-1, col_count), c.reshape(-1, col_count)], axis=0)
-
+    vmem = pl.BlockSpec(memory_space=pltpu.VMEM)
+    msg_rows = (planes + 1) * margin + planes * reach
+    lat_msg = jax.ShapeDtypeStruct((msg_rows, col_count), jnp.float32)
+    north_out, south_out = pl.pallas_call(
+        functools.partial(lat_pack_kernel, margin, reach),
+        out_shape=(lat_msg, lat_msg),
+        in_specs=[vmem] * 3,
+        out_specs=(vmem, vmem),
+        interpret=INTERPRET,
+    )(state, cotangent, depth)
     lat_count = lax.axis_size("lat")
-    north = lax.ppermute(lat_message(True), "lat", ring(lat_count, 1))
-    south = lax.ppermute(lat_message(False), "lat", ring(lat_count, -1))
-    split = (planes + 1) * margin
+    north = lax.ppermute(north_out, "lat", ring(lat_count, 1))
+    south = lax.ppermute(south_out, "lat", ring(lat_count, -1))
     frame_rows = row_count + 2 * margin
     frame_cols = -(-(col_count + 2 * margin) // 128) * 128
-    msg_cols = -(-(12 * (2 * planes + 1)) // 128) * 128
-
-    def lon_message(take_last):
-        lo, hi = (col_count - 12, col_count) if take_last else (0, 12)
-        a = jnp.concatenate(
-            [
-                stacked[:, :, lo:hi],
-                south[:split, lo:hi].reshape(planes + 1, margin, 12),
-                north[:split, lo:hi].reshape(planes + 1, margin, 12),
-            ],
-            axis=1,
-        )
-        c = jnp.concatenate(
-            [
-                cot[:, :, lo:hi],
-                south[split:, lo:hi].reshape(planes, reach, 12),
-                jnp.zeros((planes, 2 * (margin - reach), 12), jnp.float32),
-                north[split:, lo:hi].reshape(planes, reach, 12),
-            ],
-            axis=1,
-        )
-        m = jnp.transpose(jnp.concatenate([a, c], axis=0), (1, 0, 2)).reshape(frame_rows, -1)
-        return jnp.pad(m, ((0, 0), (0, msg_cols - m.shape[1])))
-
+    msg_cols = 128 * (-(-(2 * planes + 1) // 10))
+    lon_msg = jax.ShapeDtypeStruct((frame_rows, msg_cols), jnp.float32)
+    west_out, east_out = pl.pallas_call(
+        functools.partial(lon_pack_kernel, margin, reach),
+        out_shape=(lon_msg, lon_msg),
+        in_specs=[vmem] * 5,
+        out_specs=(vmem, vmem),
+        scratch_shapes=[pltpu.VMEM((frame_rows, col_count), jnp.float32)],
+        interpret=INTERPRET,
+    )(state, cotangent, depth, north, south)
     lon_count = lax.axis_size("lon")
-    west = lax.ppermute(lon_message(True), "lon", ring(lon_count, 1))
-    east = lax.ppermute(lon_message(False), "lon", ring(lon_count, -1))
+    west = lax.ppermute(west_out, "lon", ring(lon_count, 1))
+    east = lax.ppermute(east_out, "lon", ring(lon_count, -1))
     frame_index = jnp.arange(frame_rows, dtype=jnp.int32)
     global_row = lat_start + jnp.where(frame_index < row_count + margin, frame_index, frame_index - frame_rows)
     rowmask = ((global_row >= 0) & (global_row < lat_total)).astype(jnp.float32)[:, None]
@@ -269,7 +321,6 @@
     cor = (rotation * jnp.sin(latitude))[:, None]
     frame = (fields, level_count, frame_rows, frame_cols)
     out_block = jax.ShapeDtypeStruct((fields, level_count, row_count, col_count), jnp.float32)
-    vmem = pl.BlockSpec(memory_space=pltpu.VMEM)
     final_state, adjoint_state = pl.pallas_call(
         functools.partial(two_step_kernel, margin, reach),
         out_shape=(out_block, out_block),

time: 59.1 us -> 53.9 us (0.912)
  local copies, waits for them, and re-layouts: 15.1 us -> 2.02 us
  Pallas kernels: 21.7 us -> 26.2 us
  waiting for transfers between devices: 7.66 us -> 11.8 us
  other arithmetic: 3.34 us -> 2.72 us
    reshape x18 -> x0, local copies, waits for them, and re-layouts: 6.35 us -> none  [the longest x4 5.53 us: lat_message(): c.reshape(-1, col_count)]
    pallas_call x0 -> x2, Pallas kernels: none -> 4.74 us  [the longest x1 2.64 us: shards(): pl.pallas_call(functools.partial(lon_pack_kernel, margin, reach), out_sha...]
    ppermute x4, waiting for transfers between devices: 7.66 us -> 11.8 us  [the longest x1 5.2 us: shards(): south = lax.ppermute(south_out, 'lat', ring(lat_count, -1))]
    slice x10 -> x0, local copies, waits for them, and re-layouts: 3.89 us -> none  [the longest x1 2.62 us: lat_message(): c = cot[:, row_count - reach:, :] if take_last else cot[:, :reach, :]]
    concatenate x6 -> x0, other arithmetic: 1.77 us -> none  [the longest x2 1.48 us: lat_message(): jnp.concatenate([a.reshape(-1, col_count), c.reshape(-1, col_count)], axi...]
    unnamed x21 -> x8, local copies, waits for them, and re-layouts: 3.51 us -> 2.02 us
    convert_element_type x1, other arithmetic: 0.01 us -> 1.39 us  [shards(): depth = (seamask * levels).astype(jnp.float32)]
    concatenate x3 -> x0, local copies, waits for them, and re-layouts: 1.21 us -> none  [the longest x1 0.68 us: lon_message(): jnp.concatenate([cot[:, :, lo:hi], south[split:, lo:hi].reshape(planes, r...]
  transfers between devices with their start and end apart: 4 -> 4, of which waited for: 2 -> 3; matrix products, arithmetic and copies ran while one was open for 11% -> 2% of each run, Pallas kernels for 0% -> 0%
where the time goes in v4:
time: 53.9 us; the launch traced here: 53.7 us
  Pallas kernels  26.2 us (49%)
  waiting for transfers between devices  11.8 us (22%)
  starting transfers between devices  10.3 us (19%)
  other arithmetic  2.72 us (5%)
  local copies, waits for them, and re-layouts  2.02 us (4%)
  between operations  0.64 us (1%)
    pallas_call x1, Pallas kernels, shards(): pl.pallas_call(functools.partial(two_step_kernel, margin, reach), out_sha...  21.5 us
    ppermute x1, waiting for transfers between devices, shards(): south = lax.ppermute(south_out, 'lat', ring(lat_count, -1))  5.2 us
    ppermute x1, starting transfers between devices, shards(): east = lax.ppermute(east_out, 'lon', ring(lon_count, -1))  4.87 us
    ppermute x1, waiting for transfers between devices, shards(): north = lax.ppermute(north_out, 'lat', ring(lat_count, 1))  4.16 us
    ppermute x1, starting transfers between devices, shards(): north = lax.ppermute(north_out, 'lat', ring(lat_count, 1))  4.12 us
    pallas_call x1, Pallas kernels, shards(): pl.pallas_call(functools.partial(lon_pack_kernel, margin, reach), out_sha...  2.64 us
    ppermute x1, waiting for transfers between devices, shards(): west = lax.ppermute(west_out, 'lon', ring(lon_count, 1))  2.4 us
    pallas_call x1, Pallas kernels, shards(): pl.pallas_call(functools.partial(lat_pack_kernel, margin, reach), out_sha...  2.1 us
  transfers between devices with their start and end apart: 4, of which 3 were waited for; matrix products, arithmetic and copies ran while one was open for 2% of the time, Pallas kernels for 0%

profile of v4, /device:TPU:1, one launch (start us, length us, event | category | flops | bytes accessed | tf_op | source)
XLA Modules:
  0.0 53.7 jit_solution(5131476793555743416)
XLA Ops:
  0.6 1.4 %multiply_convert_fusion.own_d = f32[32,256]{1,0:T(8,128)} fusion(s32[32,256]{1,0:T(8,128)} %param.6, s32[32,256]{1,0:T(8,128)} %param.7), kind=kLoop, calls=%fused_computation.1 | loop fusion | flops 16384 | bytes 98304 | tf_op jit(solution)/shard_map/convert_element_type | solution.py:288
  2.0 2.1 %shard_map.59 = (f32[300,256]{1,0:T(8,128)}, f32[300,256]{1,0:T(8,128)}) custom-call(f32[4,4,32,256]{3,2,1,0:T(8,128)} %own_x.5, f32[4,4,32,256]{3,2,1,0:T(8,128)} %own_c.5, f32[32,256]{1,0:T(8,128)} %multiply_convert_fusion.own_d), custom_call_target="tpu_custom_call" | custom-call | tf_op jit(solution)/shard_map/pallas_call | solution.py:292
  4.1 4.1 %collective-permute-start = (f32[300,256]{1,0:T(8,128)}, f32[300,256]{1,0:T(8,128)S(1)}, u32[]{:S(2)}, u32[]{:S(2)}) collective-permute-start(f32[300,256]{1,0:T(8,128)} %get-tuple-element.6), channel_id=1, source_target_pairs={{0,1},{1,2},{2,3},{3,4},{4,5},{5,6},{6,7},{7,8},{8,9},{9,10},{10,1... | collective-permute-start | bytes 921608 | tf_op jit(solution)/shard_map/ppermute | solution.py:300
  8.2 0.0 collective-permute-start.1
  8.2 4.2 %collective-permute-done.north = f32[300,256]{1,0:T(8,128)S(1)} collective-permute-done((f32[300,256]{1,0:T(8,128)}, f32[300,256]{1,0:T(8,128)S(1)}, u32[]{:S(2)}, u32[]{:S(2)}) %collective-permute-start) | collective-permute-done | bytes 307232 | tf_op jit(solution)/shard_map/ppermute | solution.py:300
  12.4 0.0 copy-start
  12.4 5.2 %collective-permute-done.1.south = f32[300,256]{1,0:T(8,128)S(1)} collective-permute-done((f32[300,256]{1,0:T(8,128)}, f32[300,256]{1,0:T(8,128)S(1)}, u32[]{:S(2)}, u32[]{:S(2)}) %collective-permute-start.1) | collective-permute-done | bytes 307232 | tf_op jit(solution)/shard_map/ppermute | solution.py:301
  17.6 0.0 copy-done
  17.6 0.0 copy-start.1
  17.6 0.7 %copy-done.1 = f32[300,256]{1,0:T(8,128)} copy-done((f32[300,256]{1,0:T(8,128)}, f32[300,256]{1,0:T(8,128)S(1)}, u32[]{:S(2)}) %copy-start.1) | copy-done | bytes 307224
  18.3 2.6 %shard_map.60 = (f32[56,512]{1,0:T(8,128)}, f32[56,512]{1,0:T(8,128)}) custom-call(f32[4,4,32,256]{3,2,1,0:T(8,128)} %own_x.5, f32[4,4,32,256]{3,2,1,0:T(8,128)} %own_c.5, f32[32,256]{1,0:T(8,128)} %multiply_convert_fusion.own_d, f32[300,256]{1,0:T(8,128)} %copy-done, f32[300,256]{1,0:T(8,128)} %copy-done.1), custom_call_target="tpu_custom_call" | custom-call | tf_op jit(solution)/shard_map/pallas_call | solution.py:306
  21.0 1.3 %collective-permute-start.2 = (f32[56,512]{1,0:T(8,128)}, f32[56,512]{1,0:T(8,128)S(1)}, u32[]{:S(2)}, u32[]{:S(2)}) collective-permute-start(f32[56,512]{1,0:T(8,128)} %get-tuple-element.8), channel_id=1, source_target_pairs={{0,16},{16,32},{32,48},{48,64},{64,80},{80,96},{96,112},{112,128},... | collective-permute-start | bytes 344072 | tf_op jit(solution)/shard_map/ppermute | solution.py:315
  22.3 4.9 %collective-permute-start.3 = (f32[56,512]{1,0:T(8,128)}, f32[56,512]{1,0:T(8,128)S(1)}, u32[]{:S(2)}, u32[]{:S(2)}) collective-permute-start(f32[56,512]{1,0:T(8,128)} %get-tuple-element.9), channel_id=1, source_target_pairs={{0,240},{16,0},{32,16},{48,32},{64,48},{80,64},{96,80},{112,96},{1... | collective-permute-start | bytes 344072 | tf_op jit(solution)/shard_map/ppermute | solution.py:316
  27.2 0.7 %sine_multiply_fusion.cor_ref = f32[56,1]{1,0:T(8,128)} fusion(s32[]{:T(128)S(6)} %mul.33), kind=kLoop, calls=%fused_computation.3 | loop fusion | flops 560 | bytes 228 | tf_op jit(solution)/shard_map/mul | solution.py:321
  27.9 0.6 %fusion.4.rowmask_ref = f32[56,1]{1,0:T(8,128)} fusion(s32[]{:T(128)S(6)} %mul.33), kind=kLoop, calls=%fused_computation.7 | loop fusion | flops 448 | bytes 228 | tf_op jit(solution)/shard_map/convert_element_type | solution.py:319
  28.5 2.4 %collective-permute-done.2.west = f32[56,512]{1,0:T(8,128)S(1)} collective-permute-done((f32[56,512]{1,0:T(8,128)}, f32[56,512]{1,0:T(8,128)S(1)}, u32[]{:S(2)}, u32[]{:S(2)}) %collective-permute-start.2) | collective-permute-done | bytes 114720 | tf_op jit(solution)/shard_map/ppermute | solution.py:315
  30.9 0.0 copy-start.2
  30.9 0.0 collective-permute-done.3.east
  30.9 0.6 %copy-done.2 = f32[56,512]{1,0:T(8,128)} copy-done((f32[56,512]{1,0:T(8,128)}, f32[56,512]{1,0:T(8,128)S(1)}, u32[]{:S(2)}) %copy-start.2) | copy-done | bytes 114712
  31.6 0.0 copy-start.3
  31.6 0.6 %copy-done.3 = f32[56,512]{1,0:T(8,128)} copy-done((f32[56,512]{1,0:T(8,128)}, f32[56,512]{1,0:T(8,128)S(1)}, u32[]{:S(2)}) %copy-start.3) | copy-done | bytes 114712
  32.2 21.5 %shard_map.61 = (f32[4,4,32,256]{3,2,1,0:T(8,128)}, f32[4,4,32,256]{3,2,1,0:T(8,128)}) custom-call(f32[4,4,32,256]{3,2,1,0:T(8,128)} %own_x.5, f32[4,4,32,256]{3,2,1,0:T(8,128)} %own_c.5, f32[32,256]{1,0:T(8,128)} %multiply_convert_fusion.own_d, f32[300,256]{1,0:T(8,128)} %copy-done, f32[300,256]{1,0:T(8,128)} %copy-done.1, f32[56,512]{1,0:T(8,128)} %copy-done.2, ...), custom_call_target="tpu_custom_call" | custom-call | tf_op jit(solution)/shard_map/pallas_call | solution.py:324
Async XLA Ops:
  4.1 8.3 %collective-permute-start = (f32[300,256]{1,0:T(8,128)}, f32[300,256]{1,0:T(8,128)S(1)}, u32[]{:S(2)}, u32[]{:S(2)}) collective-permute-start(f32[300,256]{1,0:T(8,128)} %get-tuple-element.6), channel_id=1, source_target_pairs={{0,1},{1,2},{2,3},{3,4},{4,5},{5,6},{6,7},{7,8},{8,9},{9,10},{10,1... | collective-permute-start | bytes 921608 | tf_op jit(solution)/shard_map/ppermute | solution.py:300
  8.2 9.4 %collective-permute-start.1 = (f32[300,256]{1,0:T(8,128)}, f32[300,256]{1,0:T(8,128)S(1)}, u32[]{:S(2)}, u32[]{:S(2)}) collective-permute-start(f32[300,256]{1,0:T(8,128)} %get-tuple-element.7), channel_id=1, source_target_pairs={{0,15},{1,0},{2,1},{3,2},{4,3},{5,4},{6,5},{7,6},{8,7},{9,8},{10,9... | collective-permute-start | bytes 921608 | tf_op jit(solution)/shard_map/ppermute | solution.py:301
  12.4 5.2 %copy-start = (f32[300,256]{1,0:T(8,128)}, f32[300,256]{1,0:T(8,128)S(1)}, u32[]{:S(2)}) copy-start(f32[300,256]{1,0:T(8,128)S(1)} %collective-permute-done.north) | copy-start | bytes 921604
  17.6 0.7 %copy-start.1 = (f32[300,256]{1,0:T(8,128)}, f32[300,256]{1,0:T(8,128)S(1)}, u32[]{:S(2)}) copy-start(f32[300,256]{1,0:T(8,128)S(1)} %collective-permute-done.1.south) | copy-start | bytes 921604
  21.0 9.9 %collective-permute-start.2 = (f32[56,512]{1,0:T(8,128)}, f32[56,512]{1,0:T(8,128)S(1)}, u32[]{:S(2)}, u32[]{:S(2)}) collective-permute-start(f32[56,512]{1,0:T(8,128)} %get-tuple-element.8), channel_id=1, source_target_pairs={{0,16},{16,32},{32,48},{48,64},{64,80},{80,96},{96,112},{112,128},... | collective-permute-start | bytes 344072 | tf_op jit(solution)/shard_map/ppermute | solution.py:315
  22.3 8.6 %collective-permute-start.3 = (f32[56,512]{1,0:T(8,128)}, f32[56,512]{1,0:T(8,128)S(1)}, u32[]{:S(2)}, u32[]{:S(2)}) collective-permute-start(f32[56,512]{1,0:T(8,128)} %get-tuple-element.9), channel_id=1, source_target_pairs={{0,240},{16,0},{32,16},{48,32},{64,48},{80,64},{96,80},{112,96},{1... | collective-permute-start | bytes 344072 | tf_op jit(solution)/shard_map/ppermute | solution.py:316
  30.9 0.6 %copy-start.2 = (f32[56,512]{1,0:T(8,128)}, f32[56,512]{1,0:T(8,128)S(1)}, u32[]{:S(2)}) copy-start(f32[56,512]{1,0:T(8,128)S(1)} %collective-permute-done.2.west) | copy-start | bytes 344068
  31.6 0.6 %copy-start.3 = (f32[56,512]{1,0:T(8,128)}, f32[56,512]{1,0:T(8,128)S(1)}, u32[]{:S(2)}) copy-start(f32[56,512]{1,0:T(8,128)S(1)} %collective-permute-done.3.east) | copy-start | bytes 344068

commit v5 on v4

--- a/solution.py
+++ b/solution.py
@@ -53,7 +53,7 @@
     return open_face, w, s
 
 
-def forward(src, store, depth, cor):
+def forward(src, store, depth, cor, terms):
     level_count = src.shape[1]
     column = None
     for k in range(level_count):
@@ -64,10 +64,12 @@
         column = density if column is None else column + density
         pressure = buoyancy * column
         div = [None] * 4
-        for axis, speed in ((1, q[2]), (0, q[3])):
+        for d, (axis, speed) in enumerate(((1, q[2]), (0, q[3]))):
             open_face, w, s = face_speed(wet, speed, axis)
+            ratio = w / s
             for f in range(4):
                 central, damping = face_terms(q[f], axis)
+                terms[d, f, k] = central - ratio * damping
                 flux = open_face * (w * central - s * damping)
                 part = flux - shifted(flux, -1, axis)
                 div[f] = part if div[f] is None else div[f] + part
@@ -92,7 +94,7 @@
             store(f, k, value * wet)
 
 
-def backward(x, lam, store, g_ref, depth, cor):
+def backward(x, lam, store, g_ref, depth, cor, terms):
     level_count = x.shape[1]
     for k in range(level_count):
         wet = wet_of(depth, k)
@@ -127,14 +129,12 @@
         acc[0] = acc[0] - 0.2 * wet * density_bar[k]
         acc[1] = acc[1] + 0.8 * wet * density_bar[k]
         div_bar = [-courant * g[f] for f in range(4)]
-        for axis, speed_field in ((1, 2), (0, 3)):
+        for d, (axis, speed_field) in enumerate(((1, 2), (0, 3))):
             open_face, w, s = face_speed(wet, q[speed_field], axis)
-            ratio = w / s
             w_bar = None
             for f in range(4):
                 flux_bar = open_face * (div_bar[f] - shifted(div_bar[f], 1, axis))
-                central, damping = face_terms(q[f], axis)
-                part = flux_bar * (central - ratio * damping)
+                part = flux_bar * terms[d, f, k]
                 w_bar = part if w_bar is None else w_bar + part
                 alpha = flux_bar * w * SIXTIETH
                 beta = -flux_bar * s * SIXTIETH
@@ -167,7 +167,7 @@
 
 def two_step_kernel(
     margin, reach, own_x, own_c, own_d, north, south, west, east, rowmask_ref, cor_ref,
-    final_ref, grad_ref, x0, lam, x1, mu, g_ref, depth_ref,
+    final_ref, grad_ref, x0, lam, x1, mu, g_ref, depth_ref, terms_first, terms_second,
 ):
     fields, level_count, rows, cols = own_x.shape
     planes = fields * level_count
@@ -208,14 +208,15 @@
             ref[f, k] = value[:rows, :cols]
         return put
 
-    forward(x0, keep(x1), depth, cor)
-    forward(x1, keep_cropped(final_ref), depth, cor)
-    backward(x1, lam, keep(mu), g_ref, depth, cor)
-    backward(x0, mu, keep_cropped(grad_ref), g_ref, depth, cor)
-
-
-def lat_pack_kernel(margin, reach, own_x, own_c, own_d, north_msg, south_msg):
+    forward(x0, keep(x1), depth, cor, terms_first)
+    forward(x1, keep_cropped(final_ref), depth, cor, terms_second)
+    backward(x1, lam, keep(mu), g_ref, depth, cor, terms_second)
+    backward(x0, mu, keep_cropped(grad_ref), g_ref, depth, cor, terms_first)
+
+
+def lat_pack_kernel(margin, reach, own_x, own_c, sea_ref, level_ref, north_msg, south_msg, own_d):
     fields, level_count, rows, cols = own_x.shape
+    own_d[...] = (sea_ref[...] * level_ref[...]).astype(jnp.float32)
     planes = fields * level_count
     for f in range(fields):
         for k in range(level_count):
@@ -285,17 +286,16 @@
     margin = 12
     reach = 6
     planes = fields * level_count
-    depth = (seamask * levels).astype(jnp.float32)
     vmem = pl.BlockSpec(memory_space=pltpu.VMEM)
     msg_rows = (planes + 1) * margin + planes * reach
     lat_msg = jax.ShapeDtypeStruct((msg_rows, col_count), jnp.float32)
-    north_out, south_out = pl.pallas_call(
+    north_out, south_out, depth = pl.pallas_call(
         functools.partial(lat_pack_kernel, margin, reach),
-        out_shape=(lat_msg, lat_msg),
-        in_specs=[vmem] * 3,
-        out_specs=(vmem, vmem),
+        out_shape=(lat_msg, lat_msg, jax.ShapeDtypeStruct((row_count, col_count), jnp.float32)),
+        in_specs=[vmem] * 4,
+        out_specs=(vmem, vmem, vmem),
         interpret=INTERPRET,
-    )(state, cotangent, depth)
+    )(state, cotangent, seamask, levels)
     lat_count = lax.axis_size("lat")
     north = lax.ppermute(north_out, "lat", ring(lat_count, 1))
     south = lax.ppermute(south_out, "lat", ring(lat_count, -1))
@@ -327,7 +327,8 @@
         in_specs=[vmem] * 9,
         out_specs=(vmem, vmem),
         scratch_shapes=[pltpu.VMEM(frame, jnp.float32) for _ in range(5)]
-        + [pltpu.VMEM((frame_rows, frame_cols), jnp.float32)],
+        + [pltpu.VMEM((frame_rows, frame_cols), jnp.float32)]
+        + [pltpu.VMEM((2,) + frame, jnp.float32) for _ in range(2)],
         interpret=INTERPRET,
     )(state, cotangent, depth, north, south, west, east, rowmask, cor)
     return (final_state, adjoint_state)

time: 53.9 us -> 50.3 us (0.933)
  other arithmetic: 2.72 us -> 1.34 us
  Pallas kernels: 26.2 us -> 24.9 us
  waiting for transfers between devices: 11.8 us -> 10.9 us
    convert_element_type x1 -> x0, other arithmetic: 1.39 us -> none  [shards(): depth = (seamask * levels).astype(jnp.float32)]
    pallas_call x1, Pallas kernels: 21.5 us -> 20.2 us  [shards(): pl.pallas_call(functools.partial(two_step_kernel, margin, reach), out_sha...]
    ppermute x1, waiting for transfers between devices: 2.4 us -> 1.57 us  [shards(): west = lax.ppermute(west_out, 'lon', ring(lon_count, 1))]
  transfers between devices with their start and end apart: 4 -> 4, of which waited for: 3 -> 3; matrix products, arithmetic and copies ran while one was open for 2% -> 3% of each run, Pallas kernels for 0% -> 0%
where the time goes in v5:
time: 50.3 us; the launch traced here: 50.2 us
  Pallas kernels  24.9 us (50%)
  waiting for transfers between devices  10.9 us (22%)
  starting transfers between devices  10.3 us (20%)
  local copies, waits for them, and re-layouts  2.01 us (4%)
  other arithmetic  1.34 us (3%)
  between operations  0.64 us (1%)
    pallas_call x1, Pallas kernels, shards(): pl.pallas_call(functools.partial(two_step_kernel, margin, reach), out_sha...  20.2 us
    ppermute x1, waiting for transfers between devices, shards(): south = lax.ppermute(south_out, 'lat', ring(lat_count, -1))  5.2 us
    ppermute x1, starting transfers between devices, shards(): east = lax.ppermute(east_out, 'lon', ring(lon_count, -1))  4.87 us
    ppermute x1, waiting for transfers between devices, shards(): north = lax.ppermute(north_out, 'lat', ring(lat_count, 1))  4.16 us
    ppermute x1, starting transfers between devices, shards(): north = lax.ppermute(north_out, 'lat', ring(lat_count, 1))  4.12 us
    pallas_call x1, Pallas kernels, shards(): pl.pallas_call(functools.partial(lon_pack_kernel, margin, reach), out_sha...  2.64 us
    pallas_call x1, Pallas kernels, shards(): pl.pallas_call(functools.partial(lat_pack_kernel, margin, reach), out_sha...  2.08 us
    unnamed x8, local copies, waits for them, and re-layouts  2.01 us
  transfers between devices with their start and end apart: 4, of which 3 were waited for; matrix products, arithmetic and copies ran while one was open for 3% of the time, Pallas kernels for 0%

profile of v5, /device:TPU:1, one launch (start us, length us, event | category | flops | bytes accessed | tf_op | source)
XLA Modules:
  0.0 50.2 jit_solution(16281526255329844009)
XLA Ops:
  0.6 2.1 %shard_map.59 = (f32[300,256]{1,0:T(8,128)}, f32[300,256]{1,0:T(8,128)}, f32[32,256]{1,0:T(8,128)}) custom-call(f32[4,4,32,256]{3,2,1,0:T(8,128)} %own_x.5, f32[4,4,32,256]{3,2,1,0:T(8,128)} %own_c.5, s32[32,256]{1,0:T(8,128)} %sea_ref.1, s32[32,256]{1,0:T(8,128)} %level_ref.1), custom_call_target="tpu_custom_call" | custom-call | tf_op jit(solution)/shard_map/pallas_call | solution.py:292
  2.7 4.1 %collective-permute-start = (f32[300,256]{1,0:T(8,128)}, f32[300,256]{1,0:T(8,128)S(1)}, u32[]{:S(2)}, u32[]{:S(2)}) collective-permute-start(f32[300,256]{1,0:T(8,128)} %get-tuple-element.8), channel_id=1, source_target_pairs={{0,1},{1,2},{2,3},{3,4},{4,5},{5,6},{6,7},{7,8},{8,9},{9,10},{10,1... | collective-permute-start | bytes 921608 | tf_op jit(solution)/shard_map/ppermute | solution.py:300
  6.8 0.0 collective-permute-start.1
  6.8 4.2 %collective-permute-done.north = f32[300,256]{1,0:T(8,128)S(1)} collective-permute-done((f32[300,256]{1,0:T(8,128)}, f32[300,256]{1,0:T(8,128)S(1)}, u32[]{:S(2)}, u32[]{:S(2)}) %collective-permute-start) | collective-permute-done | bytes 307232 | tf_op jit(solution)/shard_map/ppermute | solution.py:300
  11.0 0.0 copy-start
  11.0 5.2 %collective-permute-done.1.south = f32[300,256]{1,0:T(8,128)S(1)} collective-permute-done((f32[300,256]{1,0:T(8,128)}, f32[300,256]{1,0:T(8,128)S(1)}, u32[]{:S(2)}, u32[]{:S(2)}) %collective-permute-start.1) | collective-permute-done | bytes 307232 | tf_op jit(solution)/shard_map/ppermute | solution.py:301
  16.2 0.0 copy-start.1
  16.2 0.0 copy-done
  16.2 0.7 %copy-done.1 = f32[300,256]{1,0:T(8,128)} copy-done((f32[300,256]{1,0:T(8,128)}, f32[300,256]{1,0:T(8,128)S(1)}, u32[]{:S(2)}) %copy-start.1) | copy-done | bytes 307224
  16.9 2.6 %shard_map.60 = (f32[56,512]{1,0:T(8,128)}, f32[56,512]{1,0:T(8,128)}) custom-call(f32[4,4,32,256]{3,2,1,0:T(8,128)} %own_x.5, f32[4,4,32,256]{3,2,1,0:T(8,128)} %own_c.5, f32[32,256]{1,0:T(8,128)} %get-tuple-element.7.own_d, f32[300,256]{1,0:T(8,128)} %copy-done, f32[300,256]{1,0:T(8,128)} %copy-done.1), custom_call_target="tpu_custom_call" | custom-call | tf_op jit(solution)/shard_map/pallas_call | solution.py:306
  19.6 1.3 %collective-permute-start.2 = (f32[56,512]{1,0:T(8,128)}, f32[56,512]{1,0:T(8,128)S(1)}, u32[]{:S(2)}, u32[]{:S(2)}) collective-permute-start(f32[56,512]{1,0:T(8,128)} %get-tuple-element.10), channel_id=1, source_target_pairs={{0,16},{16,32},{32,48},{48,64},{64,80},{80,96},{96,112},{112,128},... | collective-permute-start | bytes 344072 | tf_op jit(solution)/shard_map/ppermute | solution.py:315
  20.9 4.9 %collective-permute-start.3 = (f32[56,512]{1,0:T(8,128)}, f32[56,512]{1,0:T(8,128)S(1)}, u32[]{:S(2)}, u32[]{:S(2)}) collective-permute-start(f32[56,512]{1,0:T(8,128)} %get-tuple-element.11), channel_id=1, source_target_pairs={{0,240},{16,0},{32,16},{48,32},{64,48},{80,64},{96,80},{112,96},{1... | collective-permute-start | bytes 344072 | tf_op jit(solution)/shard_map/ppermute | solution.py:316
  25.8 0.7 %sine_multiply_fusion.cor_ref = f32[56,1]{1,0:T(8,128)} fusion(s32[]{:T(128)S(6)} %mul.29), kind=kLoop, calls=%fused_computation.2 | loop fusion | flops 560 | bytes 228 | tf_op jit(solution)/shard_map/mul | solution.py:321
  26.5 0.6 %fusion.4.rowmask_ref = f32[56,1]{1,0:T(8,128)} fusion(s32[]{:T(128)S(6)} %mul.29), kind=kLoop, calls=%fused_computation.6 | loop fusion | flops 448 | bytes 228 | tf_op jit(solution)/shard_map/convert_element_type | solution.py:319
  27.1 1.6 %collective-permute-done.2.west = f32[56,512]{1,0:T(8,128)S(1)} collective-permute-done((f32[56,512]{1,0:T(8,128)}, f32[56,512]{1,0:T(8,128)S(1)}, u32[]{:S(2)}, u32[]{:S(2)}) %collective-permute-start.2) | collective-permute-done | bytes 114720 | tf_op jit(solution)/shard_map/ppermute | solution.py:315
  28.7 0.0 copy-start.2
  28.7 0.0 collective-permute-done.3.east
  28.7 0.6 %copy-done.2 = f32[56,512]{1,0:T(8,128)} copy-done((f32[56,512]{1,0:T(8,128)}, f32[56,512]{1,0:T(8,128)S(1)}, u32[]{:S(2)}) %copy-start.2) | copy-done | bytes 114712
  29.3 0.0 copy-start.3
  29.3 0.6 %copy-done.3 = f32[56,512]{1,0:T(8,128)} copy-done((f32[56,512]{1,0:T(8,128)}, f32[56,512]{1,0:T(8,128)S(1)}, u32[]{:S(2)}) %copy-start.3) | copy-done | bytes 114712
  30.0 20.2 %shard_map.61 = (f32[4,4,32,256]{3,2,1,0:T(8,128)}, f32[4,4,32,256]{3,2,1,0:T(8,128)}) custom-call(f32[4,4,32,256]{3,2,1,0:T(8,128)} %own_x.5, f32[4,4,32,256]{3,2,1,0:T(8,128)} %own_c.5, f32[32,256]{1,0:T(8,128)} %get-tuple-element.7.own_d, f32[300,256]{1,0:T(8,128)} %copy-done, f32[300,256]{1,0:T(8,128)} %copy-done.1, f32[56,512]{1,0:T(8,128)} %copy-done.2, ...), custom_call_target="tpu_custom_call" | custom-call | tf_op jit(solution)/shard_map/pallas_call | solution.py:324
Async XLA Ops:
  2.7 8.3 %collective-permute-start = (f32[300,256]{1,0:T(8,128)}, f32[300,256]{1,0:T(8,128)S(1)}, u32[]{:S(2)}, u32[]{:S(2)}) collective-permute-start(f32[300,256]{1,0:T(8,128)} %get-tuple-element.8), channel_id=1, source_target_pairs={{0,1},{1,2},{2,3},{3,4},{4,5},{5,6},{6,7},{7,8},{8,9},{9,10},{10,1... | collective-permute-start | bytes 921608 | tf_op jit(solution)/shard_map/ppermute | solution.py:300
  6.8 9.4 %collective-permute-start.1 = (f32[300,256]{1,0:T(8,128)}, f32[300,256]{1,0:T(8,128)S(1)}, u32[]{:S(2)}, u32[]{:S(2)}) collective-permute-start(f32[300,256]{1,0:T(8,128)} %get-tuple-element.9), channel_id=1, source_target_pairs={{0,15},{1,0},{2,1},{3,2},{4,3},{5,4},{6,5},{7,6},{8,7},{9,8},{10,9... | collective-permute-start | bytes 921608 | tf_op jit(solution)/shard_map/ppermute | solution.py:301
  11.0 5.2 %copy-start = (f32[300,256]{1,0:T(8,128)}, f32[300,256]{1,0:T(8,128)S(1)}, u32[]{:S(2)}) copy-start(f32[300,256]{1,0:T(8,128)S(1)} %collective-permute-done.north) | copy-start | bytes 921604
  16.2 0.7 %copy-start.1 = (f32[300,256]{1,0:T(8,128)}, f32[300,256]{1,0:T(8,128)S(1)}, u32[]{:S(2)}) copy-start(f32[300,256]{1,0:T(8,128)S(1)} %collective-permute-done.1.south) | copy-start | bytes 921604
  19.6 9.1 %collective-permute-start.2 = (f32[56,512]{1,0:T(8,128)}, f32[56,512]{1,0:T(8,128)S(1)}, u32[]{:S(2)}, u32[]{:S(2)}) collective-permute-start(f32[56,512]{1,0:T(8,128)} %get-tuple-element.10), channel_id=1, source_target_pairs={{0,16},{16,32},{32,48},{48,64},{64,80},{80,96},{96,112},{112,128},... | collective-permute-start | bytes 344072 | tf_op jit(solution)/shard_map/ppermute | solution.py:315
  20.9 7.8 %collective-permute-start.3 = (f32[56,512]{1,0:T(8,128)}, f32[56,512]{1,0:T(8,128)S(1)}, u32[]{:S(2)}, u32[]{:S(2)}) collective-permute-start(f32[56,512]{1,0:T(8,128)} %get-tuple-element.11), channel_id=1, source_target_pairs={{0,240},{16,0},{32,16},{48,32},{64,48},{80,64},{96,80},{112,96},{1... | collective-permute-start | bytes 344072 | tf_op jit(solution)/shard_map/ppermute | solution.py:316
  28.7 0.6 %copy-start.2 = (f32[56,512]{1,0:T(8,128)}, f32[56,512]{1,0:T(8,128)S(1)}, u32[]{:S(2)}) copy-start(f32[56,512]{1,0:T(8,128)S(1)} %collective-permute-done.2.west) | copy-start | bytes 344068
  29.3 0.6 %copy-start.3 = (f32[56,512]{1,0:T(8,128)}, f32[56,512]{1,0:T(8,128)S(1)}, u32[]{:S(2)}) copy-start(f32[56,512]{1,0:T(8,128)S(1)} %collective-permute-done.3.east) | copy-start | bytes 344068

commit v6 on v5

--- a/solution.py
+++ b/solution.py
@@ -41,8 +41,8 @@
     p1 = shifted(q, 1, axis)
     p2 = shifted(q, 2, axis)
     p3 = shifted(q, 3, axis)
-    central = (37.0 * (q + p1) - 8.0 * (m1 + p2) + (m2 + p3)) * SIXTIETH
-    damping = (10.0 * (p1 - q) - 5.0 * (p2 - m1) + (p3 - m2)) * SIXTIETH
+    central = 37.0 * (q + p1) - 8.0 * (m1 + p2) + (m2 + p3)
+    damping = 10.0 * (p1 - q) - 5.0 * (p2 - m1) + (p3 - m2)
     return central, damping
 
 
@@ -67,6 +67,8 @@
         for d, (axis, speed) in enumerate(((1, q[2]), (0, q[3]))):
             open_face, w, s = face_speed(wet, speed, axis)
             ratio = w / s
+            w = w * SIXTIETH
+            s = s * SIXTIETH
             for f in range(4):
                 central, damping = face_terms(q[f], axis)
                 terms[d, f, k] = central - ratio * damping
@@ -131,16 +133,18 @@
         div_bar = [-courant * g[f] for f in range(4)]
         for d, (axis, speed_field) in enumerate(((1, 2), (0, 3))):
             open_face, w, s = face_speed(wet, q[speed_field], axis)
+            w = w * SIXTIETH
+            s = s * SIXTIETH
             w_bar = None
             for f in range(4):
                 flux_bar = open_face * (div_bar[f] - shifted(div_bar[f], 1, axis))
                 part = flux_bar * terms[d, f, k]
                 w_bar = part if w_bar is None else w_bar + part
-                alpha = flux_bar * w * SIXTIETH
-                beta = -flux_bar * s * SIXTIETH
+                alpha = flux_bar * w
+                beta = -flux_bar * s
                 for j in range(-2, 4):
                     acc[f] = acc[f] + shifted(CENTRAL[j] * alpha + DAMPING[j] * beta, -j, axis)
-            acc[speed_field] = acc[speed_field] + 0.5 * (w_bar + shifted(w_bar, -1, axis))
+            acc[speed_field] = acc[speed_field] + (0.5 * SIXTIETH) * (w_bar + shifted(w_bar, -1, axis))
         for f in range(4):
             store(f, k, acc[f])
 
@@ -285,12 +289,13 @@
     lat_start = lax.axis_index("lat") * row_count
     margin = 12
     reach = 6
+    rim = 10
     planes = fields * level_count
     vmem = pl.BlockSpec(memory_space=pltpu.VMEM)
-    msg_rows = (planes + 1) * margin + planes * reach
+    msg_rows = (planes + 1) * rim + planes * reach
     lat_msg = jax.ShapeDtypeStruct((msg_rows, col_count), jnp.float32)
     north_out, south_out, depth = pl.pallas_call(
-        functools.partial(lat_pack_kernel, margin, reach),
+        functools.partial(lat_pack_kernel, rim, reach),
         out_shape=(lat_msg, lat_msg, jax.ShapeDtypeStruct((row_count, col_count), jnp.float32)),
         in_specs=[vmem] * 4,
         out_specs=(vmem, vmem, vmem),
@@ -304,7 +309,7 @@
     msg_cols = 128 * (-(-(2 * planes + 1) // 10))
     lon_msg = jax.ShapeDtypeStruct((frame_rows, msg_cols), jnp.float32)
     west_out, east_out = pl.pallas_call(
-        functools.partial(lon_pack_kernel, margin, reach),
+        functools.partial(lon_pack_kernel, rim, reach),
         out_shape=(lon_msg, lon_msg),
         in_specs=[vmem] * 5,
         out_specs=(vmem, vmem),
@@ -322,7 +327,7 @@
     frame = (fields, level_count, frame_rows, frame_cols)
     out_block = jax.ShapeDtypeStruct((fields, level_count, row_count, col_count), jnp.float32)
     final_state, adjoint_state = pl.pallas_call(
-        functools.partial(two_step_kernel, margin, reach),
+        functools.partial(two_step_kernel, rim, reach),
         out_shape=(out_block, out_block),
         in_specs=[vmem] * 9,
         out_specs=(vmem, vmem),

time: 50.3 us -> 47.9 us (0.952)
  Pallas kernels: 24.9 us -> 23.2 us
  waiting for transfers between devices: 10.9 us -> 10.2 us
    pallas_call x3, Pallas kernels: 24.9 us -> 23.2 us  [the longest x1 18.5 us: shards(): pl.pallas_call(functools.partial(two_step_kernel, rim, reach), out_shape=...]
where the time goes in v6:
time: 47.9 us; the launch traced here: 47.7 us
  Pallas kernels  23.2 us (48%)
  starting transfers between devices  10.3 us (22%)
  waiting for transfers between devices  10.2 us (21%)
  local copies, waits for them, and re-layouts  1.98 us (4%)
  other arithmetic  1.34 us (3%)
  between operations  0.64 us (1%)
    pallas_call x1, Pallas kernels, shards(): pl.pallas_call(functools.partial(two_step_kernel, rim, reach), out_shape=...  18.5 us
    ppermute x1, starting transfers between devices, shards(): east = lax.ppermute(east_out, 'lon', ring(lon_count, -1))  4.87 us
    ppermute x1, waiting for transfers between devices, shards(): south = lax.ppermute(south_out, 'lat', ring(lat_count, -1))  4.85 us
    ppermute x1, starting transfers between devices, shards(): north = lax.ppermute(north_out, 'lat', ring(lat_count, 1))  4.12 us
    ppermute x1, waiting for transfers between devices, shards(): north = lax.ppermute(north_out, 'lat', ring(lat_count, 1))  3.81 us
    pallas_call x1, Pallas kernels, shards(): pl.pallas_call(functools.partial(lon_pack_kernel, rim, reach), out_shape=...  2.62 us
    pallas_call x1, Pallas kernels, shards(): pl.pallas_call(functools.partial(lat_pack_kernel, rim, reach), out_shape=...  2.06 us
    unnamed x8, local copies, waits for them, and re-layouts  1.98 us
  transfers between devices with their start and end apart: 4, of which 3 were waited for; matrix products, arithmetic and copies ran while one was open for 3% of the time, Pallas kernels for 0%

profile of v6, /device:TPU:1, one launch (start us, length us, event | category | flops | bytes accessed | tf_op | source)
XLA Modules:
  0.0 47.7 jit_solution(5765957317926462652)
XLA Ops:
  0.6 2.1 %shard_map.59 = (f32[266,256]{1,0:T(8,128)}, f32[266,256]{1,0:T(8,128)}, f32[32,256]{1,0:T(8,128)}) custom-call(f32[4,4,32,256]{3,2,1,0:T(8,128)} %own_x.5, f32[4,4,32,256]{3,2,1,0:T(8,128)} %own_c.5, s32[32,256]{1,0:T(8,128)} %sea_ref.1, s32[32,256]{1,0:T(8,128)} %level_ref.1), custom_call_target="tpu_custom_call" | custom-call | tf_op jit(solution)/shard_map/pallas_call | solution.py:297
  2.7 4.1 %collective-permute-start = (f32[266,256]{1,0:T(8,128)}, f32[266,256]{1,0:T(8,128)S(1)}, u32[]{:S(2)}, u32[]{:S(2)}) collective-permute-start(f32[266,256]{1,0:T(8,128)} %get-tuple-element.8), channel_id=1, source_target_pairs={{0,1},{1,2},{2,3},{3,4},{4,5},{5,6},{6,7},{7,8},{8,9},{9,10},{10,1... | collective-permute-start | bytes 817160 | tf_op jit(solution)/shard_map/ppermute | solution.py:305
  6.8 0.0 collective-permute-start.1
  6.8 3.8 %collective-permute-done.north = f32[266,256]{1,0:T(8,128)S(1)} collective-permute-done((f32[266,256]{1,0:T(8,128)}, f32[266,256]{1,0:T(8,128)S(1)}, u32[]{:S(2)}, u32[]{:S(2)}) %collective-permute-start) | collective-permute-done | bytes 272416 | tf_op jit(solution)/shard_map/ppermute | solution.py:305
  10.6 0.0 copy-start
  10.6 4.8 %collective-permute-done.1.south = f32[266,256]{1,0:T(8,128)S(1)} collective-permute-done((f32[266,256]{1,0:T(8,128)}, f32[266,256]{1,0:T(8,128)S(1)}, u32[]{:S(2)}, u32[]{:S(2)}) %collective-permute-start.1) | collective-permute-done | bytes 272416 | tf_op jit(solution)/shard_map/ppermute | solution.py:306
  15.5 0.0 copy-start.1
  15.5 0.0 copy-done
  15.5 0.7 %copy-done.1 = f32[266,256]{1,0:T(8,128)} copy-done((f32[266,256]{1,0:T(8,128)}, f32[266,256]{1,0:T(8,128)S(1)}, u32[]{:S(2)}) %copy-start.1) | copy-done | bytes 272408
  16.2 2.6 %shard_map.60 = (f32[56,512]{1,0:T(8,128)}, f32[56,512]{1,0:T(8,128)}) custom-call(f32[4,4,32,256]{3,2,1,0:T(8,128)} %own_x.5, f32[4,4,32,256]{3,2,1,0:T(8,128)} %own_c.5, f32[32,256]{1,0:T(8,128)} %get-tuple-element.7.own_d, f32[266,256]{1,0:T(8,128)} %copy-done, f32[266,256]{1,0:T(8,128)} %copy-done.1), custom_call_target="tpu_custom_call" | custom-call | tf_op jit(solution)/shard_map/pallas_call | solution.py:311
  18.8 1.3 %collective-permute-start.2 = (f32[56,512]{1,0:T(8,128)}, f32[56,512]{1,0:T(8,128)S(1)}, u32[]{:S(2)}, u32[]{:S(2)}) collective-permute-start(f32[56,512]{1,0:T(8,128)} %get-tuple-element.10), channel_id=1, source_target_pairs={{0,16},{16,32},{32,48},{48,64},{64,80},{80,96},{96,112},{112,128},... | collective-permute-start | bytes 344072 | tf_op jit(solution)/shard_map/ppermute | solution.py:320
  20.1 4.9 %collective-permute-start.3 = (f32[56,512]{1,0:T(8,128)}, f32[56,512]{1,0:T(8,128)S(1)}, u32[]{:S(2)}, u32[]{:S(2)}) collective-permute-start(f32[56,512]{1,0:T(8,128)} %get-tuple-element.11), channel_id=1, source_target_pairs={{0,240},{16,0},{32,16},{48,32},{64,48},{80,64},{96,80},{112,96},{1... | collective-permute-start | bytes 344072 | tf_op jit(solution)/shard_map/ppermute | solution.py:321
  25.0 0.7 %sine_multiply_fusion.cor_ref = f32[56,1]{1,0:T(8,128)} fusion(s32[]{:T(128)S(6)} %mul.29), kind=kLoop, calls=%fused_computation.2 | loop fusion | flops 560 | bytes 228 | tf_op jit(solution)/shard_map/mul | solution.py:326
  25.7 0.6 %fusion.4.rowmask_ref = f32[56,1]{1,0:T(8,128)} fusion(s32[]{:T(128)S(6)} %mul.29), kind=kLoop, calls=%fused_computation.6 | loop fusion | flops 448 | bytes 228 | tf_op jit(solution)/shard_map/convert_element_type | solution.py:324
  26.3 1.6 %collective-permute-done.2.west = f32[56,512]{1,0:T(8,128)S(1)} collective-permute-done((f32[56,512]{1,0:T(8,128)}, f32[56,512]{1,0:T(8,128)S(1)}, u32[]{:S(2)}, u32[]{:S(2)}) %collective-permute-start.2) | collective-permute-done | bytes 114720 | tf_op jit(solution)/shard_map/ppermute | solution.py:320
  27.9 0.0 copy-start.2
  27.9 0.0 collective-permute-done.3.east
  27.9 0.6 %copy-done.2 = f32[56,512]{1,0:T(8,128)} copy-done((f32[56,512]{1,0:T(8,128)}, f32[56,512]{1,0:T(8,128)S(1)}, u32[]{:S(2)}) %copy-start.2) | copy-done | bytes 114712
  28.6 0.0 copy-start.3
  28.6 0.6 %copy-done.3 = f32[56,512]{1,0:T(8,128)} copy-done((f32[56,512]{1,0:T(8,128)}, f32[56,512]{1,0:T(8,128)S(1)}, u32[]{:S(2)}) %copy-start.3) | copy-done | bytes 114712
  29.2 18.5 %shard_map.61 = (f32[4,4,32,256]{3,2,1,0:T(8,128)}, f32[4,4,32,256]{3,2,1,0:T(8,128)}) custom-call(f32[4,4,32,256]{3,2,1,0:T(8,128)} %own_x.5, f32[4,4,32,256]{3,2,1,0:T(8,128)} %own_c.5, f32[32,256]{1,0:T(8,128)} %get-tuple-element.7.own_d, f32[266,256]{1,0:T(8,128)} %copy-done, f32[266,256]{1,0:T(8,128)} %copy-done.1, f32[56,512]{1,0:T(8,128)} %copy-done.2, ...), custom_call_target="tpu_custom_call" | custom-call | tf_op jit(solution)/shard_map/pallas_call | solution.py:329
Async XLA Ops:
  2.7 7.9 %collective-permute-start = (f32[266,256]{1,0:T(8,128)}, f32[266,256]{1,0:T(8,128)S(1)}, u32[]{:S(2)}, u32[]{:S(2)}) collective-permute-start(f32[266,256]{1,0:T(8,128)} %get-tuple-element.8), channel_id=1, source_target_pairs={{0,1},{1,2},{2,3},{3,4},{4,5},{5,6},{6,7},{7,8},{8,9},{9,10},{10,1... | collective-permute-start | bytes 817160 | tf_op jit(solution)/shard_map/ppermute | solution.py:305
  6.8 8.7 %collective-permute-start.1 = (f32[266,256]{1,0:T(8,128)}, f32[266,256]{1,0:T(8,128)S(1)}, u32[]{:S(2)}, u32[]{:S(2)}) collective-permute-start(f32[266,256]{1,0:T(8,128)} %get-tuple-element.9), channel_id=1, source_target_pairs={{0,15},{1,0},{2,1},{3,2},{4,3},{5,4},{6,5},{7,6},{8,7},{9,8},{10,9... | collective-permute-start | bytes 817160 | tf_op jit(solution)/shard_map/ppermute | solution.py:306
  10.6 4.9 %copy-start = (f32[266,256]{1,0:T(8,128)}, f32[266,256]{1,0:T(8,128)S(1)}, u32[]{:S(2)}) copy-start(f32[266,256]{1,0:T(8,128)S(1)} %collective-permute-done.north) | copy-start | bytes 817156
  15.5 0.7 %copy-start.1 = (f32[266,256]{1,0:T(8,128)}, f32[266,256]{1,0:T(8,128)S(1)}, u32[]{:S(2)}) copy-start(f32[266,256]{1,0:T(8,128)S(1)} %collective-permute-done.1.south) | copy-start | bytes 817156
  18.8 9.1 %collective-permute-start.2 = (f32[56,512]{1,0:T(8,128)}, f32[56,512]{1,0:T(8,128)S(1)}, u32[]{:S(2)}, u32[]{:S(2)}) collective-permute-start(f32[56,512]{1,0:T(8,128)} %get-tuple-element.10), channel_id=1, source_target_pairs={{0,16},{16,32},{32,48},{48,64},{64,80},{80,96},{96,112},{112,128},... | collective-permute-start | bytes 344072 | tf_op jit(solution)/shard_map/ppermute | solution.py:320
  20.1 7.8 %collective-permute-start.3 = (f32[56,512]{1,0:T(8,128)}, f32[56,512]{1,0:T(8,128)S(1)}, u32[]{:S(2)}, u32[]{:S(2)}) collective-permute-start(f32[56,512]{1,0:T(8,128)} %get-tuple-element.11), channel_id=1, source_target_pairs={{0,240},{16,0},{32,16},{48,32},{64,48},{80,64},{96,80},{112,96},{1... | collective-permute-start | bytes 344072 | tf_op jit(solution)/shard_map/ppermute | solution.py:321
  27.9 0.6 %copy-start.2 = (f32[56,512]{1,0:T(8,128)}, f32[56,512]{1,0:T(8,128)S(1)}, u32[]{:S(2)}) copy-start(f32[56,512]{1,0:T(8,128)S(1)} %collective-permute-done.2.west) | copy-start | bytes 344068
  28.6 0.6 %copy-start.3 = (f32[56,512]{1,0:T(8,128)}, f32[56,512]{1,0:T(8,128)S(1)}, u32[]{:S(2)}) copy-start(f32[56,512]{1,0:T(8,128)S(1)} %collective-permute-done.3.east) | copy-start | bytes 344068

commit v7 on v6

--- a/solution.py
+++ b/solution.py
@@ -237,46 +237,63 @@
             south_msg[base + reach * p : base + reach * (p + 1), :] = own_c[f, k, 0:reach, :]
 
 
-def lon_pack_kernel(margin, reach, own_x, own_c, own_d, north, south, west_msg, east_msg, ext):
+def lon_strips(west_acc, east_acc, lane, p, ext_value):
+    cols = ext_value.shape[1]
+    block, offset = strip_place(p)
+    keep = (lane >= offset) & (lane < offset + 12)
+    last = shifted(ext_value[:, cols - 128 : cols], 116 - offset, 1)
+    first = shifted(ext_value[:, 0:128], -offset, 1)
+    west_acc[block] = west_acc[block] + jnp.where(keep, last, 0.0)
+    east_acc[block] = east_acc[block] + jnp.where(keep, first, 0.0)
+
+
+def lon_pack_own_kernel(own_x, own_c, own_d, west_msg, east_msg):
     fields, level_count, rows, cols = own_x.shape
     planes = fields * level_count
-    frame_rows = ext.shape[0]
-    lane = lax.broadcasted_iota(jnp.int32, (frame_rows, 128), 1)
-    west_acc = [jnp.zeros((frame_rows, 128), jnp.float32) for _ in range(west_msg.shape[1] // 128)]
-    east_acc = [jnp.zeros((frame_rows, 128), jnp.float32) for _ in range(east_msg.shape[1] // 128)]
-
-    def add_plane(p, own, south_rows, north_rows):
+    lane = lax.broadcasted_iota(jnp.int32, (rows, 128), 1)
+    blocks = west_msg.shape[1] // 128
+    west_acc = [jnp.zeros((rows, 128), jnp.float32) for _ in range(blocks)]
+    east_acc = [jnp.zeros((rows, 128), jnp.float32) for _ in range(blocks)]
+    for f in range(fields):
+        for k in range(level_count):
+            p = f * level_count + k
+            lon_strips(west_acc, east_acc, lane, p, own_x[f, k])
+            lon_strips(west_acc, east_acc, lane, planes + 1 + p, own_c[f, k])
+    lon_strips(west_acc, east_acc, lane, planes, own_d[...])
+    for block in range(blocks):
+        west_msg[:, 128 * block : 128 * (block + 1)] = west_acc[block]
+        east_msg[:, 128 * block : 128 * (block + 1)] = east_acc[block]
+
+
+def lon_pack_halo_kernel(margin, reach, west_own, east_own, north, south, west_msg, east_msg, ext):
+    rows = west_own.shape[0]
+    planes = (north.shape[0] - margin) // (margin + reach)
+    halo_rows = ext.shape[0]
+    lane = lax.broadcasted_iota(jnp.int32, (halo_rows, 128), 1)
+    blocks = west_msg.shape[1] // 128
+    west_acc = [jnp.zeros((halo_rows, 128), jnp.float32) for _ in range(blocks)]
+    east_acc = [jnp.zeros((halo_rows, 128), jnp.float32) for _ in range(blocks)]
+
+    def add_plane(p, south_rows, north_rows):
         depth = south_rows.shape[0]
         ext[...] = jnp.zeros(ext.shape, jnp.float32)
-        ext[0:rows, :] = own
-        ext[rows : rows + depth, :] = south_rows
-        ext[frame_rows - depth : frame_rows, :] = north_rows
-        block, offset = strip_place(p)
-        keep = (lane >= offset) & (lane < offset + 12)
-        last = shifted(ext[:, cols - 128 : cols], 116 - offset, 1)
-        first = shifted(ext[:, 0:128], -offset, 1)
-        west_acc[block] = west_acc[block] + jnp.where(keep, last, 0.0)
-        east_acc[block] = east_acc[block] + jnp.where(keep, first, 0.0)
-
-    for f in range(fields):
-        for k in range(level_count):
-            p = f * level_count + k
-            add_plane(p, own_x[f, k], south[margin * p : margin * (p + 1), :], north[margin * p : margin * (p + 1), :])
-    add_plane(
-        planes, own_d[...], south[margin * planes : margin * (planes + 1), :],
-        north[margin * planes : margin * (planes + 1), :],
-    )
+        ext[0:depth, :] = south_rows
+        ext[halo_rows - depth : halo_rows, :] = north_rows
+        lon_strips(west_acc, east_acc, lane, p, ext[...])
+
+    for p in range(planes + 1):
+        add_plane(p, south[margin * p : margin * (p + 1), :], north[margin * p : margin * (p + 1), :])
     base = margin * (planes + 1)
-    for f in range(fields):
-        for k in range(level_count):
-            p = f * level_count + k
-            add_plane(
-                planes + 1 + p, own_c[f, k], south[base + reach * p : base + reach * (p + 1), :],
-                north[base + reach * p : base + reach * (p + 1), :],
-            )
-    for block in range(len(west_acc)):
-        west_msg[:, 128 * block : 128 * (block + 1)] = west_acc[block]
-        east_msg[:, 128 * block : 128 * (block + 1)] = east_acc[block]
+    for p in range(planes):
+        add_plane(
+            planes + 1 + p, south[base + reach * p : base + reach * (p + 1), :],
+            north[base + reach * p : base + reach * (p + 1), :],
+        )
+    west_msg[0:rows, :] = west_own[...]
+    east_msg[0:rows, :] = east_own[...]
+    for block in range(blocks):
+        west_msg[rows:, 128 * block : 128 * (block + 1)] = west_acc[block]
+        east_msg[rows:, 128 * block : 128 * (block + 1)] = east_acc[block]
 
 
 def ring(count, step):
@@ -308,14 +325,22 @@
     frame_cols = -(-(col_count + 2 * margin) // 128) * 128
     msg_cols = 128 * (-(-(2 * planes + 1) // 10))
     lon_msg = jax.ShapeDtypeStruct((frame_rows, msg_cols), jnp.float32)
+    own_msg = jax.ShapeDtypeStruct((row_count, msg_cols), jnp.float32)
+    west_own, east_own = pl.pallas_call(
+        lon_pack_own_kernel,
+        out_shape=(own_msg, own_msg),
+        in_specs=[vmem] * 3,
+        out_specs=(vmem, vmem),
+        interpret=INTERPRET,
+    )(state, cotangent, depth)
     west_out, east_out = pl.pallas_call(
-        functools.partial(lon_pack_kernel, rim, reach),
+        functools.partial(lon_pack_halo_kernel, rim, reach),
         out_shape=(lon_msg, lon_msg),
-        in_specs=[vmem] * 5,
+        in_specs=[vmem] * 4,
         out_specs=(vmem, vmem),
-        scratch_shapes=[pltpu.VMEM((frame_rows, col_count), jnp.float32)],
+        scratch_shapes=[pltpu.VMEM((frame_rows - row_count, col_count), jnp.float32)],
         interpret=INTERPRET,
-    )(state, cotangent, depth, north, south)
+    )(west_own, east_own, north, south)
     lon_count = lax.axis_size("lon")
     west = lax.ppermute(west_out, "lon", ring(lon_count, 1))
     east = lax.ppermute(east_out, "lon", ring(lon_count, -1))

time: 47.9 us -> 47.4 us (0.990)
  waiting for transfers between devices: 10.2 us -> 8.05 us
  Pallas kernels: 23.2 us -> 24.9 us
    ppermute x1, waiting for transfers between devices: 3.81 us -> 1.63 us  [shards(): north = lax.ppermute(north_out, 'lat', ring(lat_count, 1))]
    pallas_call x1 -> x2, Pallas kernels: 2.62 us -> 4.3 us  [the longest x1 2.18 us: shards(): pl.pallas_call(lon_pack_own_kernel, out_shape=(own_msg, own_msg), in_spec...]
  transfers between devices with their start and end apart: 4 -> 4, of which waited for: 3 -> 3; matrix products, arithmetic and copies ran while one was open for 3% -> 3% of each run, Pallas kernels for 0% -> 5%
where the time goes in v7:
time: 47.4 us; the launch traced here: 47.3 us
  Pallas kernels  24.9 us (53%)
  starting transfers between devices  10.3 us (22%)
  waiting for transfers between devices  8.05 us (17%)
  local copies, waits for them, and re-layouts  1.98 us (4%)
  other arithmetic  1.35 us (3%)
  between operations  0.64 us (1%)
    pallas_call x1, Pallas kernels, shards(): pl.pallas_call(functools.partial(two_step_kernel, rim, reach), out_shape=...  18.5 us
    ppermute x1, starting transfers between devices, shards(): east = lax.ppermute(east_out, 'lon', ring(lon_count, -1))  4.87 us
    ppermute x1, waiting for transfers between devices, shards(): south = lax.ppermute(south_out, 'lat', ring(lat_count, -1))  4.85 us
    ppermute x1, starting transfers between devices, shards(): north = lax.ppermute(north_out, 'lat', ring(lat_count, 1))  4.12 us
    pallas_call x1, Pallas kernels, shards(): pl.pallas_call(lon_pack_own_kernel, out_shape=(own_msg, own_msg), in_spec...  2.18 us
    pallas_call x1, Pallas kernels, shards(): pl.pallas_call(functools.partial(lon_pack_halo_kernel, rim, reach), out_s...  2.12 us
    pallas_call x1, Pallas kernels, shards(): pl.pallas_call(functools.partial(lat_pack_kernel, rim, reach), out_shape=...  2.06 us
    unnamed x8, local copies, waits for them, and re-layouts  1.98 us
  transfers between devices with their start and end apart: 4, of which 3 were waited for; matrix products, arithmetic and copies ran while one was open for 3% of the time, Pallas kernels for 5%

profile of v7, /device:TPU:1, one launch (start us, length us, event | category | flops | bytes accessed | tf_op | source)
XLA Modules:
  0.0 47.3 jit_solution(18176241312114179896)
XLA Ops:
  0.6 2.1 %shard_map.59 = (f32[266,256]{1,0:T(8,128)}, f32[266,256]{1,0:T(8,128)}, f32[32,256]{1,0:T(8,128)}) custom-call(f32[4,4,32,256]{3,2,1,0:T(8,128)} %own_x.5, f32[4,4,32,256]{3,2,1,0:T(8,128)} %own_c.5, s32[32,256]{1,0:T(8,128)} %sea_ref.1, s32[32,256]{1,0:T(8,128)} %level_ref.1), custom_call_target="tpu_custom_call" | custom-call | tf_op jit(solution)/shard_map/pallas_call | solution.py:314
  2.7 4.1 %collective-permute-start = (f32[266,256]{1,0:T(8,128)}, f32[266,256]{1,0:T(8,128)S(1)}, u32[]{:S(2)}, u32[]{:S(2)}) collective-permute-start(f32[266,256]{1,0:T(8,128)} %get-tuple-element.10), channel_id=1, source_target_pairs={{0,1},{1,2},{2,3},{3,4},{4,5},{5,6},{6,7},{7,8},{8,9},{9,10},{10,1... | collective-permute-start | bytes 817160 | tf_op jit(solution)/shard_map/ppermute | solution.py:322
  6.8 0.0 collective-permute-start.1
  6.8 2.2 %shard_map.60 = (f32[32,512]{1,0:T(8,128)}, f32[32,512]{1,0:T(8,128)}) custom-call(f32[4,4,32,256]{3,2,1,0:T(8,128)} %own_x.5, f32[4,4,32,256]{3,2,1,0:T(8,128)} %own_c.5, f32[32,256]{1,0:T(8,128)} %get-tuple-element.9.own_d), custom_call_target="tpu_custom_call" | custom-call | tf_op jit(solution)/shard_map/pallas_call | solution.py:329
  9.0 1.6 %collective-permute-done.north = f32[266,256]{1,0:T(8,128)S(1)} collective-permute-done((f32[266,256]{1,0:T(8,128)}, f32[266,256]{1,0:T(8,128)S(1)}, u32[]{:S(2)}, u32[]{:S(2)}) %collective-permute-start) | collective-permute-done | bytes 272416 | tf_op jit(solution)/shard_map/ppermute | solution.py:322
  10.6 0.0 copy-start
  10.6 4.8 %collective-permute-done.1.south = f32[266,256]{1,0:T(8,128)S(1)} collective-permute-done((f32[266,256]{1,0:T(8,128)}, f32[266,256]{1,0:T(8,128)S(1)}, u32[]{:S(2)}, u32[]{:S(2)}) %collective-permute-start.1) | collective-permute-done | bytes 272416 | tf_op jit(solution)/shard_map/ppermute | solution.py:323
  15.5 0.0 copy-start.1
  15.5 0.0 copy-done
  15.5 0.7 %copy-done.1 = f32[266,256]{1,0:T(8,128)} copy-done((f32[266,256]{1,0:T(8,128)}, f32[266,256]{1,0:T(8,128)S(1)}, u32[]{:S(2)}) %copy-start.1) | copy-done | bytes 272408
  16.2 2.1 %shard_map.61 = (f32[56,512]{1,0:T(8,128)}, f32[56,512]{1,0:T(8,128)}) custom-call(f32[32,512]{1,0:T(8,128)} %get-tuple-element.12.west_own, f32[32,512]{1,0:T(8,128)} %get-tuple-element.13.east_own, f32[266,256]{1,0:T(8,128)} %copy-done, f32[266,256]{1,0:T(8,128)} %copy-done.1), custom_call_target="tpu_custom_call" | custom-call | tf_op jit(solution)/shard_map/pallas_call | solution.py:336
  18.3 1.3 %collective-permute-start.2 = (f32[56,512]{1,0:T(8,128)}, f32[56,512]{1,0:T(8,128)S(1)}, u32[]{:S(2)}, u32[]{:S(2)}) collective-permute-start(f32[56,512]{1,0:T(8,128)} %get-tuple-element.14), channel_id=1, source_target_pairs={{0,16},{16,32},{32,48},{48,64},{64,80},{80,96},{96,112},{112,128},... | collective-permute-start | bytes 344072 | tf_op jit(solution)/shard_map/ppermute | solution.py:345
  19.6 4.9 %collective-permute-start.3 = (f32[56,512]{1,0:T(8,128)}, f32[56,512]{1,0:T(8,128)S(1)}, u32[]{:S(2)}, u32[]{:S(2)}) collective-permute-start(f32[56,512]{1,0:T(8,128)} %get-tuple-element.15), channel_id=1, source_target_pairs={{0,240},{16,0},{32,16},{48,32},{64,48},{80,64},{96,80},{112,96},{1... | collective-permute-start | bytes 344072 | tf_op jit(solution)/shard_map/ppermute | solution.py:346
  24.5 0.7 %sine_multiply_fusion.cor_ref = f32[56,1]{1,0:T(8,128)} fusion(s32[]{:T(128)S(6)} %mul.29), kind=kLoop, calls=%fused_computation.2 | loop fusion | flops 560 | bytes 228 | tf_op jit(solution)/shard_map/mul | solution.py:351
  25.2 0.6 %fusion.4.rowmask_ref = f32[56,1]{1,0:T(8,128)} fusion(s32[]{:T(128)S(6)} %mul.29), kind=kLoop, calls=%fused_computation.6 | loop fusion | flops 448 | bytes 228 | tf_op jit(solution)/shard_map/convert_element_type | solution.py:349
  25.9 1.6 %collective-permute-done.2.west = f32[56,512]{1,0:T(8,128)S(1)} collective-permute-done((f32[56,512]{1,0:T(8,128)}, f32[56,512]{1,0:T(8,128)S(1)}, u32[]{:S(2)}, u32[]{:S(2)}) %collective-permute-start.2) | collective-permute-done | bytes 114720 | tf_op jit(solution)/shard_map/ppermute | solution.py:345
  27.4 0.0 copy-start.2
  27.4 0.0 collective-permute-done.3.east
  27.4 0.6 %copy-done.2 = f32[56,512]{1,0:T(8,128)} copy-done((f32[56,512]{1,0:T(8,128)}, f32[56,512]{1,0:T(8,128)S(1)}, u32[]{:S(2)}) %copy-start.2) | copy-done | bytes 114712
  28.1 0.0 copy-start.3
  28.1 0.6 %copy-done.3 = f32[56,512]{1,0:T(8,128)} copy-done((f32[56,512]{1,0:T(8,128)}, f32[56,512]{1,0:T(8,128)S(1)}, u32[]{:S(2)}) %copy-start.3) | copy-done | bytes 114712
  28.7 18.5 %shard_map.62 = (f32[4,4,32,256]{3,2,1,0:T(8,128)}, f32[4,4,32,256]{3,2,1,0:T(8,128)}) custom-call(f32[4,4,32,256]{3,2,1,0:T(8,128)} %own_x.5, f32[4,4,32,256]{3,2,1,0:T(8,128)} %own_c.5, f32[32,256]{1,0:T(8,128)} %get-tuple-element.9.own_d, f32[266,256]{1,0:T(8,128)} %copy-done, f32[266,256]{1,0:T(8,128)} %copy-done.1, f32[56,512]{1,0:T(8,128)} %copy-done.2, ...), custom_call_target="tpu_custom_call" | custom-call | tf_op jit(solution)/shard_map/pallas_call | solution.py:354
Async XLA Ops:
  2.7 7.9 %collective-permute-start = (f32[266,256]{1,0:T(8,128)}, f32[266,256]{1,0:T(8,128)S(1)}, u32[]{:S(2)}, u32[]{:S(2)}) collective-permute-start(f32[266,256]{1,0:T(8,128)} %get-tuple-element.10), channel_id=1, source_target_pairs={{0,1},{1,2},{2,3},{3,4},{4,5},{5,6},{6,7},{7,8},{8,9},{9,10},{10,1... | collective-permute-start | bytes 817160 | tf_op jit(solution)/shard_map/ppermute | solution.py:322
  6.8 8.7 %collective-permute-start.1 = (f32[266,256]{1,0:T(8,128)}, f32[266,256]{1,0:T(8,128)S(1)}, u32[]{:S(2)}, u32[]{:S(2)}) collective-permute-start(f32[266,256]{1,0:T(8,128)} %get-tuple-element.11), channel_id=1, source_target_pairs={{0,15},{1,0},{2,1},{3,2},{4,3},{5,4},{6,5},{7,6},{8,7},{9,8},{10,9... | collective-permute-start | bytes 817160 | tf_op jit(solution)/shard_map/ppermute | solution.py:323
  10.6 4.9 %copy-start = (f32[266,256]{1,0:T(8,128)}, f32[266,256]{1,0:T(8,128)S(1)}, u32[]{:S(2)}) copy-start(f32[266,256]{1,0:T(8,128)S(1)} %collective-permute-done.north) | copy-start | bytes 817156
  15.5 0.7 %copy-start.1 = (f32[266,256]{1,0:T(8,128)}, f32[266,256]{1,0:T(8,128)S(1)}, u32[]{:S(2)}) copy-start(f32[266,256]{1,0:T(8,128)S(1)} %collective-permute-done.1.south) | copy-start | bytes 817156
  18.3 9.1 %collective-permute-start.2 = (f32[56,512]{1,0:T(8,128)}, f32[56,512]{1,0:T(8,128)S(1)}, u32[]{:S(2)}, u32[]{:S(2)}) collective-permute-start(f32[56,512]{1,0:T(8,128)} %get-tuple-element.14), channel_id=1, source_target_pairs={{0,16},{16,32},{32,48},{48,64},{64,80},{80,96},{96,112},{112,128},... | collective-permute-start | bytes 344072 | tf_op jit(solution)/shard_map/ppermute | solution.py:345
  19.6 7.8 %collective-permute-start.3 = (f32[56,512]{1,0:T(8,128)}, f32[56,512]{1,0:T(8,128)S(1)}, u32[]{:S(2)}, u32[]{:S(2)}) collective-permute-start(f32[56,512]{1,0:T(8,128)} %get-tuple-element.15), channel_id=1, source_target_pairs={{0,240},{16,0},{32,16},{48,32},{64,48},{80,64},{96,80},{112,96},{1... | collective-permute-start | bytes 344072 | tf_op jit(solution)/shard_map/ppermute | solution.py:346
  27.4 0.6 %copy-start.2 = (f32[56,512]{1,0:T(8,128)}, f32[56,512]{1,0:T(8,128)S(1)}, u32[]{:S(2)}) copy-start(f32[56,512]{1,0:T(8,128)S(1)} %collective-permute-done.2.west) | copy-start | bytes 344068
  28.1 0.6 %copy-start.3 = (f32[56,512]{1,0:T(8,128)}, f32[56,512]{1,0:T(8,128)S(1)}, u32[]{:S(2)}) copy-start(f32[56,512]{1,0:T(8,128)S(1)} %collective-permute-done.3.east) | copy-start | bytes 344068

commit v8 on v7

--- a/solution.py
+++ b/solution.py
@@ -53,7 +53,7 @@
     return open_face, w, s
 
 
-def forward(src, store, depth, cor, terms):
+def forward(src, store, depth, cor, terms, faces):
     level_count = src.shape[1]
     column = None
     for k in range(level_count):
@@ -69,6 +69,9 @@
             ratio = w / s
             w = w * SIXTIETH
             s = s * SIXTIETH
+            faces[d, k, 0] = open_face
+            faces[d, k, 1] = w
+            faces[d, k, 2] = s
             for f in range(4):
                 central, damping = face_terms(q[f], axis)
                 terms[d, f, k] = central - ratio * damping
@@ -96,7 +99,7 @@
             store(f, k, value * wet)
 
 
-def backward(x, lam, store, g_ref, depth, cor, terms):
+def backward(x, lam, store, g_ref, depth, cor, terms, faces):
     level_count = x.shape[1]
     for k in range(level_count):
         wet = wet_of(depth, k)
@@ -132,9 +135,9 @@
         acc[1] = acc[1] + 0.8 * wet * density_bar[k]
         div_bar = [-courant * g[f] for f in range(4)]
         for d, (axis, speed_field) in enumerate(((1, 2), (0, 3))):
-            open_face, w, s = face_speed(wet, q[speed_field], axis)
-            w = w * SIXTIETH
-            s = s * SIXTIETH
+            open_face = faces[d, k, 0]
+            w = faces[d, k, 1]
+            s = faces[d, k, 2]
             w_bar = None
             for f in range(4):
                 flux_bar = open_face * (div_bar[f] - shifted(div_bar[f], 1, axis))
@@ -172,6 +175,7 @@
 def two_step_kernel(
     margin, reach, own_x, own_c, own_d, north, south, west, east, rowmask_ref, cor_ref,
     final_ref, grad_ref, x0, lam, x1, mu, g_ref, depth_ref, terms_first, terms_second,
+    faces_first, faces_second,
 ):
     fields, level_count, rows, cols = own_x.shape
     planes = fields * level_count
@@ -212,10 +216,10 @@
             ref[f, k] = value[:rows, :cols]
         return put
 
-    forward(x0, keep(x1), depth, cor, terms_first)
-    forward(x1, keep_cropped(final_ref), depth, cor, terms_second)
-    backward(x1, lam, keep(mu), g_ref, depth, cor, terms_second)
-    backward(x0, mu, keep_cropped(grad_ref), g_ref, depth, cor, terms_first)
+    forward(x0, keep(x1), depth, cor, terms_first, faces_first)
+    forward(x1, keep_cropped(final_ref), depth, cor, terms_second, faces_second)
+    backward(x1, lam, keep(mu), g_ref, depth, cor, terms_second, faces_second)
+    backward(x0, mu, keep_cropped(grad_ref), g_ref, depth, cor, terms_first, faces_first)
 
 
 def lat_pack_kernel(margin, reach, own_x, own_c, sea_ref, level_ref, north_msg, south_msg, own_d):
@@ -358,7 +362,8 @@
         out_specs=(vmem, vmem),
         scratch_shapes=[pltpu.VMEM(frame, jnp.float32) for _ in range(5)]
         + [pltpu.VMEM((frame_rows, frame_cols), jnp.float32)]
-        + [pltpu.VMEM((2,) + frame, jnp.float32) for _ in range(2)],
+        + [pltpu.VMEM((2,) + frame, jnp.float32) for _ in range(2)]
+        + [pltpu.VMEM((2, level_count, 3, frame_rows, frame_cols), jnp.float32) for _ in range(2)],
         interpret=INTERPRET,
     )(state, cotangent, depth, north, south, west, east, rowmask, cor)
     return (final_state, adjoint_state)

time: 47.4 us -> 47.2 us (level)
  no operation moved by 1% of the time
where the time goes in v8:
time: 47.2 us; the launch traced here: 47 us
  Pallas kernels  24.6 us (52%)
  starting transfers between devices  10.3 us (22%)
  waiting for transfers between devices  8.05 us (17%)
  local copies, waits for them, and re-layouts  1.98 us (4%)
  other arithmetic  1.35 us (3%)
  between operations  0.64 us (1%)
    pallas_call x1, Pallas kernels, shards(): pl.pallas_call(functools.partial(two_step_kernel, rim, reach), out_shape=...  18.3 us
    ppermute x1, starting transfers between devices, shards(): east = lax.ppermute(east_out, 'lon', ring(lon_count, -1))  4.87 us
    ppermute x1, waiting for transfers between devices, shards(): south = lax.ppermute(south_out, 'lat', ring(lat_count, -1))  4.85 us
    ppermute x1, starting transfers between devices, shards(): north = lax.ppermute(north_out, 'lat', ring(lat_count, 1))  4.12 us
    pallas_call x1, Pallas kernels, shards(): pl.pallas_call(lon_pack_own_kernel, out_shape=(own_msg, own_msg), in_spec...  2.18 us
    pallas_call x1, Pallas kernels, shards(): pl.pallas_call(functools.partial(lon_pack_halo_kernel, rim, reach), out_s...  2.12 us
    pallas_call x1, Pallas kernels, shards(): pl.pallas_call(functools.partial(lat_pack_kernel, rim, reach), out_shape=...  2.06 us
    unnamed x8, local copies, waits for them, and re-layouts  1.98 us
  transfers between devices with their start and end apart: 4, of which 3 were waited for; matrix products, arithmetic and copies ran while one was open for 3% of the time, Pallas kernels for 5%

profile of v8, /device:TPU:1, one launch (start us, length us, event | category | flops | bytes accessed | tf_op | source)
XLA Modules:
  0.0 47.0 jit_solution(12583054734432859401)
XLA Ops:
  0.6 2.1 %shard_map.59 = (f32[266,256]{1,0:T(8,128)}, f32[266,256]{1,0:T(8,128)}, f32[32,256]{1,0:T(8,128)}) custom-call(f32[4,4,32,256]{3,2,1,0:T(8,128)} %own_x.5, f32[4,4,32,256]{3,2,1,0:T(8,128)} %own_c.5, s32[32,256]{1,0:T(8,128)} %sea_ref.1, s32[32,256]{1,0:T(8,128)} %level_ref.1), custom_call_target="tpu_custom_call" | custom-call | tf_op jit(solution)/shard_map/pallas_call | solution.py:318
  2.7 4.1 %collective-permute-start = (f32[266,256]{1,0:T(8,128)}, f32[266,256]{1,0:T(8,128)S(1)}, u32[]{:S(2)}, u32[]{:S(2)}) collective-permute-start(f32[266,256]{1,0:T(8,128)} %get-tuple-element.10), channel_id=1, source_target_pairs={{0,1},{1,2},{2,3},{3,4},{4,5},{5,6},{6,7},{7,8},{8,9},{9,10},{10,1... | collective-permute-start | bytes 817160 | tf_op jit(solution)/shard_map/ppermute | solution.py:326
  6.8 0.0 collective-permute-start.1
  6.8 2.2 %shard_map.60 = (f32[32,512]{1,0:T(8,128)}, f32[32,512]{1,0:T(8,128)}) custom-call(f32[4,4,32,256]{3,2,1,0:T(8,128)} %own_x.5, f32[4,4,32,256]{3,2,1,0:T(8,128)} %own_c.5, f32[32,256]{1,0:T(8,128)} %get-tuple-element.9.own_d), custom_call_target="tpu_custom_call" | custom-call | tf_op jit(solution)/shard_map/pallas_call | solution.py:333
  9.0 1.6 %collective-permute-done.north = f32[266,256]{1,0:T(8,128)S(1)} collective-permute-done((f32[266,256]{1,0:T(8,128)}, f32[266,256]{1,0:T(8,128)S(1)}, u32[]{:S(2)}, u32[]{:S(2)}) %collective-permute-start) | collective-permute-done | bytes 272416 | tf_op jit(solution)/shard_map/ppermute | solution.py:326
  10.6 0.0 copy-start
  10.6 4.8 %collective-permute-done.1.south = f32[266,256]{1,0:T(8,128)S(1)} collective-permute-done((f32[266,256]{1,0:T(8,128)}, f32[266,256]{1,0:T(8,128)S(1)}, u32[]{:S(2)}, u32[]{:S(2)}) %collective-permute-start.1) | collective-permute-done | bytes 272416 | tf_op jit(solution)/shard_map/ppermute | solution.py:327
  15.5 0.0 copy-start.1
  15.5 0.0 copy-done
  15.5 0.7 %copy-done.1 = f32[266,256]{1,0:T(8,128)} copy-done((f32[266,256]{1,0:T(8,128)}, f32[266,256]{1,0:T(8,128)S(1)}, u32[]{:S(2)}) %copy-start.1) | copy-done | bytes 272408
  16.2 2.1 %shard_map.61 = (f32[56,512]{1,0:T(8,128)}, f32[56,512]{1,0:T(8,128)}) custom-call(f32[32,512]{1,0:T(8,128)} %get-tuple-element.12.west_own, f32[32,512]{1,0:T(8,128)} %get-tuple-element.13.east_own, f32[266,256]{1,0:T(8,128)} %copy-done, f32[266,256]{1,0:T(8,128)} %copy-done.1), custom_call_target="tpu_custom_call" | custom-call | tf_op jit(solution)/shard_map/pallas_call | solution.py:340
  18.3 1.3 %collective-permute-start.2 = (f32[56,512]{1,0:T(8,128)}, f32[56,512]{1,0:T(8,128)S(1)}, u32[]{:S(2)}, u32[]{:S(2)}) collective-permute-start(f32[56,512]{1,0:T(8,128)} %get-tuple-element.14), channel_id=1, source_target_pairs={{0,16},{16,32},{32,48},{48,64},{64,80},{80,96},{96,112},{112,128},... | collective-permute-start | bytes 344072 | tf_op jit(solution)/shard_map/ppermute | solution.py:349
  19.6 4.9 %collective-permute-start.3 = (f32[56,512]{1,0:T(8,128)}, f32[56,512]{1,0:T(8,128)S(1)}, u32[]{:S(2)}, u32[]{:S(2)}) collective-permute-start(f32[56,512]{1,0:T(8,128)} %get-tuple-element.15), channel_id=1, source_target_pairs={{0,240},{16,0},{32,16},{48,32},{64,48},{80,64},{96,80},{112,96},{1... | collective-permute-start | bytes 344072 | tf_op jit(solution)/shard_map/ppermute | solution.py:350
  24.5 0.7 %sine_multiply_fusion.cor_ref = f32[56,1]{1,0:T(8,128)} fusion(s32[]{:T(128)S(6)} %mul.29), kind=kLoop, calls=%fused_computation.2 | loop fusion | flops 560 | bytes 228 | tf_op jit(solution)/shard_map/mul | solution.py:355
  25.2 0.6 %fusion.4.rowmask_ref = f32[56,1]{1,0:T(8,128)} fusion(s32[]{:T(128)S(6)} %mul.29), kind=kLoop, calls=%fused_computation.6 | loop fusion | flops 448 | bytes 228 | tf_op jit(solution)/shard_map/convert_element_type | solution.py:353
  25.9 1.6 %collective-permute-done.2.west = f32[56,512]{1,0:T(8,128)S(1)} collective-permute-done((f32[56,512]{1,0:T(8,128)}, f32[56,512]{1,0:T(8,128)S(1)}, u32[]{:S(2)}, u32[]{:S(2)}) %collective-permute-start.2) | collective-permute-done | bytes 114720 | tf_op jit(solution)/shard_map/ppermute | solution.py:349
  27.4 0.0 copy-start.2
  27.4 0.0 collective-permute-done.3.east
  27.4 0.6 %copy-done.2 = f32[56,512]{1,0:T(8,128)} copy-done((f32[56,512]{1,0:T(8,128)}, f32[56,512]{1,0:T(8,128)S(1)}, u32[]{:S(2)}) %copy-start.2) | copy-done | bytes 114712
  28.1 0.0 copy-start.3
  28.1 0.6 %copy-done.3 = f32[56,512]{1,0:T(8,128)} copy-done((f32[56,512]{1,0:T(8,128)}, f32[56,512]{1,0:T(8,128)S(1)}, u32[]{:S(2)}) %copy-start.3) | copy-done | bytes 114712
  28.7 18.3 %shard_map.62 = (f32[4,4,32,256]{3,2,1,0:T(8,128)}, f32[4,4,32,256]{3,2,1,0:T(8,128)}) custom-call(f32[4,4,32,256]{3,2,1,0:T(8,128)} %own_x.5, f32[4,4,32,256]{3,2,1,0:T(8,128)} %own_c.5, f32[32,256]{1,0:T(8,128)} %get-tuple-element.9.own_d, f32[266,256]{1,0:T(8,128)} %copy-done, f32[266,256]{1,0:T(8,128)} %copy-done.1, f32[56,512]{1,0:T(8,128)} %copy-done.2, ...), custom_call_target="tpu_custom_call" | custom-call | tf_op jit(solution)/shard_map/pallas_call | solution.py:358
Async XLA Ops:
  2.7 7.9 %collective-permute-start = (f32[266,256]{1,0:T(8,128)}, f32[266,256]{1,0:T(8,128)S(1)}, u32[]{:S(2)}, u32[]{:S(2)}) collective-permute-start(f32[266,256]{1,0:T(8,128)} %get-tuple-element.10), channel_id=1, source_target_pairs={{0,1},{1,2},{2,3},{3,4},{4,5},{5,6},{6,7},{7,8},{8,9},{9,10},{10,1... | collective-permute-start | bytes 817160 | tf_op jit(solution)/shard_map/ppermute | solution.py:326
  6.8 8.7 %collective-permute-start.1 = (f32[266,256]{1,0:T(8,128)}, f32[266,256]{1,0:T(8,128)S(1)}, u32[]{:S(2)}, u32[]{:S(2)}) collective-permute-start(f32[266,256]{1,0:T(8,128)} %get-tuple-element.11), channel_id=1, source_target_pairs={{0,15},{1,0},{2,1},{3,2},{4,3},{5,4},{6,5},{7,6},{8,7},{9,8},{10,9... | collective-permute-start | bytes 817160 | tf_op jit(solution)/shard_map/ppermute | solution.py:327
  10.6 4.9 %copy-start = (f32[266,256]{1,0:T(8,128)}, f32[266,256]{1,0:T(8,128)S(1)}, u32[]{:S(2)}) copy-start(f32[266,256]{1,0:T(8,128)S(1)} %collective-permute-done.north) | copy-start | bytes 817156
  15.5 0.7 %copy-start.1 = (f32[266,256]{1,0:T(8,128)}, f32[266,256]{1,0:T(8,128)S(1)}, u32[]{:S(2)}) copy-start(f32[266,256]{1,0:T(8,128)S(1)} %collective-permute-done.1.south) | copy-start | bytes 817156
  18.3 9.1 %collective-permute-start.2 = (f32[56,512]{1,0:T(8,128)}, f32[56,512]{1,0:T(8,128)S(1)}, u32[]{:S(2)}, u32[]{:S(2)}) collective-permute-start(f32[56,512]{1,0:T(8,128)} %get-tuple-element.14), channel_id=1, source_target_pairs={{0,16},{16,32},{32,48},{48,64},{64,80},{80,96},{96,112},{112,128},... | collective-permute-start | bytes 344072 | tf_op jit(solution)/shard_map/ppermute | solution.py:349
  19.6 7.8 %collective-permute-start.3 = (f32[56,512]{1,0:T(8,128)}, f32[56,512]{1,0:T(8,128)S(1)}, u32[]{:S(2)}, u32[]{:S(2)}) collective-permute-start(f32[56,512]{1,0:T(8,128)} %get-tuple-element.15), channel_id=1, source_target_pairs={{0,240},{16,0},{32,16},{48,32},{64,48},{80,64},{96,80},{112,96},{1... | collective-permute-start | bytes 344072 | tf_op jit(solution)/shard_map/ppermute | solution.py:350
  27.4 0.6 %copy-start.2 = (f32[56,512]{1,0:T(8,128)}, f32[56,512]{1,0:T(8,128)S(1)}, u32[]{:S(2)}) copy-start(f32[56,512]{1,0:T(8,128)S(1)} %collective-permute-done.2.west) | copy-start | bytes 344068
  28.1 0.6 %copy-start.3 = (f32[56,512]{1,0:T(8,128)}, f32[56,512]{1,0:T(8,128)S(1)}, u32[]{:S(2)}) copy-start(f32[56,512]{1,0:T(8,128)S(1)} %collective-permute-done.3.east) | copy-start | bytes 344068

commit v9 on v8

--- a/solution.py
+++ b/solution.py
@@ -145,8 +145,19 @@
                 w_bar = part if w_bar is None else w_bar + part
                 alpha = flux_bar * w
                 beta = -flux_bar * s
-                for j in range(-2, 4):
-                    acc[f] = acc[f] + shifted(CENTRAL[j] * alpha + DAMPING[j] * beta, -j, axis)
+                alpha8 = 8.0 * alpha
+                beta5 = 5.0 * beta
+                alpha37 = 37.0 * alpha
+                beta10 = 10.0 * beta
+                acc[f] = (
+                    acc[f]
+                    + (alpha37 - beta10)
+                    + shifted(alpha - beta, 2, axis)
+                    + shifted(beta5 - alpha8, 1, axis)
+                    + shifted(alpha37 + beta10, -1, axis)
+                    - shifted(alpha8 + beta5, -2, axis)
+                    + shifted(alpha + beta, -3, axis)
+                )
             acc[speed_field] = acc[speed_field] + (0.5 * SIXTIETH) * (w_bar + shifted(w_bar, -1, axis))
         for f in range(4):
             store(f, k, acc[f])

time: 47.2 us -> 47.1 us (level)
  no operation moved by 1% of the time
where the time goes in v9:
time: 47.1 us; the launch traced here: 46.9 us
  Pallas kernels  24.6 us (52%)
  starting transfers between devices  10.3 us (22%)
  waiting for transfers between devices  8.05 us (17%)
  local copies, waits for them, and re-layouts  1.98 us (4%)
  other arithmetic  1.35 us (3%)
  between operations  0.64 us (1%)
    pallas_call x1, Pallas kernels, shards(): pl.pallas_call(functools.partial(two_step_kernel, rim, reach), out_shape=...  18.2 us
    ppermute x1, starting transfers between devices, shards(): east = lax.ppermute(east_out, 'lon', ring(lon_count, -1))  4.87 us
    ppermute x1, waiting for transfers between devices, shards(): south = lax.ppermute(south_out, 'lat', ring(lat_count, -1))  4.85 us
    ppermute x1, starting transfers between devices, shards(): north = lax.ppermute(north_out, 'lat', ring(lat_count, 1))  4.12 us
    pallas_call x1, Pallas kernels, shards(): pl.pallas_call(lon_pack_own_kernel, out_shape=(own_msg, own_msg), in_spec...  2.18 us
    pallas_call x1, Pallas kernels, shards(): pl.pallas_call(functools.partial(lon_pack_halo_kernel, rim, reach), out_s...  2.12 us
    pallas_call x1, Pallas kernels, shards(): pl.pallas_call(functools.partial(lat_pack_kernel, rim, reach), out_shape=...  2.06 us
    unnamed x8, local copies, waits for them, and re-layouts  1.98 us
  transfers between devices with their start and end apart: 4, of which 3 were waited for; matrix products, arithmetic and copies ran while one was open for 3% of the time, Pallas kernels for 5%

profile of v9, /device:TPU:1, one launch (start us, length us, event | category | flops | bytes accessed | tf_op | source)
XLA Modules:
  0.0 46.9 jit_solution(10566316160232712052)
XLA Ops:
  0.6 2.1 %shard_map.59 = (f32[266,256]{1,0:T(8,128)}, f32[266,256]{1,0:T(8,128)}, f32[32,256]{1,0:T(8,128)}) custom-call(f32[4,4,32,256]{3,2,1,0:T(8,128)} %own_x.5, f32[4,4,32,256]{3,2,1,0:T(8,128)} %own_c.5, s32[32,256]{1,0:T(8,128)} %sea_ref.1, s32[32,256]{1,0:T(8,128)} %level_ref.1), custom_call_target="tpu_custom_call" | custom-call | tf_op jit(solution)/shard_map/pallas_call | solution.py:329
  2.7 4.1 %collective-permute-start = (f32[266,256]{1,0:T(8,128)}, f32[266,256]{1,0:T(8,128)S(1)}, u32[]{:S(2)}, u32[]{:S(2)}) collective-permute-start(f32[266,256]{1,0:T(8,128)} %get-tuple-element.10), channel_id=1, source_target_pairs={{0,1},{1,2},{2,3},{3,4},{4,5},{5,6},{6,7},{7,8},{8,9},{9,10},{10,1... | collective-permute-start | bytes 817160 | tf_op jit(solution)/shard_map/ppermute | solution.py:337
  6.8 0.0 collective-permute-start.1
  6.8 2.2 %shard_map.60 = (f32[32,512]{1,0:T(8,128)}, f32[32,512]{1,0:T(8,128)}) custom-call(f32[4,4,32,256]{3,2,1,0:T(8,128)} %own_x.5, f32[4,4,32,256]{3,2,1,0:T(8,128)} %own_c.5, f32[32,256]{1,0:T(8,128)} %get-tuple-element.9.own_d), custom_call_target="tpu_custom_call" | custom-call | tf_op jit(solution)/shard_map/pallas_call | solution.py:344
  9.0 1.6 %collective-permute-done.north = f32[266,256]{1,0:T(8,128)S(1)} collective-permute-done((f32[266,256]{1,0:T(8,128)}, f32[266,256]{1,0:T(8,128)S(1)}, u32[]{:S(2)}, u32[]{:S(2)}) %collective-permute-start) | collective-permute-done | bytes 272416 | tf_op jit(solution)/shard_map/ppermute | solution.py:337
  10.6 0.0 copy-start
  10.6 4.8 %collective-permute-done.1.south = f32[266,256]{1,0:T(8,128)S(1)} collective-permute-done((f32[266,256]{1,0:T(8,128)}, f32[266,256]{1,0:T(8,128)S(1)}, u32[]{:S(2)}, u32[]{:S(2)}) %collective-permute-start.1) | collective-permute-done | bytes 272416 | tf_op jit(solution)/shard_map/ppermute | solution.py:338
  15.5 0.0 copy-start.1
  15.5 0.0 copy-done
  15.5 0.7 %copy-done.1 = f32[266,256]{1,0:T(8,128)} copy-done((f32[266,256]{1,0:T(8,128)}, f32[266,256]{1,0:T(8,128)S(1)}, u32[]{:S(2)}) %copy-start.1) | copy-done | bytes 272408
  16.2 2.1 %shard_map.61 = (f32[56,512]{1,0:T(8,128)}, f32[56,512]{1,0:T(8,128)}) custom-call(f32[32,512]{1,0:T(8,128)} %get-tuple-element.12.west_own, f32[32,512]{1,0:T(8,128)} %get-tuple-element.13.east_own, f32[266,256]{1,0:T(8,128)} %copy-done, f32[266,256]{1,0:T(8,128)} %copy-done.1), custom_call_target="tpu_custom_call" | custom-call | tf_op jit(solution)/shard_map/pallas_call | solution.py:351
  18.3 1.3 %collective-permute-start.2 = (f32[56,512]{1,0:T(8,128)}, f32[56,512]{1,0:T(8,128)S(1)}, u32[]{:S(2)}, u32[]{:S(2)}) collective-permute-start(f32[56,512]{1,0:T(8,128)} %get-tuple-element.14), channel_id=1, source_target_pairs={{0,16},{16,32},{32,48},{48,64},{64,80},{80,96},{96,112},{112,128},... | collective-permute-start | bytes 344072 | tf_op jit(solution)/shard_map/ppermute | solution.py:360
  19.6 4.9 %collective-permute-start.3 = (f32[56,512]{1,0:T(8,128)}, f32[56,512]{1,0:T(8,128)S(1)}, u32[]{:S(2)}, u32[]{:S(2)}) collective-permute-start(f32[56,512]{1,0:T(8,128)} %get-tuple-element.15), channel_id=1, source_target_pairs={{0,240},{16,0},{32,16},{48,32},{64,48},{80,64},{96,80},{112,96},{1... | collective-permute-start | bytes 344072 | tf_op jit(solution)/shard_map/ppermute | solution.py:361
  24.5 0.7 %sine_multiply_fusion.cor_ref = f32[56,1]{1,0:T(8,128)} fusion(s32[]{:T(128)S(6)} %mul.29), kind=kLoop, calls=%fused_computation.2 | loop fusion | flops 560 | bytes 228 | tf_op jit(solution)/shard_map/mul | solution.py:366
  25.2 0.6 %fusion.4.rowmask_ref = f32[56,1]{1,0:T(8,128)} fusion(s32[]{:T(128)S(6)} %mul.29), kind=kLoop, calls=%fused_computation.6 | loop fusion | flops 448 | bytes 228 | tf_op jit(solution)/shard_map/convert_element_type | solution.py:364
  25.9 1.6 %collective-permute-done.2.west = f32[56,512]{1,0:T(8,128)S(1)} collective-permute-done((f32[56,512]{1,0:T(8,128)}, f32[56,512]{1,0:T(8,128)S(1)}, u32[]{:S(2)}, u32[]{:S(2)}) %collective-permute-start.2) | collective-permute-done | bytes 114720 | tf_op jit(solution)/shard_map/ppermute | solution.py:360
  27.4 0.0 copy-start.2
  27.4 0.0 collective-permute-done.3.east
  27.4 0.6 %copy-done.2 = f32[56,512]{1,0:T(8,128)} copy-done((f32[56,512]{1,0:T(8,128)}, f32[56,512]{1,0:T(8,128)S(1)}, u32[]{:S(2)}) %copy-start.2) | copy-done | bytes 114712
  28.1 0.0 copy-start.3
  28.1 0.6 %copy-done.3 = f32[56,512]{1,0:T(8,128)} copy-done((f32[56,512]{1,0:T(8,128)}, f32[56,512]{1,0:T(8,128)S(1)}, u32[]{:S(2)}) %copy-start.3) | copy-done | bytes 114712
  28.7 18.2 %shard_map.62 = (f32[4,4,32,256]{3,2,1,0:T(8,128)}, f32[4,4,32,256]{3,2,1,0:T(8,128)}) custom-call(f32[4,4,32,256]{3,2,1,0:T(8,128)} %own_x.5, f32[4,4,32,256]{3,2,1,0:T(8,128)} %own_c.5, f32[32,256]{1,0:T(8,128)} %get-tuple-element.9.own_d, f32[266,256]{1,0:T(8,128)} %copy-done, f32[266,256]{1,0:T(8,128)} %copy-done.1, f32[56,512]{1,0:T(8,128)} %copy-done.2, ...), custom_call_target="tpu_custom_call" | custom-call | tf_op jit(solution)/shard_map/pallas_call | solution.py:369
Async XLA Ops:
  2.7 7.9 %collective-permute-start = (f32[266,256]{1,0:T(8,128)}, f32[266,256]{1,0:T(8,128)S(1)}, u32[]{:S(2)}, u32[]{:S(2)}) collective-permute-start(f32[266,256]{1,0:T(8,128)} %get-tuple-element.10), channel_id=1, source_target_pairs={{0,1},{1,2},{2,3},{3,4},{4,5},{5,6},{6,7},{7,8},{8,9},{9,10},{10,1... | collective-permute-start | bytes 817160 | tf_op jit(solution)/shard_map/ppermute | solution.py:337
  6.8 8.7 %collective-permute-start.1 = (f32[266,256]{1,0:T(8,128)}, f32[266,256]{1,0:T(8,128)S(1)}, u32[]{:S(2)}, u32[]{:S(2)}) collective-permute-start(f32[266,256]{1,0:T(8,128)} %get-tuple-element.11), channel_id=1, source_target_pairs={{0,15},{1,0},{2,1},{3,2},{4,3},{5,4},{6,5},{7,6},{8,7},{9,8},{10,9... | collective-permute-start | bytes 817160 | tf_op jit(solution)/shard_map/ppermute | solution.py:338
  10.6 4.9 %copy-start = (f32[266,256]{1,0:T(8,128)}, f32[266,256]{1,0:T(8,128)S(1)}, u32[]{:S(2)}) copy-start(f32[266,256]{1,0:T(8,128)S(1)} %collective-permute-done.north) | copy-start | bytes 817156
  15.5 0.7 %copy-start.1 = (f32[266,256]{1,0:T(8,128)}, f32[266,256]{1,0:T(8,128)S(1)}, u32[]{:S(2)}) copy-start(f32[266,256]{1,0:T(8,128)S(1)} %collective-permute-done.1.south) | copy-start | bytes 817156
  18.3 9.1 %collective-permute-start.2 = (f32[56,512]{1,0:T(8,128)}, f32[56,512]{1,0:T(8,128)S(1)}, u32[]{:S(2)}, u32[]{:S(2)}) collective-permute-start(f32[56,512]{1,0:T(8,128)} %get-tuple-element.14), channel_id=1, source_target_pairs={{0,16},{16,32},{32,48},{48,64},{64,80},{80,96},{96,112},{112,128},... | collective-permute-start | bytes 344072 | tf_op jit(solution)/shard_map/ppermute | solution.py:360
  19.6 7.8 %collective-permute-start.3 = (f32[56,512]{1,0:T(8,128)}, f32[56,512]{1,0:T(8,128)S(1)}, u32[]{:S(2)}, u32[]{:S(2)}) collective-permute-start(f32[56,512]{1,0:T(8,128)} %get-tuple-element.15), channel_id=1, source_target_pairs={{0,240},{16,0},{32,16},{48,32},{64,48},{80,64},{96,80},{112,96},{1... | collective-permute-start | bytes 344072 | tf_op jit(solution)/shard_map/ppermute | solution.py:361
  27.4 0.6 %copy-start.2 = (f32[56,512]{1,0:T(8,128)}, f32[56,512]{1,0:T(8,128)S(1)}, u32[]{:S(2)}) copy-start(f32[56,512]{1,0:T(8,128)S(1)} %collective-permute-done.2.west) | copy-start | bytes 344068
  28.1 0.6 %copy-start.3 = (f32[56,512]{1,0:T(8,128)}, f32[56,512]{1,0:T(8,128)S(1)}, u32[]{:S(2)}) copy-start(f32[56,512]{1,0:T(8,128)S(1)} %collective-permute-done.3.east) | copy-start | bytes 344068

commit v10 on v8

--- a/solution.py
+++ b/solution.py
@@ -133,14 +133,13 @@
         acc[3] = acc[3] + cor * g[2] - bottom_drag * bottom * g[3]
         acc[0] = acc[0] - 0.2 * wet * density_bar[k]
         acc[1] = acc[1] + 0.8 * wet * density_bar[k]
-        div_bar = [-courant * g[f] for f in range(4)]
         for d, (axis, speed_field) in enumerate(((1, 2), (0, 3))):
             open_face = faces[d, k, 0]
             w = faces[d, k, 1]
             s = faces[d, k, 2]
             w_bar = None
             for f in range(4):
-                flux_bar = open_face * (div_bar[f] - shifted(div_bar[f], 1, axis))
+                flux_bar = (-courant * open_face) * (g[f] - shifted(g[f], 1, axis))
                 part = flux_bar * terms[d, f, k]
                 w_bar = part if w_bar is None else w_bar + part
                 alpha = flux_bar * w

time: 47.2 us -> 47 us (level)
  no operation moved by 1% of the time
where the time goes in v10:
time: 47 us; the launch traced here: 46.8 us
  Pallas kernels  24.5 us (52%)
  starting transfers between devices  10.3 us (22%)
  waiting for transfers between devices  8.05 us (17%)
  local copies, waits for them, and re-layouts  1.98 us (4%)
  other arithmetic  1.35 us (3%)
  between operations  0.64 us (1%)
    pallas_call x1, Pallas kernels, shards(): pl.pallas_call(functools.partial(two_step_kernel, rim, reach), out_shape=...  18.1 us
    ppermute x1, starting transfers between devices, shards(): east = lax.ppermute(east_out, 'lon', ring(lon_count, -1))  4.87 us
    ppermute x1, waiting for transfers between devices, shards(): south = lax.ppermute(south_out, 'lat', ring(lat_count, -1))  4.85 us
    ppermute x1, starting transfers between devices, shards(): north = lax.ppermute(north_out, 'lat', ring(lat_count, 1))  4.12 us
    pallas_call x1, Pallas kernels, shards(): pl.pallas_call(lon_pack_own_kernel, out_shape=(own_msg, own_msg), in_spec...  2.18 us
    pallas_call x1, Pallas kernels, shards(): pl.pallas_call(functools.partial(lon_pack_halo_kernel, rim, reach), out_s...  2.12 us
    pallas_call x1, Pallas kernels, shards(): pl.pallas_call(functools.partial(lat_pack_kernel, rim, reach), out_shape=...  2.06 us
    unnamed x8, local copies, waits for them, and re-layouts  1.98 us
  transfers between devices with their start and end apart: 4, of which 3 were waited for; matrix products, arithmetic and copies ran while one was open for 3% of the time, Pallas kernels for 5%

profile of v10, /device:TPU:1, one launch (start us, length us, event | category | flops | bytes accessed | tf_op | source)
XLA Modules:
  0.0 46.8 jit_solution(6340737684253245281)
XLA Ops:
  0.6 2.1 %shard_map.59 = (f32[266,256]{1,0:T(8,128)}, f32[266,256]{1,0:T(8,128)}, f32[32,256]{1,0:T(8,128)}) custom-call(f32[4,4,32,256]{3,2,1,0:T(8,128)} %own_x.5, f32[4,4,32,256]{3,2,1,0:T(8,128)} %own_c.5, s32[32,256]{1,0:T(8,128)} %sea_ref.1, s32[32,256]{1,0:T(8,128)} %level_ref.1), custom_call_target="tpu_custom_call" | custom-call | tf_op jit(solution)/shard_map/pallas_call | solution.py:317
  2.7 4.1 %collective-permute-start = (f32[266,256]{1,0:T(8,128)}, f32[266,256]{1,0:T(8,128)S(1)}, u32[]{:S(2)}, u32[]{:S(2)}) collective-permute-start(f32[266,256]{1,0:T(8,128)} %get-tuple-element.10), channel_id=1, source_target_pairs={{0,1},{1,2},{2,3},{3,4},{4,5},{5,6},{6,7},{7,8},{8,9},{9,10},{10,1... | collective-permute-start | bytes 817160 | tf_op jit(solution)/shard_map/ppermute | solution.py:325
  6.8 0.0 collective-permute-start.1
  6.8 2.2 %shard_map.60 = (f32[32,512]{1,0:T(8,128)}, f32[32,512]{1,0:T(8,128)}) custom-call(f32[4,4,32,256]{3,2,1,0:T(8,128)} %own_x.5, f32[4,4,32,256]{3,2,1,0:T(8,128)} %own_c.5, f32[32,256]{1,0:T(8,128)} %get-tuple-element.9.own_d), custom_call_target="tpu_custom_call" | custom-call | tf_op jit(solution)/shard_map/pallas_call | solution.py:332
  9.0 1.6 %collective-permute-done.north = f32[266,256]{1,0:T(8,128)S(1)} collective-permute-done((f32[266,256]{1,0:T(8,128)}, f32[266,256]{1,0:T(8,128)S(1)}, u32[]{:S(2)}, u32[]{:S(2)}) %collective-permute-start) | collective-permute-done | bytes 272416 | tf_op jit(solution)/shard_map/ppermute | solution.py:325
  10.6 0.0 copy-start
  10.6 4.8 %collective-permute-done.1.south = f32[266,256]{1,0:T(8,128)S(1)} collective-permute-done((f32[266,256]{1,0:T(8,128)}, f32[266,256]{1,0:T(8,128)S(1)}, u32[]{:S(2)}, u32[]{:S(2)}) %collective-permute-start.1) | collective-permute-done | bytes 272416 | tf_op jit(solution)/shard_map/ppermute | solution.py:326
  15.5 0.0 copy-start.1
  15.5 0.0 copy-done
  15.5 0.7 %copy-done.1 = f32[266,256]{1,0:T(8,128)} copy-done((f32[266,256]{1,0:T(8,128)}, f32[266,256]{1,0:T(8,128)S(1)}, u32[]{:S(2)}) %copy-start.1) | copy-done | bytes 272408
  16.2 2.1 %shard_map.61 = (f32[56,512]{1,0:T(8,128)}, f32[56,512]{1,0:T(8,128)}) custom-call(f32[32,512]{1,0:T(8,128)} %get-tuple-element.12.west_own, f32[32,512]{1,0:T(8,128)} %get-tuple-element.13.east_own, f32[266,256]{1,0:T(8,128)} %copy-done, f32[266,256]{1,0:T(8,128)} %copy-done.1), custom_call_target="tpu_custom_call" | custom-call | tf_op jit(solution)/shard_map/pallas_call | solution.py:339
  18.3 1.3 %collective-permute-start.2 = (f32[56,512]{1,0:T(8,128)}, f32[56,512]{1,0:T(8,128)S(1)}, u32[]{:S(2)}, u32[]{:S(2)}) collective-permute-start(f32[56,512]{1,0:T(8,128)} %get-tuple-element.14), channel_id=1, source_target_pairs={{0,16},{16,32},{32,48},{48,64},{64,80},{80,96},{96,112},{112,128},... | collective-permute-start | bytes 344072 | tf_op jit(solution)/shard_map/ppermute | solution.py:348
  19.6 4.9 %collective-permute-start.3 = (f32[56,512]{1,0:T(8,128)}, f32[56,512]{1,0:T(8,128)S(1)}, u32[]{:S(2)}, u32[]{:S(2)}) collective-permute-start(f32[56,512]{1,0:T(8,128)} %get-tuple-element.15), channel_id=1, source_target_pairs={{0,240},{16,0},{32,16},{48,32},{64,48},{80,64},{96,80},{112,96},{1... | collective-permute-start | bytes 344072 | tf_op jit(solution)/shard_map/ppermute | solution.py:349
  24.5 0.7 %sine_multiply_fusion.cor_ref = f32[56,1]{1,0:T(8,128)} fusion(s32[]{:T(128)S(6)} %mul.29), kind=kLoop, calls=%fused_computation.2 | loop fusion | flops 560 | bytes 228 | tf_op jit(solution)/shard_map/mul | solution.py:354
  25.2 0.6 %fusion.4.rowmask_ref = f32[56,1]{1,0:T(8,128)} fusion(s32[]{:T(128)S(6)} %mul.29), kind=kLoop, calls=%fused_computation.6 | loop fusion | flops 448 | bytes 228 | tf_op jit(solution)/shard_map/convert_element_type | solution.py:352
  25.9 1.6 %collective-permute-done.2.west = f32[56,512]{1,0:T(8,128)S(1)} collective-permute-done((f32[56,512]{1,0:T(8,128)}, f32[56,512]{1,0:T(8,128)S(1)}, u32[]{:S(2)}, u32[]{:S(2)}) %collective-permute-start.2) | collective-permute-done | bytes 114720 | tf_op jit(solution)/shard_map/ppermute | solution.py:348
  27.4 0.0 copy-start.2
  27.4 0.0 collective-permute-done.3.east
  27.4 0.6 %copy-done.2 = f32[56,512]{1,0:T(8,128)} copy-done((f32[56,512]{1,0:T(8,128)}, f32[56,512]{1,0:T(8,128)S(1)}, u32[]{:S(2)}) %copy-start.2) | copy-done | bytes 114712
  28.1 0.0 copy-start.3
  28.1 0.6 %copy-done.3 = f32[56,512]{1,0:T(8,128)} copy-done((f32[56,512]{1,0:T(8,128)}, f32[56,512]{1,0:T(8,128)S(1)}, u32[]{:S(2)}) %copy-start.3) | copy-done | bytes 114712
  28.7 18.1 %shard_map.62 = (f32[4,4,32,256]{3,2,1,0:T(8,128)}, f32[4,4,32,256]{3,2,1,0:T(8,128)}) custom-call(f32[4,4,32,256]{3,2,1,0:T(8,128)} %own_x.5, f32[4,4,32,256]{3,2,1,0:T(8,128)} %own_c.5, f32[32,256]{1,0:T(8,128)} %get-tuple-element.9.own_d, f32[266,256]{1,0:T(8,128)} %copy-done, f32[266,256]{1,0:T(8,128)} %copy-done.1, f32[56,512]{1,0:T(8,128)} %copy-done.2, ...), custom_call_target="tpu_custom_call" | custom-call | tf_op jit(solution)/shard_map/pallas_call | solution.py:357
Async XLA Ops:
  2.7 7.9 %collective-permute-start = (f32[266,256]{1,0:T(8,128)}, f32[266,256]{1,0:T(8,128)S(1)}, u32[]{:S(2)}, u32[]{:S(2)}) collective-permute-start(f32[266,256]{1,0:T(8,128)} %get-tuple-element.10), channel_id=1, source_target_pairs={{0,1},{1,2},{2,3},{3,4},{4,5},{5,6},{6,7},{7,8},{8,9},{9,10},{10,1... | collective-permute-start | bytes 817160 | tf_op jit(solution)/shard_map/ppermute | solution.py:325
  6.8 8.7 %collective-permute-start.1 = (f32[266,256]{1,0:T(8,128)}, f32[266,256]{1,0:T(8,128)S(1)}, u32[]{:S(2)}, u32[]{:S(2)}) collective-permute-start(f32[266,256]{1,0:T(8,128)} %get-tuple-element.11), channel_id=1, source_target_pairs={{0,15},{1,0},{2,1},{3,2},{4,3},{5,4},{6,5},{7,6},{8,7},{9,8},{10,9... | collective-permute-start | bytes 817160 | tf_op jit(solution)/shard_map/ppermute | solution.py:326
  10.6 4.9 %copy-start = (f32[266,256]{1,0:T(8,128)}, f32[266,256]{1,0:T(8,128)S(1)}, u32[]{:S(2)}) copy-start(f32[266,256]{1,0:T(8,128)S(1)} %collective-permute-done.north) | copy-start | bytes 817156
  15.5 0.7 %copy-start.1 = (f32[266,256]{1,0:T(8,128)}, f32[266,256]{1,0:T(8,128)S(1)}, u32[]{:S(2)}) copy-start(f32[266,256]{1,0:T(8,128)S(1)} %collective-permute-done.1.south) | copy-start | bytes 817156
  18.3 9.1 %collective-permute-start.2 = (f32[56,512]{1,0:T(8,128)}, f32[56,512]{1,0:T(8,128)S(1)}, u32[]{:S(2)}, u32[]{:S(2)}) collective-permute-start(f32[56,512]{1,0:T(8,128)} %get-tuple-element.14), channel_id=1, source_target_pairs={{0,16},{16,32},{32,48},{48,64},{64,80},{80,96},{96,112},{112,128},... | collective-permute-start | bytes 344072 | tf_op jit(solution)/shard_map/ppermute | solution.py:348
  19.6 7.8 %collective-permute-start.3 = (f32[56,512]{1,0:T(8,128)}, f32[56,512]{1,0:T(8,128)S(1)}, u32[]{:S(2)}, u32[]{:S(2)}) collective-permute-start(f32[56,512]{1,0:T(8,128)} %get-tuple-element.15), channel_id=1, source_target_pairs={{0,240},{16,0},{32,16},{48,32},{64,48},{80,64},{96,80},{112,96},{1... | collective-permute-start | bytes 344072 | tf_op jit(solution)/shard_map/ppermute | solution.py:349
  27.4 0.6 %copy-start.2 = (f32[56,512]{1,0:T(8,128)}, f32[56,512]{1,0:T(8,128)S(1)}, u32[]{:S(2)}) copy-start(f32[56,512]{1,0:T(8,128)S(1)} %collective-permute-done.2.west) | copy-start | bytes 344068
  28.1 0.6 %copy-start.3 = (f32[56,512]{1,0:T(8,128)}, f32[56,512]{1,0:T(8,128)S(1)}, u32[]{:S(2)}) copy-start(f32[56,512]{1,0:T(8,128)S(1)} %collective-permute-done.3.east) | copy-start | bytes 344068
